TPU v7x, 256 devices: a whole 4x4x8 slice. The times are simulated.
256 devices in a mesh: dp: 32 (over z, x), mp: 8 (over y, core).
Axes of the slice: x: 4, y: 4, z: 8, core: 2. Of those that a mesh axis runs over, the one named last changes fastest.
Arguments:
- token_ids: int32 [2048, 7], replicated, may hold values from 0 to 65535
- lengths: int32 [2048], replicated, may hold values from 1 to 7, as said below
- pack_dest: int32 [2048], replicated, may hold values from 0 to 31, as said below
- ref_hidden: bfloat16 [2048, 7, 4096], P('dp', None, 'mp'), may hold values from -45 to 45
- reward_hidden: bfloat16 [2048, 7, 4096], P('dp', None, 'mp'), may hold values from -140 to 140
- head_weight: bfloat16 [4096, 65536], P('mp', 'dp'), may hold values from -0.25 to 0.25
- norm_gain: float32 [4096], P('mp'), may hold values from 0.1 to 1.9
- score_weight: float32 [4096], P('mp'), may hold values from -0.09375 to 0.09375
- value_weight: float32 [4096], P('mp'), may hold values from -0.09375 to 0.09375
- old_logprob: float32 [8192], P('dp'), may hold values from -14 to -1
Outputs:
- ref_logprob: float32 [8192], P('dp')
- advantage: float32 [8192], P('dp')
Inputs may be any that keep to these rules, and one draw needn't show every extreme that they name: `pack_dest`: request i belongs to request shard i // 64. Each request shard sends exactly 2 of its requests to every packed shard. A packed shard lists its requests by request shard, then by request index, and packs their tokens in that order from slot 0. In that order the requests of a packed shard form pairs whose lengths sum to 8, so every packed shard holds exactly 256 tokens; every packed shard has a request of length 1 and one of length 7.
All inputs are finite; a program needn't handle non-finite values.
Results may differ from a plain program's by a relative error of at most 0.0003.
Values may be sent and summed in bfloat16 or wider, within the bound.
No kernel may reach another device: no remote copies, remote signals or barrier semaphores. Data moves between devices by JAX's collectives and lax.ppermute only.
A program may use at most 192 MiB of HBM per device.

v0:
```python
import math

import jax
import jax.numpy as jnp
from jax import lax
from jax.sharding import PartitionSpec as P

kl_coef = 0.1
discount = 0.99
gae_mix = 0.95
norm_eps = 1e-05


def combined_all(part, axis, combine):
    gathered = jax.tree.map(lambda a: lax.all_gather(a, axis), part)

    def take(source):
        return jax.tree.map(lambda a: lax.dynamic_index_in_dim(a, source, 0, False), gathered)

    return lax.fori_loop(
        1, lax.axis_size(axis), lambda source, state: combine(state, take(source)), take(0)
    )


def pack_tables(pack_dest, lengths, shards, req_dev, slot_dev):
    per_pair = req_dev // shards
    target_shard = pack_dest.reshape(shards, req_dev)
    same_shard = target_shard[:, :, None] == target_shard[:, None, :]
    earlier = (
        jnp.arange(req_dev, dtype=jnp.int32)[None, :]
        < jnp.arange(req_dev, dtype=jnp.int32)[:, None]
    )
    rank_in = jnp.sum(jnp.logical_and(same_shard, earlier[None]).astype(jnp.int32), axis=2)
    packed_pos = jnp.arange(shards, dtype=jnp.int32)[:, None] * per_pair + rank_in
    packed_place = (target_shard * req_dev + packed_pos).reshape(-1)
    source_of = (
        jnp.zeros((shards * req_dev,), jnp.int32)
        .at[packed_place]
        .set(jnp.arange(shards * req_dev, dtype=jnp.int32))
        .reshape(shards, req_dev)
    )
    packed_len = lengths[source_of]
    offsets = jnp.cumsum(packed_len, axis=1, dtype=jnp.int32) - packed_len
    slot_ids = jnp.arange(slot_dev, dtype=jnp.int32)
    request_at = (
        jnp.sum((offsets[:, None, :] <= slot_ids[None, :, None]).astype(jnp.int32), axis=2) - 1
    )
    start_at = jnp.take_along_axis(offsets, request_at, axis=1)
    offset_in = slot_ids[None, :] - start_at
    is_last = offset_in == jnp.take_along_axis(packed_len, request_at, axis=1) - 1
    source_prompt = jnp.take_along_axis(source_of, request_at, axis=1)
    return (target_shard, packed_pos, request_at, offset_in, is_last, source_prompt)


def advantages(reward, value_est, is_last, request_at):
    slot_count = reward.shape[0]
    next_value = jnp.concatenate([value_est[1:], jnp.zeros((1,), jnp.float32)])
    not_last = 1.0 - is_last.astype(jnp.float32)
    td_error = reward + discount * next_value * not_last - value_est
    slot_ids = jnp.arange(slot_count, dtype=jnp.int32)
    step_gap = (slot_ids[None, :] - slot_ids[:, None]).astype(jnp.float32)
    same_req = jnp.logical_and(request_at[:, None] == request_at[None, :], step_gap >= 0)
    weights = jnp.where(
        same_req, jnp.exp(jnp.maximum(step_gap, 0.0) * math.log(discount * gae_mix)), 0.0
    )
    return jnp.dot(weights, td_error, precision=lax.Precision.HIGHEST)


def combine_softmax(left_part, right_part):
    joint_max = jnp.maximum(left_part[0], right_part[0])
    joint_total = left_part[1] * jnp.exp(left_part[0] - joint_max) + right_part[1] * jnp.exp(
        right_part[0] - joint_max
    )
    return (joint_max, joint_total, left_part[2] + right_part[2])


def body(
    token_ids,
    lengths,
    pack_dest,
    ref_hidden,
    reward_hidden,
    head_weight,
    norm_gain,
    score_weight,
    value_weight,
    old_logprob,
):
    shards = lax.axis_size("dp")
    tensor_ways = lax.axis_size("mp")
    shard_index = lax.axis_index("dp")
    part_index = lax.axis_index("mp")
    req_dev, max_len, width_dev = ref_hidden.shape
    slot_dev = req_dev // 2 * (max_len + 1)
    sub_len = slot_dev // tensor_ways
    per_pair = req_dev // shards
    target_shard, packed_pos, request_at, offset_in, is_last, source_prompt = pack_tables(
        pack_dest, lengths, shards, req_dev, slot_dev
    )
    my_shards = lax.dynamic_index_in_dim(target_shard, shard_index, 0, keepdims=False)
    my_rank = (
        lax.dynamic_index_in_dim(packed_pos, shard_index, 0, keepdims=False)
        - shard_index * per_pair
    )
    send_place = my_shards * per_pair + my_rank
    send_order = (
        jnp.zeros((req_dev,), jnp.int32).at[send_place].set(jnp.arange(req_dev, dtype=jnp.int32))
    )
    ref_send = jnp.take(ref_hidden, send_order, axis=0).reshape(
        shards, per_pair * max_len, width_dev
    )
    reward_send = jnp.take(reward_hidden, send_order, axis=0).reshape(
        shards, per_pair * max_len, width_dev
    )
    ref_got, reward_got = (
        lax.all_to_all(ref_send, "dp", split_axis=0, concat_axis=0, tiled=True),
        lax.all_to_all(reward_send, "dp", split_axis=0, concat_axis=0, tiled=True),
    )
    my_request = lax.dynamic_index_in_dim(request_at, shard_index, 0, keepdims=False)
    my_offset = lax.dynamic_index_in_dim(offset_in, shard_index, 0, keepdims=False)
    my_last = lax.dynamic_index_in_dim(is_last, shard_index, 0, keepdims=False)
    row_index = my_request * max_len + my_offset
    ref_packed = jnp.take(ref_got.reshape(req_dev * max_len, width_dev), row_index, axis=0)
    reward_packed = jnp.take(reward_got.reshape(req_dev * max_len, width_dev), row_index, axis=0)
    all_targets = token_ids.reshape(-1)[(source_prompt * max_len + offset_in).reshape(-1)].reshape(
        shards, slot_dev
    )
    target_order = jnp.transpose(
        all_targets.reshape(shards, tensor_ways, sub_len), (1, 0, 2)
    ).reshape(-1)
    my_targets = lax.dynamic_index_in_dim(
        target_order.reshape(tensor_ways, -1), part_index, 0, keepdims=False
    )
    vocab_dev = head_weight.shape[1]
    vocab_base = shard_index * vocab_dev
    own_rows = lax.all_to_all(
        ref_packed.reshape(tensor_ways, sub_len, width_dev),
        "mp",
        split_axis=0,
        concat_axis=2,
        tiled=True,
    )
    block_rows = lax.all_gather(own_rows, "dp", axis=0, tiled=True).reshape(
        -1, width_dev * tensor_ways
    )
    logits = jnp.dot(
        block_rows,
        lax.all_gather(head_weight, "mp", axis=0, tiled=True),
        preferred_element_type=jnp.float32,
    )
    row_max = jnp.max(logits, axis=1)
    exp_total = jnp.sum(jnp.exp(logits - row_max[:, None]), axis=1)
    matches = jnp.arange(vocab_dev, dtype=jnp.int32)[None, :] + vocab_base == my_targets[:, None]
    target_logit = jnp.sum(jnp.where(matches, logits, 0.0), axis=1)
    row_max, exp_total, target_logit = combined_all(
        (row_max, exp_total, target_logit), "dp", combine_softmax
    )
    block_logprob = (target_logit - row_max - jnp.log(exp_total)).reshape(shards, sub_len)
    own_block = lax.dynamic_index_in_dim(block_logprob, shard_index, 0, keepdims=False)
    ref_logprob = lax.all_gather(own_block, "mp", axis=0, tiled=True)
    width_full = width_dev * tensor_ways
    hidden_f = reward_packed.astype(jnp.float32)
    squares = lax.psum(jnp.sum(hidden_f * hidden_f, axis=1), "mp")
    inv_rms = lax.rsqrt(squares / width_full + norm_eps)
    normed = hidden_f * inv_rms[:, None] * norm_gain
    score, value_est = lax.psum(
        (jnp.sum(normed * score_weight, axis=1), jnp.sum(normed * value_weight, axis=1)), "mp"
    )
    reward = -kl_coef * (old_logprob - ref_logprob) + jnp.where(my_last, score, 0.0)
    advantage = advantages(reward, value_est, my_last, my_request)
    return (ref_logprob, advantage)


def solution(mesh):
    return jax.shard_map(
        body,
        mesh=mesh,
        in_specs=(
            P(),
            P(),
            P(),
            P("dp", None, "mp"),
            P("dp", None, "mp"),
            P("mp", "dp"),
            P("mp"),
            P("mp"),
            P("mp"),
            P("dp"),
        ),
        out_specs=(P("dp"), P("dp")),
        check_vma=False,
    )
```

profile of v0, /device:TPU:1, one launch (start us, length us, event | category | flops | bytes accessed | tf_op | source)
XLA Modules:
  0.0 584.4 jit_solution(3837817773530225008)
XLA Ops:
  7.2 0.8 reshape.192
  8.1 0.9 convert_reduce_fusion.1
  9.1 0.8 scatter_custom_fusion
  9.9 1.9 gather_fusion.7
  11.9 1.9 gather_fusion.2
  13.9 0.2 broadcast_select_fusion
  14.1 0.3 copy.26
  14.3 0.9 reshape.193
  15.2 11.9 %all-to-all-start = ((bf16[32,14,512]{2,1,0:T(8,128)(2,1)}), bf16[32,14,512]{2,1,0:T(8,128)(2,1)S(1)}, u32[]{:S(2)}, u32[]{:S(2)}) async-start(bf16[32,14,512]{2,1,0:T(8,128)(2,1)} %reshape.193), calls=%async_computation | async-start | bytes 1048576 | tf_op jit(solution)/shard_map/all_to_all | solution.py:116
  27.2 8.0 %scatter_custom_fusion.1 = s32[2048]{0:T(1024)S(1)} fusion(s32[2048]{0:T(1024)S(1)} %compare_select_fusion.3, s32[2048]{0:T(1024)S(1)} %iota.45, s32[]{:T(128)} %constant.142.clone.1), kind=kCustom, calls=%fused_computation.65 | custom fusion | bytes 8196 | tf_op jit(solution)/shard_map/scatter | solution.py:39
  35.5 11.8 %gather_fusion = s32[2048]{0:T(1024)S(1)} fusion(s32[2048]{0:T(1024)S(1)} %copy-done.1, s32[2048]{0:T(1024)S(1)} %broadcast_clamp_fusion.1), kind=kCustom, calls=%fused_computation.7 | custom fusion | bytes 24576 | tf_op jit(solution)/shard_map/gather | solution.py:42
  47.4 0.2 reduce_window_sum.11
  47.6 0.5 convert_reduce_fusion
  48.1 52.9 %gather_fusion.3 = s32[8192]{0:T(1024)S(1)} fusion(s32[32,64]{1,0:T(8,128)S(1)} %sub.102, s32[8192]{0:T(1024)S(1)} %bitcast.52), kind=kCustom, calls=%fused_computation.1.clone | custom fusion | bytes 131072 | tf_op jit(solution)/shard_map/jit(take_along_axis)/gather | solution.py:48
  101.0 52.9 %gather_fusion.5 = s32[8192]{0:T(1024)S(1)} fusion(s32[32,64]{1,0:T(8,128)S(1)} %reshape.199, s32[8192]{0:T(1024)S(1)} %bitcast.53), kind=kCustom, calls=%fused_computation.4.clone | custom fusion | bytes 131072 | tf_op jit(solution)/shard_map/jit(take_along_axis)/gather | solution.py:51
  154.0 52.9 %gather_fusion.6 = s32[8192]{0:T(1024)S(1)} fusion(s32[32,64]{1,0:T(8,128)S(1)} %reshape.257, s32[8192]{0:T(1024)S(1)} %bitcast.54), kind=kCustom, calls=%fused_computation.5.clone | custom fusion | bytes 131072 | tf_op jit(solution)/shard_map/jit(take_along_axis)/gather | solution.py:50
  207.0 0.1 reshape.194
  207.1 1.2 gather_fusion.4
  208.3 0.1 broadcast_select_fusion.3
  208.4 11.7 %all_to_all.28 = bf16[8,32,512]{2,1,0:T(8,128)(2,1)S(1)} all-to-all(bf16[8,32,512]{2,1,0:T(8,128)(2,1)S(1)} %bitcast.55), channel_id=1, replica_groups=mesh['dp'=32,'mp'=8] {'mp'}, dimensions={0} | all-to-all | bytes 524288 | tf_op jit(solution)/shard_map/all_to_all | solution.py:136
  220.1 0.7 copy.31
  220.9 0.7 all-gather.9.cloned.1.call-update
  221.6 0.3 copy.30
  221.9 1.0 reshape.202
  222.9 9.7 %all-to-all-start.2 = ((bf16[32,14,512]{2,1,0:T(8,128)(2,1)}), bf16[32,14,512]{2,1,0:T(8,128)(2,1)S(1)}, u32[]{:S(2)}, u32[]{:S(2)}) async-start(bf16[32,14,512]{2,1,0:T(8,128)(2,1)} %reshape.202), calls=%async_computation.2 | async-start | bytes 1048576 | tf_op jit(solution)/shard_map/all_to_all | solution.py:117
  232.6 0.4 copy.28
  233.0 0.7 reshape.198
  233.7 45.5 %gather_fusion.1 = s32[8192]{0:T(1024)S(1)} fusion(s32[14336]{0:T(1024)S(1)} %reshape.198, s32[8192]{0:T(1024)S(1)} %broadcast_clamp_fusion), kind=kCustom, calls=%fused_computation.8 | custom fusion | bytes 98304 | tf_op jit(solution)/shard_map/gather | solution.py:125
  279.3 0.1 reshape_reshape.6
  279.5 0.1 reshape_reshape.7
  279.6 0.6 dynamic-slice
  280.9 0.1 reshape.203
  281.0 1.2 gather_fusion.8
  282.1 0.2 fusion
  282.4 13.5 %psum.21 = f32[256]{0:T(256)S(1)} all-reduce(f32[256]{0:T(256)S(1)} %fusion), channel_id=1, replica_groups=mesh['dp'=32,'mp'=8] {'mp'}, use_global_device_ids=true, to_apply=%region_11.15 | all-reduce | flops 256 | bytes 2048 | tf_op jit(solution)/shard_map/psum | solution.py:163
  295.9 0.3 fusion.4
  296.2 24.2 %all-gather.7.cloned.1.call-done = bf16[32,32,4096]{2,1,0:T(8,128)(2,1)} async-done(((bf16[1,32,4096]{2,1,0:T(8,128)(2,1)}), bf16[32,32,4096]{2,1,0:T(8,128)(2,1)}) %all-gather.7.cloned.1.call-update) | async-done | bytes 8388624 | tf_op jit(solution)/shard_map/all_gather | solution.py:143
  320.4 87.6 %all-gather.9.cloned.1.call-done = bf16[4096,2048]{1,0:T(8,128)(2,1)} async-done(((bf16[512,2048]{1,0:T(8,128)(2,1)}), bf16[4096,2048]{1,0:T(8,128)(2,1)}) %all-gather.9.cloned.1.call-update) | async-done | bytes 16777232 | tf_op jit(solution)/shard_map/all_gather | solution.py:148
  408.0 22.9 %fusion.36 = (f32[1024]{0:T(1024)S(1)}, f32[1024,2048]{1,0:T(8,128)S(1)}) fusion(bf16[1024,4096]{1,0:T(8,128)(2,1)} %bitcast.69, bf16[4096,2048]{1,0:T(8,128)(2,1)} %all-gather.9.cloned.1.call-done), kind=kOutput, calls=%fused_computation.97 | convolution fusion | flops 17181966336 | bytes 33558528 | tf_op jit(solution)/shard_map/dot_general | solution.py:146
  431.0 2.8 select_reduce_fusion
  433.8 34.3 %all-gather.1 = f32[32768]{0:T(1024)S(1)} all-gather(f32[1024]{0:T(1024)S(1)} %get-tuple-element.187), channel_id=3, replica_groups=mesh['dp'=32,'mp'=8] {'dp'}, dimensions={0}, use_global_device_ids=true | all-gather | bytes 135168 | tf_op jit(solution)/shard_map/all_gather | solution.py:15
  468.1 31.8 %all-gather.2 = f32[32768]{0:T(1024)S(1)} all-gather(f32[1024]{0:T(1024)S(1)} %get-tuple-element.186), channel_id=4, replica_groups=mesh['dp'=32,'mp'=8] {'dp'}, dimensions={0}, use_global_device_ids=true | all-gather | bytes 135168 | tf_op jit(solution)/shard_map/all_gather | solution.py:15
  499.9 32.4 %all-gather = f32[32768]{0:T(1024)S(1)} all-gather(f32[1024]{0:T(1024)S(1)} %get-tuple-element.220), channel_id=2, replica_groups=mesh['dp'=32,'mp'=8] {'dp'}, dimensions={0}, use_global_device_ids=true | all-gather | bytes 135168 | tf_op jit(solution)/shard_map/all_gather | solution.py:15
  532.4 2.9 while.19
  535.4 0.1 fusion.30
  535.5 41.0 %all-reduce.1 = (f32[256]{0:T(256)S(1)}, f32[256]{0:T(256)S(1)}, f32[256]{0:T(256)S(1)}) all-reduce(f32[256]{0:T(256)S(1)} %fusion.30, f32[256]{0:T(256)S(1)} %get-tuple-element.189, f32[256]{0:T(256)S(1)} %get-tuple-element.188), channel_id=5, replica_groups=mesh['dp'=32,'mp'=8] {'mp'}, use_global_device_ids=true, to_apply=%add | all-reduce | flops 768 | bytes 6144 | tf_op jit(solution)/shard_map/all_gather | solution.py:160
  576.5 0.1 fusion.25
  576.6 1.0 fusion.6
  (197 shorter events, 2.6 us)
Async XLA Ops:
  7.2 2.8 copy-start
  7.2 4.7 copy-start.2
  11.9 15.3 %copy-start.4 = (s32[2048]{0:T(1024)S(1)}, s32[2048]{0:T(1024)}, u32[]{:S(2)}) copy-start(s32[2048]{0:T(1024)} %param.20) | copy-start | bytes 24580
  11.9 23.6 %copy-start.1 = (s32[2048]{0:T(1024)S(1)}, s32[2048]{0:T(1024)}, u32[]{:S(2)}) copy-start(s32[2048]{0:T(1024)} %param.19) | copy-start | bytes 24580
  15.2 191.7 %all-to-all-start = ((bf16[32,14,512]{2,1,0:T(8,128)(2,1)}), bf16[32,14,512]{2,1,0:T(8,128)(2,1)S(1)}, u32[]{:S(2)}, u32[]{:S(2)}) async-start(bf16[32,14,512]{2,1,0:T(8,128)(2,1)} %reshape.193), calls=%async_computation | async-start | bytes 1048576 | tf_op jit(solution)/shard_map/all_to_all | solution.py:116
  27.1 293.3 %all-gather.7.cloned.1.call-start = ((), (), s32[]{:S(2)}) async-start(), calls=%async_computation.3 | async-start | bytes 8650752 | tf_op jit(solution)/shard_map/all_gather | solution.py:143
  207.1 25.5 %copy-start.3 = (s32[2048,7]{0,1:T(8,128)S(1)}, s32[2048,7]{0,1:T(8,128)}, u32[]{:S(2)}) copy-start(s32[2048,7]{0,1:T(8,128)} %param.18) | copy-start | bytes 172036
  220.9 187.1 %all-gather.9.cloned.1.call-start = ((), (), s32[]{:S(2)}) async-start(), calls=%async_computation.4 | async-start | bytes 18874368 | tf_op jit(solution)/shard_map/all_gather | solution.py:148
  222.9 58.0 %all-to-all-start.2 = ((bf16[32,14,512]{2,1,0:T(8,128)(2,1)}), bf16[32,14,512]{2,1,0:T(8,128)(2,1)S(1)}, u32[]{:S(2)}, u32[]{:S(2)}) async-start(bf16[32,14,512]{2,1,0:T(8,128)(2,1)} %reshape.202), calls=%async_computation.2 | async-start | bytes 1048576 | tf_op jit(solution)/shard_map/all_to_all | solution.py:117
  233.7 45.8 %copy-start.10 = (u32[256]{0:T(256)S(1)}, u32[256]{0:T(256)}, u32[]{:S(2)}) copy-start(u32[256]{0:T(256)} %constant.204) | copy-start | bytes 3076
  279.3 16.6 %copy-start.5 = (f32[512]{0:T(512)S(1)}, f32[512]{0:T(512)}, u32[]{:S(2)}) copy-start(f32[512]{0:T(512)} %param.25) | copy-start | bytes 6148
  279.3 16.6 %copy-start.6 = (f32[512]{0:T(512)S(1)}, f32[512]{0:T(512)}, u32[]{:S(2)}) copy-start(f32[512]{0:T(512)} %param.24) | copy-start | bytes 6148
  279.3 16.6 %copy-start.7 = (f32[512]{0:T(512)S(1)}, f32[512]{0:T(512)}, u32[]{:S(2)}) copy-start(f32[512]{0:T(512)} %param.26) | copy-start | bytes 6148
  431.0 145.5 %copy-start.8 = (f32[256]{0:T(256)S(1)}, f32[256]{0:T(256)}, u32[]{:S(2)}) copy-start(f32[256]{0:T(256)} %param.27) | copy-start | bytes 3076
  576.4 1.1 copy-start.9
Sparse Core Ops, SparseCore 0:
  221.0 99.3 all-gather.6
  322.2 85.7 all-gather.8
where the time goes:
time: 585 us; the launch traced here: 584 us
  local copies, waits for them, and re-layouts  239 us (41%)
  blocking collectives  165 us (28%)
  waiting for transfers between devices  113 us (19%)
  matrix products  23.9 us (4%)
  starting transfers between devices  21.6 us (4%)
  between operations  15.3 us (3%)
  other arithmetic  6.09 us (1%)
    all_gather x3, blocking collectives, combined_all(): gathered = jax.tree.map(lambda a: lax.all_gather(a, axis), part)  98.5 us
    all_gather x1, waiting for transfers between devices, body(): lax.all_gather(head_weight, 'mp', axis=0, tiled=True)  87.6 us
    gather x2, local copies, waits for them, and re-layouts, pack_tables(): start_at = jnp.take_along_axis(offsets, request_at, axis=1)  52.9 us
    gather x2, local copies, waits for them, and re-layouts, pack_tables(): jnp.take_along_axis(packed_len, request_at, axis=1) - 1  52.9 us
    gather x2, local copies, waits for them, and re-layouts, pack_tables(): source_prompt = jnp.take_along_axis(source_of, request_at, axis=1)  52.9 us
    gather x1, local copies, waits for them, and re-layouts, body(): token_ids.reshape(-1)[(source_prompt * max_len + offset_in).reshape(-1)]  45.5 us
    all_gather x1, blocking collectives, body(): ref_logprob = lax.all_gather(own_block, 'mp', axis=0, tiled=True)  41 us
    all_gather x1, waiting for transfers between devices, body(): lax.all_gather(own_rows, 'dp', axis=0, tiled=True)  24.2 us
  transfers between devices with their start and end apart: 4, of which 2 were waited for; matrix products, arithmetic and copies ran while one was open for 39% of the time, Pallas kernels for 0%

commit v1 on v0

v1 whole, which is shorter than its diff:
```python
import jax
import jax.numpy as jnp
from jax import lax
from jax.sharding import PartitionSpec as P

kl_coef = 0.1
discount = 0.99
gae_mix = 0.95
norm_eps = 1e-05


def pair_rank(dest):
    count = dest.shape[-1]
    idx = jnp.arange(count, dtype=jnp.int32)
    same = dest[..., None, :] == dest[..., :, None]
    earlier = idx[None, :] < idx[:, None]
    return jnp.sum(jnp.logical_and(same, earlier).astype(jnp.int32), axis=-1)


def body(
    token_ids,
    lengths,
    pack_dest,
    ref_hidden,
    reward_hidden,
    head_weight,
    norm_gain,
    score_weight,
    value_weight,
    old_logprob,
):
    shards = lax.axis_size("dp")
    ways = lax.axis_size("mp")
    me = lax.axis_index("dp")
    part = lax.axis_index("mp")
    req_dev, max_len, width_dev = ref_hidden.shape
    pair_len = max_len + 1
    slot_dev = shards * pair_len
    sub_len = slot_dev // ways
    blocks = sub_len // pair_len
    width_full = width_dev * ways
    steps = jnp.arange(max_len, dtype=jnp.int32)

    dest = lax.dynamic_slice_in_dim(pack_dest, me * req_dev, req_dev)
    size = lax.dynamic_slice_in_dim(lengths, me * req_dev, req_dev)
    rank = pair_rank(dest)
    row = dest[:, None] * pair_len + steps[None, :] + rank[:, None] * (pair_len - size[:, None])
    row = jnp.where(steps[None, :] < size[:, None], row, -1).reshape(-1)
    onehot = (row[None, :] == jnp.arange(slot_dev, dtype=jnp.int32)[:, None]).astype(jnp.bfloat16)
    ref_send = jnp.dot(
        onehot, ref_hidden.reshape(req_dev * max_len, width_dev), preferred_element_type=jnp.float32
    ).astype(jnp.bfloat16)
    reward_send = jnp.dot(
        onehot, reward_hidden.reshape(req_dev * max_len, width_dev), preferred_element_type=jnp.float32
    ).astype(jnp.bfloat16)
    send = jnp.concatenate([ref_send, reward_send], axis=1).reshape(shards, pair_len, 2 * width_dev)
    got = lax.all_to_all(send, "dp", 0, 0, tiled=True).reshape(slot_dev, 2 * width_dev)
    ref_packed = got[:, :width_dev]
    reward_packed = got[:, width_dev:]

    own_rows = lax.all_to_all(
        ref_packed.reshape(ways, sub_len, width_dev), "mp", 0, 2, tiled=True
    ).reshape(sub_len, width_full)
    block_rows = lax.all_gather(own_rows, "dp", axis=0, tiled=True)
    weight = lax.all_gather(head_weight, "mp", axis=0, tiled=True)

    first_src = part * blocks
    dest4 = lax.dynamic_slice_in_dim(pack_dest, first_src * req_dev, blocks * req_dev).reshape(
        blocks, req_dev
    )
    size4 = lax.dynamic_slice_in_dim(lengths, first_src * req_dev, blocks * req_dev).reshape(
        blocks, req_dev
    )
    tok4 = lax.dynamic_slice_in_dim(token_ids, first_src * req_dev, blocks * req_dev, axis=0)
    rank4 = pair_rank(dest4)
    key = (
        dest4[:, :, None] * sub_len
        + jnp.arange(blocks, dtype=jnp.int32)[:, None, None] * pair_len
        + steps[None, None, :]
        + rank4[:, :, None] * (pair_len - size4[:, :, None])
    )
    key = jnp.where(steps[None, None, :] < size4[:, :, None], key, -1).reshape(-1)
    hits = key[None, :] == jnp.arange(shards * sub_len, dtype=jnp.int32)[:, None]
    targets = jnp.sum(jnp.where(hits, tok4.reshape(-1)[None, :], 0), axis=1)

    logits = jnp.dot(block_rows, weight, preferred_element_type=jnp.float32)
    vocab_dev = head_weight.shape[1]
    row_max = jnp.max(logits, axis=1)
    exp_total = jnp.sum(jnp.exp(logits - row_max[:, None]), axis=1)
    column = jnp.arange(vocab_dev, dtype=jnp.int32)[None, :] + me * vocab_dev
    target_logit = jnp.sum(jnp.where(column == targets[:, None], logits, 0.0), axis=1)
    stats = jnp.stack([row_max, exp_total, target_logit]).reshape(3, shards, sub_len)
    stats = lax.all_to_all(stats, "dp", 1, 1, tiled=True)
    joint_max = jnp.max(stats[0], axis=0)
    joint_total = jnp.sum(stats[1] * jnp.exp(stats[0] - joint_max[None, :]), axis=0)
    joint_target = jnp.sum(stats[2], axis=0)
    block_logprob = joint_target - joint_max - jnp.log(joint_total)
    ref_logprob = lax.all_gather(block_logprob, "mp", axis=0, tiled=True)

    hidden_f = reward_packed.astype(jnp.float32)
    sums = jnp.stack(
        [
            jnp.sum(hidden_f * hidden_f, axis=1),
            jnp.sum(hidden_f * (norm_gain * score_weight), axis=1),
            jnp.sum(hidden_f * (norm_gain * value_weight), axis=1),
        ]
    )
    squares, score_dot, value_dot = lax.psum(sums, "mp")
    inv_rms = lax.rsqrt(squares / width_full + norm_eps)
    score = score_dot * inv_rms
    value_est = value_dot * inv_rms

    mine = (pack_dest.reshape(shards, req_dev) == me).astype(jnp.int32)
    is_first = jnp.logical_and(mine == 1, jnp.cumsum(mine, axis=1) == 1)
    first_len = jnp.sum(jnp.where(is_first, lengths.reshape(shards, req_dev), 0), axis=1)
    place = jnp.arange(pair_len, dtype=jnp.int32)[None, :]
    is_last = jnp.logical_or(place == first_len[:, None] - 1, place == pair_len - 1)
    is_last_flat = is_last.reshape(-1)

    reward = -kl_coef * (old_logprob - ref_logprob) + jnp.where(is_last_flat, score, 0.0)
    next_value = jnp.concatenate([value_est[1:], jnp.zeros((1,), jnp.float32)])
    not_last = 1.0 - is_last_flat.astype(jnp.float32)
    td_error = (reward + discount * next_value * not_last - value_est).reshape(shards, pair_len)
    decay = discount * gae_mix
    carry = td_error[:, pair_len - 1]
    columns = [carry]
    for step in range(pair_len - 2, -1, -1):
        carry = td_error[:, step] + decay * jnp.where(is_last[:, step], 0.0, carry)
        columns.append(carry)
    advantage = jnp.stack(columns[::-1], axis=1).reshape(-1)
    return (ref_logprob, advantage)


def solution(mesh):
    return jax.shard_map(
        body,
        mesh=mesh,
        in_specs=(
            P(),
            P(),
            P(),
            P("dp", None, "mp"),
            P("dp", None, "mp"),
            P("mp", "dp"),
            P("mp"),
            P("mp"),
            P("mp"),
            P("dp"),
        ),
        out_specs=(P("dp"), P("dp")),
        check_vma=False,
    )
```

time: 585 us -> 305 us (0.52)
  local copies, waits for them, and re-layouts: 239 us -> 6.68 us
  blocking collectives: 165 us -> 54.7 us
  waiting for transfers between devices: 113 us -> 184 us
  starting transfers between devices: 21.6 us -> 9.61 us
    gather x13 -> x0, local copies, waits for them, and re-layouts: 222 us -> none  [the longest x2 52.9 us: pack_tables(): start_at = jnp.take_along_axis(offsets, request_at, axis=1)]
    all_gather x4 -> x0, blocking collectives: 139 us -> none  [the longest x3 98.5 us: combined_all(): gathered = jax.tree.map(lambda a: lax.all_gather(a, axis), part)]
    all_gather x2, waiting for transfers between devices: 112 us -> 174 us  [the longest x1 87.6 us: body(): weight = lax.all_gather(head_weight, 'mp', axis=0, tiled=True)]
    all_to_all x1 -> x2, blocking collectives: 11.7 us -> 41.1 us  [the longest x1 27.9 us: body(): lax.all_to_all(send, 'dp', 0, 0, tiled=True)]
    unnamed x0 -> x1, blocking collectives: none -> 13.6 us
    psum x1 -> x0, blocking collectives: 13.5 us -> none  [body(): squares = lax.psum(jnp.sum(hidden_f * hidden_f, axis=1), 'mp')]
    all_to_all x2 -> x1, starting transfers between devices: 21.5 us -> 9.53 us  [body(): stats = lax.all_to_all(stats, 'dp', 1, 1, tiled=True)]
    all_to_all x2 -> x1, waiting for transfers between devices: 0.01 us -> 8.86 us  [body(): stats = lax.all_to_all(stats, 'dp', 1, 1, tiled=True)]
  transfers between devices with their start and end apart: 4 -> 3, of which waited for: 2 -> 3; matrix products, arithmetic and copies ran while one was open for 39% -> 1% of each run, Pallas kernels for 0% -> 0%
where the time goes in v1:
time: 305 us; the launch traced here: 304 us
  waiting for transfers between devices  184 us (60%)
  blocking collectives  54.7 us (18%)
  matrix products  24.8 us (8%)
  between operations  15 us (5%)
  starting transfers between devices  9.61 us (3%)
  other arithmetic  9.59 us (3%)
  local copies, waits for them, and re-layouts  6.68 us (2%)
    all_gather x1, waiting for transfers between devices, body(): weight = lax.all_gather(head_weight, 'mp', axis=0, tiled=True)  87.6 us
    all_gather x1, waiting for transfers between devices, body(): block_rows = lax.all_gather(own_rows, 'dp', axis=0, tiled=True)  86.8 us
    all_to_all x1, blocking collectives, body(): lax.all_to_all(send, 'dp', 0, 0, tiled=True)  27.9 us
    dot_general x1, matrix products, body(): logits = jnp.dot(block_rows, weight, preferred_element_type=jnp.float32)  24.2 us
    unnamed x1, blocking collectives  13.6 us
    all_to_all x1, blocking collectives, body(): lax.all_to_all(ref_packed.reshape(ways, sub_len, width_dev), 'mp', 0, 2,...  13.2 us
    all_to_all x1, starting transfers between devices, body(): stats = lax.all_to_all(stats, 'dp', 1, 1, tiled=True)  9.53 us
    all_to_all x1, waiting for transfers between devices, body(): stats = lax.all_to_all(stats, 'dp', 1, 1, tiled=True)  8.86 us
  transfers between devices with their start and end apart: 3, of which 3 were waited for; matrix products, arithmetic and copies ran while one was open for 1% of the time, Pallas kernels for 0%

profile of v1, /device:TPU:1, one launch (start us, length us, event | category | flops | bytes accessed | tf_op | source)
XLA Modules:
  0.0 304.3 jit_solution(12371459190618607233)
XLA Ops:
  7.3 0.8 broadcast_multiply_fusion
  8.1 0.2 convert_reduce_fusion.1
  8.2 0.8 subtract_multiply_fusion.1
  9.0 0.1 add_select_fusion.1
  9.1 0.1 select_n.99
  9.3 1.3 copy.33
  10.5 0.2 reshape.220
  10.7 1.3 copy.34
  12.0 0.2 reshape.221
  12.2 0.3 convolution_convert_fusion.1
  12.5 0.3 convolution_convert_fusion
  12.9 27.9 %all_to_all.25 = bf16[32,8,1024]{2,1,0:T(8,128)(2,1)S(1)} all-to-all(bf16[32,8,1024]{2,1,0:T(8,128)(2,1)S(1)} %maximum_bitcast_fusion), channel_id=1, replica_groups=mesh['dp'=32,'mp'=8] {'dp'}, dimensions={0} | all-to-all | bytes 1048576 | tf_op jit(solution)/shard_map/all_to_all | solution.py:57
  40.8 13.2 %all_to_all.26 = bf16[8,32,512]{2,1,0:T(8,128)(2,1)S(1)} all-to-all(bf16[8,32,512]{2,1,0:T(8,128)(2,1)S(1)} %bitcast.31), channel_id=1, replica_groups=mesh['dp'=32,'mp'=8] {'mp'}, dimensions={0} | all-to-all | bytes 524288 | tf_op jit(solution)/shard_map/all_to_all | solution.py:61
  54.0 0.7 copy.39
  54.8 0.7 all-gather.5.cloned.1.call-update
  55.5 0.1 dynamic_slice.17
  55.7 0.1 lt.91
  55.8 0.1 broadcast_in_dim_reshape.2
  56.0 0.2 reduce_window_sum.11
  56.2 0.1 select_reduce_fusion.2
  56.3 0.1 fusion.5
  56.4 0.1 or.14
  56.5 0.1 copy.36
  56.7 0.2 broadcast_in_dim.45
  56.9 0.2 convert_reduce_fusion
  57.1 0.1 subtract_multiply_fusion
  57.2 0.2 add_select_fusion
  57.4 0.2 select_n.102
  57.6 0.6 dynamic-slice
  58.9 0.8 select_reduce_fusion.1
  59.7 0.2 fusion
  59.9 86.8 %all-gather.3.cloned.1.call-done = bf16[1024,4096]{1,0:T(8,128)(2,1)} async-done(((bf16[32,4096]{1,0:T(8,128)(2,1)}), bf16[1024,4096]{1,0:T(8,128)(2,1)}) %all-gather.3.cloned.1.call-update) | async-done | bytes 8388624 | tf_op jit(solution)/shard_map/all_gather | solution.py:64
  146.7 87.6 %all-gather.5.cloned.1.call-done = bf16[4096,2048]{1,0:T(8,128)(2,1)} async-done(((bf16[512,2048]{1,0:T(8,128)(2,1)}), bf16[4096,2048]{1,0:T(8,128)(2,1)}) %all-gather.5.cloned.1.call-update) | async-done | bytes 16777232 | tf_op jit(solution)/shard_map/all_gather | solution.py:65
  234.3 24.2 %fusion.12 = (f32[1024]{0:T(1024)S(1)}, f32[1024,2048]{1,0:T(8,128)}) fusion(bf16[1024,4096]{1,0:T(8,128)(2,1)} %all-gather.3.cloned.1.call-done, bf16[4096,2048]{1,0:T(8,128)(2,1)} %all-gather.5.cloned.1.call-done), kind=kOutput, calls=%fused_computation.58 | convolution fusion | flops 17181966336 | bytes 33558528 | tf_op jit(solution)/shard_map/dot_general | solution.py:86
  258.5 0.1 stack.34
  258.6 4.7 %exponential_reduce_fusion = (f32[1024]{0:T(1024)S(1)}, f32[1024]{0:T(1024)S(1)}) fusion(f32[1024,2048]{1,0:T(8,128)} %get-tuple-element.29, f32[1024]{0:T(1024)S(1)} %get-tuple-element.28, s32[1024]{0:T(1024)S(1)} %select_reduce_fusion.1, s32[2048]{0:T(1024)S(1)} %iota_add_fusion), kind=kLoop, calls=%fused_computation.1 | loop fusion | flops 10483712 | bytes 8413184 | tf_op jit(solution)/shard_map/reduce_sum | solution.py:89
  263.2 0.1 stack.35
  263.3 0.1 stack.36
  263.4 0.7 pad_maximum_fusion
  264.1 9.5 %all-to-all-start.2 = ((f32[3,32,32]{2,0,1:T(4,128)}), f32[3,32,32]{2,0,1:T(4,128)S(1)}, u32[]{:S(2)}, u32[]{:S(2)}) async-start(f32[3,32,32]{2,0,1:T(4,128)} %pad_maximum_fusion), calls=%async_computation.2 | async-start | bytes 131072 | tf_op jit(solution)/shard_map/all_to_all | solution.py:93
  273.6 8.9 %all-to-all-done.2 = f32[3,32,32]{2,0,1:T(4,128)S(1)} async-done(((f32[3,32,32]{2,0,1:T(4,128)}), f32[3,32,32]{2,0,1:T(4,128)S(1)}, u32[]{:S(2)}, u32[]{:S(2)}) %all-to-all-start.2) | async-done | bytes 12320 | tf_op jit(solution)/shard_map/all_to_all | solution.py:93
  282.6 0.1 subtract_dynamic-update-slice_fusion
  282.7 13.6 %all-reduce.1 = (f32[256]{0:T(256)S(1)}, f32[3,256]{1,0:T(4,128)S(1)}) all-reduce(f32[256]{0:T(256)S(1)} %subtract_dynamic-update-slice_fusion, f32[3,256]{1,0:T(4,128)S(1)} %pad_maximum_fusion.1), channel_id=1, replica_groups=mesh['dp'=32,'mp'=8] {'mp'}, use_global_device_ids=true, to_apply=%add | all-reduce | flops 1024 | bytes 8192
  296.4 0.1 fusion.10
  296.5 0.1 reshape.227
  296.6 0.1 slice_add_fusion.6
  296.7 0.1 stack.42
  296.8 0.7 reshape.228
  (41 shorter events, 0.7 us)
Async XLA Ops:
  7.2 49.3 %copy-start = (s32[2048,7]{0,1:T(8,128)S(1)}, s32[2048,7]{0,1:T(8,128)}, u32[]{:S(2)}) copy-start(s32[2048,7]{0,1:T(8,128)} %param.10) | copy-start | bytes 172036
  7.2 50.4 %copy-start.8 = (u32[256]{0:T(256)S(1)}, u32[256]{0:T(256)}, u32[]{:S(2)}) copy-start(u32[256]{0:T(256)} %constant.56) | copy-start | bytes 3076
  7.2 48.4 %copy-start.2 = (s32[2048]{0:T(1024)S(1)}, s32[2048]{0:T(1024)}, u32[]{:S(2)}) copy-start(s32[2048]{0:T(1024)} %param.12) | copy-start | bytes 24580
  7.2 48.3 %copy-start.1 = (s32[2048]{0:T(1024)S(1)}, s32[2048]{0:T(1024)}, u32[]{:S(2)}) copy-start(s32[2048]{0:T(1024)} %param.11) | copy-start | bytes 24580
  7.2 51.6 %copy-start.5 = (f32[512]{0:T(512)S(1)}, f32[512]{0:T(512)}, u32[]{:S(2)}) copy-start(f32[512]{0:T(512)} %param.18) | copy-start | bytes 6148
  7.2 51.6 %copy-start.4 = (f32[512]{0:T(512)S(1)}, f32[512]{0:T(512)}, u32[]{:S(2)}) copy-start(f32[512]{0:T(512)} %param.17) | copy-start | bytes 6148
  7.2 51.6 %copy-start.3 = (f32[512]{0:T(512)S(1)}, f32[512]{0:T(512)}, u32[]{:S(2)}) copy-start(f32[512]{0:T(512)} %param.16) | copy-start | bytes 6148
  7.2 139.5 %all-gather.3.cloned.1.call-start = ((), (), s32[]{:S(2)}) async-start(), calls=%async_computation.3 | async-start | bytes 8650752 | tf_op jit(solution)/shard_map/all_gather | solution.py:64
  54.7 179.6 %all-gather.5.cloned.1.call-start = ((), (), s32[]{:S(2)}) async-start(), calls=%async_computation.4 | async-start | bytes 18874368 | tf_op jit(solution)/shard_map/all_gather | solution.py:65
  258.5 37.9 %copy-start.6 = (f32[256]{0:T(256)S(1)}, f32[256]{0:T(256)}, u32[]{:S(2)}) copy-start(f32[256]{0:T(256)} %param.19) | copy-start | bytes 3076
  264.1 18.4 %all-to-all-start.2 = ((f32[3,32,32]{2,0,1:T(4,128)}), f32[3,32,32]{2,0,1:T(4,128)S(1)}, u32[]{:S(2)}, u32[]{:S(2)}) async-start(f32[3,32,32]{2,0,1:T(4,128)} %pad_maximum_fusion), calls=%async_computation.2 | async-start | bytes 131072 | tf_op jit(solution)/shard_map/all_to_all | solution.py:93
  296.3 1.2 copy-start.7
Sparse Core Ops, SparseCore 0:
  54.8 91.8 all-gather.2
  148.6 85.6 all-gather.4

commit v2 on v1

--- a/solution.py
+++ b/solution.py
@@ -58,11 +58,28 @@
     ref_packed = got[:, :width_dev]
     reward_packed = got[:, width_dev:]
 
-    own_rows = lax.all_to_all(
-        ref_packed.reshape(ways, sub_len, width_dev), "mp", 0, 2, tiled=True
-    ).reshape(sub_len, width_full)
+    chips = ways // 2
+    own_core = [head_weight] + [
+        lax.ppermute(head_weight, "mp", [(i, (i + 2 * shift) % ways) for i in range(ways)])
+        for shift in range(1, chips)
+    ]
+    mate_core = [lax.ppermute(block, "mp", [(i, i ^ 1) for i in range(ways)]) for block in own_core]
+    weight = jnp.concatenate(own_core + mate_core, axis=0)
+    chip, core = part // 2, part % 2
+    order = jnp.arange(ways, dtype=jnp.int32)
+    source_chip = (chip - order % chips) % chips
+    source_core = jnp.where(order < chips, core, 1 - core)
+    pick = (
+        (source_chip * 2 + source_core)[:, None] == jnp.arange(ways, dtype=jnp.int32)[None, :]
+    ).astype(jnp.bfloat16)
+
+    parts_rows = lax.all_to_all(
+        ref_packed.reshape(ways, sub_len, width_dev), "mp", 0, 0, tiled=True
+    )
+    own_rows = jnp.einsum(
+        "msf,nm->snf", parts_rows, pick, preferred_element_type=jnp.float32
+    ).astype(jnp.bfloat16).reshape(sub_len, width_full)
     block_rows = lax.all_gather(own_rows, "dp", axis=0, tiled=True)
-    weight = lax.all_gather(head_weight, "mp", axis=0, tiled=True)
 
     first_src = part * blocks
     dest4 = lax.dynamic_slice_in_dim(pack_dest, first_src * req_dev, blocks * req_dev).reshape(

time: 305 us -> 244 us (0.80)
  waiting for transfers between devices: 184 us -> 56.3 us
  starting transfers between devices: 9.61 us -> 62.7 us
  local copies, waits for them, and re-layouts: 6.68 us -> 32 us
  blocking collectives: 54.7 us -> 41.1 us
    all_gather x1 -> x0, waiting for transfers between devices: 87.6 us -> none  [body(): weight = lax.all_gather(head_weight, 'mp', axis=0, tiled=True)]
    all_gather x1, waiting for transfers between devices: 86.8 us -> 0.01 us  [body(): block_rows = lax.all_gather(own_rows, 'dp', axis=0, tiled=True)]
    ppermute x0 -> x7, starting transfers between devices: none -> 51.5 us  [the longest x4 48.6 us: body(): lax.ppermute(block, 'mp', [(i, i ^ 1) for i in range(ways)])]
    ppermute x0 -> x7, waiting for transfers between devices: none -> 40.7 us  [the longest x3 40.7 us: body(): lax.ppermute(head_weight, 'mp', [(i, (i + 2 * shift) % ways) for i in ran...]
    unnamed x23 -> x32, local copies, waits for them, and re-layouts: 3.93 us -> 24.7 us
    all_to_all x1 -> x0, blocking collectives: 13.2 us -> none  [body(): lax.all_to_all(ref_packed.reshape(ways, sub_len, width_dev), 'mp', 0, 2,...]
    all_to_all x0 -> x1, starting transfers between devices: none -> 6.89 us  [body(): lax.all_to_all(ref_packed.reshape(ways, sub_len, width_dev), 'mp', 0, 0,...]
    all_to_all x0 -> x1, waiting for transfers between devices: none -> 6.45 us  [body(): lax.all_to_all(ref_packed.reshape(ways, sub_len, width_dev), 'mp', 0, 0,...]
  transfers between devices with their start and end apart: 3 -> 10, of which waited for: 3 -> 3; matrix products, arithmetic and copies ran while one was open for 1% -> 11% of each run, Pallas kernels for 0% -> 0%
where the time goes in v2:
time: 244 us; the launch traced here: 243 us
  starting transfers between devices  62.7 us (26%)
  waiting for transfers between devices  56.3 us (23%)
  blocking collectives  41.1 us (17%)
  local copies, waits for them, and re-layouts  32 us (13%)
  matrix products  26.1 us (11%)
  between operations  15 us (6%)
  other arithmetic  9.72 us (4%)
    ppermute x4, starting transfers between devices, body(): lax.ppermute(block, 'mp', [(i, i ^ 1) for i in range(ways)])  48.6 us
    ppermute x3, waiting for transfers between devices, body(): lax.ppermute(head_weight, 'mp', [(i, (i + 2 * shift) % ways) for i in ran...  40.7 us
    all_to_all x1, blocking collectives, body(): lax.all_to_all(send, 'dp', 0, 0, tiled=True)  27.9 us
    unnamed x32, local copies, waits for them, and re-layouts  24.7 us
    dot_general x1, matrix products, body(): logits = jnp.dot(block_rows, weight, preferred_element_type=jnp.float32)  24.2 us
    unnamed x1, blocking collectives  13.2 us
    all_to_all x1, waiting for transfers between devices, body(): stats = lax.all_to_all(stats, 'dp', 1, 1, tiled=True)  9.1 us
    all_to_all x1, starting transfers between devices, body(): lax.all_to_all(ref_packed.reshape(ways, sub_len, width_dev), 'mp', 0, 0,...  6.89 us
  transfers between devices with their start and end apart: 10, of which 3 were waited for; matrix products, arithmetic and copies ran while one was open for 11% of the time, Pallas kernels for 0%

profile of v2, /device:TPU:1, one launch (start us, length us, event | category | flops | bytes accessed | tf_op | source)
XLA Modules:
  0.0 243.0 jit_solution(11740245064365972340)
XLA Ops:
  7.3 0.9 broadcast_multiply_fusion
  8.2 0.2 convert_reduce_fusion.1
  8.3 0.8 subtract_multiply_fusion.1
  9.2 0.1 select_n.141
  9.4 1.3 copy.30
  10.6 0.2 reshape.245
  10.8 1.3 copy.31
  12.1 0.9 reshape.246
  13.0 0.3 convolution_convert_fusion.2
  13.3 1.3 convolution_convert_fusion.1
  14.7 27.9 %all_to_all.15 = bf16[32,8,1024]{2,1,0:T(8,128)(2,1)S(1)} all-to-all(bf16[32,8,1024]{2,1,0:T(8,128)(2,1)S(1)} %maximum_bitcast_fusion), channel_id=1, replica_groups=mesh['dp'=32,'mp'=8] {'dp'}, dimensions={0} | all-to-all | bytes 1048576 | tf_op jit(solution)/shard_map/all_to_all | solution.py:57
  42.7 0.7 slice.89
  43.4 6.9 %all-to-all-start.1 = ((bf16[8,32,512]{2,1,0:T(8,128)(2,1)}), bf16[8,32,512]{2,1,0:T(8,128)(2,1)S(1)}, u32[]{:S(2)}, u32[]{:S(2)}) async-start(bf16[8,32,512]{2,1,0:T(8,128)(2,1)} %bitcast.3), calls=%async_computation.1 | async-start | bytes 524288 | tf_op jit(solution)/shard_map/all_to_all | solution.py:76
  50.3 6.5 %all-to-all-done.1 = bf16[8,32,512]{2,1,0:T(8,128)(2,1)S(1)} async-done(((bf16[8,32,512]{2,1,0:T(8,128)(2,1)}), bf16[8,32,512]{2,1,0:T(8,128)(2,1)S(1)}, u32[]{:S(2)}, u32[]{:S(2)}) %all-to-all-start.1) | async-done | bytes 262176 | tf_op jit(solution)/shard_map/all_to_all | solution.py:76
  56.7 0.3 convolution_convert_fusion
  57.0 0.8 copy.36
  57.9 0.4 collective-permute-start
  58.2 1.8 collective-permute-start.1
  60.0 0.7 collective-permute-start.2
  60.7 1.6 collective-permute-start.3
  62.8 0.2 reduce_window_sum.11
  63.1 0.2 convert_reduce_fusion
  63.5 0.2 add_select_fusion
  63.7 1.6 constant_dynamic-update-slice_fusion.7
  65.3 40.7 %collective-permute-done = bf16[512,2048]{1,0:T(8,128)(2,1)} collective-permute-done((bf16[512,2048]{1,0:T(8,128)(2,1)S(1)}, bf16[512,2048]{1,0:T(8,128)(2,1)}, u32[]{:S(2)}, u32[]{:S(2)}) %collective-permute-start) | collective-permute-done | bytes 2097184 | tf_op jit(solution)/shard_map/ppermute | solution.py:63
  106.0 46.2 %collective-permute-start.4 = (bf16[512,2048]{1,0:T(8,128)(2,1)}, bf16[512,2048]{1,0:T(8,128)(2,1)}, u32[]{:S(2)}, u32[]{:S(2)}) collective-permute-start(bf16[512,2048]{1,0:T(8,128)(2,1)} %collective-permute-done), channel_id=1, source_target_pairs={{0,1},{1,0},{2,3},{3,2},{4,5},{5,4},{6,7},{7,6},{8,9},{9,8},{10,11... | collective-permute-start | bytes 6291464 | tf_op jit(solution)/shard_map/ppermute | solution.py:66
  152.4 0.7 collective-permute-start.6
  153.1 0.2 select_n.144
  153.3 0.1 copy.33
  153.5 0.2 broadcast_in_dim.85
  153.8 0.6 dynamic-slice
  155.0 0.8 select_reduce_fusion.1
  155.9 0.2 fusion
  156.1 3.1 %constant_dynamic-update-slice_fusion.6 = bf16[4096,2048]{1,0:T(8,128)(2,1)} fusion(bf16[4096,2048]{1,0:T(8,128)(2,1)} %constant_dynamic-update-slice_fusion.7, bf16[512,2048]{1,0:T(8,128)(2,1)} %collective-permute-done), kind=kLoop, calls=%fused_computation.32 | loop fusion | bytes 4194304
  159.2 3.2 %constant_dynamic-update-slice_fusion.5 = bf16[4096,2048]{1,0:T(8,128)(2,1)} fusion(bf16[4096,2048]{1,0:T(8,128)(2,1)} %constant_dynamic-update-slice_fusion.6, bf16[512,2048]{1,0:T(8,128)(2,1)} %collective-permute-done.1), kind=kLoop, calls=%fused_computation.31 | loop fusion | bytes 4194304
  162.4 3.2 %constant_dynamic-update-slice_fusion.4 = bf16[4096,2048]{1,0:T(8,128)(2,1)} fusion(bf16[4096,2048]{1,0:T(8,128)(2,1)} %constant_dynamic-update-slice_fusion.5, bf16[512,2048]{1,0:T(8,128)(2,1)} %collective-permute-done.2), kind=kLoop, calls=%fused_computation.30 | loop fusion | bytes 4194304
  165.6 3.2 %constant_dynamic-update-slice_fusion.3 = bf16[4096,2048]{1,0:T(8,128)(2,1)} fusion(bf16[4096,2048]{1,0:T(8,128)(2,1)} %constant_dynamic-update-slice_fusion.4, bf16[512,2048]{1,0:T(8,128)(2,1)} %collective-permute-done.3), kind=kLoop, calls=%fused_computation.29 | loop fusion | bytes 4194304
  168.8 3.1 %constant_dynamic-update-slice_fusion.2 = bf16[4096,2048]{1,0:T(8,128)(2,1)} fusion(bf16[4096,2048]{1,0:T(8,128)(2,1)} %constant_dynamic-update-slice_fusion.3, bf16[512,2048]{1,0:T(8,128)(2,1)} %collective-permute-done.4), kind=kLoop, calls=%fused_computation.28 | loop fusion | bytes 4194304
  171.9 3.2 %constant_dynamic-update-slice_fusion.1 = bf16[4096,2048]{1,0:T(8,128)(2,1)} fusion(bf16[4096,2048]{1,0:T(8,128)(2,1)} %constant_dynamic-update-slice_fusion.2, bf16[512,2048]{1,0:T(8,128)(2,1)} %collective-permute-done.5), kind=kLoop, calls=%fused_computation.27 | loop fusion | bytes 4194304
  175.1 3.2 %constant_dynamic-update-slice_fusion = bf16[4096,2048]{1,0:T(8,128)(2,1)} fusion(bf16[4096,2048]{1,0:T(8,128)(2,1)} %constant_dynamic-update-slice_fusion.1, bf16[512,2048]{1,0:T(8,128)(2,1)} %collective-permute-done.6), kind=kLoop, calls=%fused_computation.26 | loop fusion | bytes 4194304 | tf_op jit(solution)/shard_map/concatenate | solution.py:67
  178.3 24.2 %fusion.20 = (f32[1024]{0:T(1024)S(1)}, f32[1024,2048]{1,0:T(8,128)}) fusion(bf16[1024,4096]{1,0:T(8,128)(2,1)} %all-gather.2.cloned.1.call-done, bf16[4096,2048]{1,0:T(8,128)(2,1)} %constant_dynamic-update-slice_fusion), kind=kOutput, calls=%fused_computation.80 | convolution fusion | flops 17181966336 | bytes 33558528 | tf_op jit(solution)/shard_map/dot_general | solution.py:103
  202.6 4.6 %exponential_reduce_fusion = (f32[1024]{0:T(1024)S(1)}, f32[1024]{0:T(1024)S(1)}) fusion(f32[1024,2048]{1,0:T(8,128)} %get-tuple-element.29, f32[1024]{0:T(1024)S(1)} %get-tuple-element.28, s32[1024]{0:T(1024)S(1)} %select_reduce_fusion.1, s32[2048]{0:T(1024)S(1)} %iota_add_fusion), kind=kLoop, calls=%fused_computation.1 | loop fusion | flops 10483712 | bytes 8413184 | tf_op jit(solution)/shard_map/reduce_sum | solution.py:106
  207.4 0.7 pad_maximum_fusion
  208.1 4.4 %all-to-all-start.2 = ((f32[3,32,32]{2,0,1:T(4,128)}), f32[3,32,32]{2,0,1:T(4,128)S(1)}, u32[]{:S(2)}, u32[]{:S(2)}) async-start(f32[3,32,32]{2,0,1:T(4,128)} %pad_maximum_fusion), calls=%async_computation.2 | async-start | bytes 131072 | tf_op jit(solution)/shard_map/all_to_all | solution.py:110
  212.5 9.1 %all-to-all-done.2 = f32[3,32,32]{2,0,1:T(4,128)S(1)} async-done(((f32[3,32,32]{2,0,1:T(4,128)}), f32[3,32,32]{2,0,1:T(4,128)S(1)}, u32[]{:S(2)}, u32[]{:S(2)}) %all-to-all-start.2) | async-done | bytes 12320 | tf_op jit(solution)/shard_map/all_to_all | solution.py:110
  221.8 13.2 %all-reduce.1 = (f32[256]{0:T(256)S(1)}, f32[3,256]{1,0:T(4,128)S(1)}) all-reduce(f32[256]{0:T(256)S(1)} %subtract_dynamic-update-slice_fusion, f32[3,256]{1,0:T(4,128)S(1)} %pad_maximum_fusion.1), channel_id=1, replica_groups=mesh['dp'=32,'mp'=8] {'mp'}, use_global_device_ids=true, to_apply=%add | all-reduce | flops 1024 | bytes 8192
  235.2 0.1 slice_add_fusion.6
  235.5 0.7 reshape.253
  (65 shorter events, 2.0 us)
Async XLA Ops:
  7.2 145.3 %copy-start = (s32[2048,7]{0,1:T(8,128)S(1)}, s32[2048,7]{0,1:T(8,128)}, u32[]{:S(2)}) copy-start(s32[2048,7]{0,1:T(8,128)} %param.10) | copy-start | bytes 172036
  7.2 146.6 %copy-start.9 = (u32[256]{0:T(256)S(1)}, u32[256]{0:T(256)}, u32[]{:S(2)}) copy-start(u32[256]{0:T(256)} %constant.99) | copy-start | bytes 3076
  7.2 55.1 %copy-start.3 = (s32[2048]{0:T(1024)S(1)}, s32[2048]{0:T(1024)}, u32[]{:S(2)}) copy-start(s32[2048]{0:T(1024)} %param.12) | copy-start | bytes 24580
  7.2 55.2 %copy-start.2 = (s32[2048]{0:T(1024)S(1)}, s32[2048]{0:T(1024)}, u32[]{:S(2)}) copy-start(s32[2048]{0:T(1024)} %param.11) | copy-start | bytes 24580
  7.2 50.6 %copy-start.1 = (bf16[512,2048]{1,0:T(8,128)(2,1)S(1)}, bf16[512,2048]{1,0:T(8,128)(2,1)}, u32[]{:S(2)}) copy-start(bf16[512,2048]{1,0:T(8,128)(2,1)} %param.15) | copy-start | bytes 6291460
  7.2 56.2 %copy-start.4 = (f32[512]{0:T(512)S(1)}, f32[512]{0:T(512)}, u32[]{:S(2)}) copy-start(f32[512]{0:T(512)} %param.16) | copy-start | bytes 6148
  7.2 56.2 %copy-start.5 = (f32[512]{0:T(512)S(1)}, f32[512]{0:T(512)}, u32[]{:S(2)}) copy-start(f32[512]{0:T(512)} %param.17) | copy-start | bytes 6148
  7.2 56.2 %copy-start.6 = (f32[512]{0:T(512)S(1)}, f32[512]{0:T(512)}, u32[]{:S(2)}) copy-start(f32[512]{0:T(512)} %param.18) | copy-start | bytes 6148
  43.4 13.4 %all-to-all-start.1 = ((bf16[8,32,512]{2,1,0:T(8,128)(2,1)}), bf16[8,32,512]{2,1,0:T(8,128)(2,1)S(1)}, u32[]{:S(2)}, u32[]{:S(2)}) async-start(bf16[8,32,512]{2,1,0:T(8,128)(2,1)} %bitcast.3), calls=%async_computation.1 | async-start | bytes 524288 | tf_op jit(solution)/shard_map/all_to_all | solution.py:76
  50.3 128.0 %all-gather.2.cloned.1.call-start = ((), (), s32[]{:S(2)}) async-start(), calls=%async_computation.3 | async-start | bytes 8650752 | tf_op jit(solution)/shard_map/all_gather | solution.py:82
  57.9 48.1 %collective-permute-start = (bf16[512,2048]{1,0:T(8,128)(2,1)S(1)}, bf16[512,2048]{1,0:T(8,128)(2,1)}, u32[]{:S(2)}, u32[]{:S(2)}) collective-permute-start(bf16[512,2048]{1,0:T(8,128)(2,1)S(1)} %copy-done.1), channel_id=1, source_target_pairs={{0,2},{1,3},{2,4},{3,5},{4,6},{5,7},{6,0},{7,1},{8,10},{9,11},{10,... | collective-permute-start | bytes 6291464 | tf_op jit(solution)/shard_map/ppermute | solution.py:63
  58.2 94.0 %collective-permute-start.1 = (bf16[512,2048]{1,0:T(8,128)(2,1)S(1)}, bf16[512,2048]{1,0:T(8,128)(2,1)}, u32[]{:S(2)}, u32[]{:S(2)}) collective-permute-start(bf16[512,2048]{1,0:T(8,128)(2,1)S(1)} %copy-done.1), channel_id=1, source_target_pairs={{0,4},{1,5},{2,6},{3,7},{4,0},{5,1},{6,2},{7,3},{8,12},{9,13},{10,... | collective-permute-start | bytes 6291464 | tf_op jit(solution)/shard_map/ppermute | solution.py:63
  60.0 92.4 %collective-permute-start.2 = (bf16[512,2048]{1,0:T(8,128)(2,1)S(1)}, bf16[512,2048]{1,0:T(8,128)(2,1)}, u32[]{:S(2)}, u32[]{:S(2)}) collective-permute-start(bf16[512,2048]{1,0:T(8,128)(2,1)S(1)} %copy-done.1), channel_id=1, source_target_pairs={{0,6},{1,7},{2,0},{3,1},{4,2},{5,3},{6,4},{7,5},{8,14},{9,15},{10,... | collective-permute-start | bytes 6291464 | tf_op jit(solution)/shard_map/ppermute | solution.py:63
  60.7 104.8 %collective-permute-start.3 = (bf16[512,2048]{1,0:T(8,128)(2,1)S(1)}, bf16[512,2048]{1,0:T(8,128)(2,1)}, u32[]{:S(2)}, u32[]{:S(2)}) collective-permute-start(bf16[512,2048]{1,0:T(8,128)(2,1)S(1)} %copy-done.1), channel_id=1, source_target_pairs={{0,1},{1,0},{2,3},{3,2},{4,5},{5,4},{6,7},{7,6},{8,9},{9,8},{10,11... | collective-permute-start | bytes 6291464 | tf_op jit(solution)/shard_map/ppermute | solution.py:66
  106.0 62.8 %collective-permute-start.4 = (bf16[512,2048]{1,0:T(8,128)(2,1)}, bf16[512,2048]{1,0:T(8,128)(2,1)}, u32[]{:S(2)}, u32[]{:S(2)}) collective-permute-start(bf16[512,2048]{1,0:T(8,128)(2,1)} %collective-permute-done), channel_id=1, source_target_pairs={{0,1},{1,0},{2,3},{3,2},{4,5},{5,4},{6,7},{7,6},{8,9},{9,8},{10,11... | collective-permute-start | bytes 6291464 | tf_op jit(solution)/shard_map/ppermute | solution.py:66
  152.3 19.7 %collective-permute-start.5 = (bf16[512,2048]{1,0:T(8,128)(2,1)}, bf16[512,2048]{1,0:T(8,128)(2,1)}, u32[]{:S(2)}, u32[]{:S(2)}) collective-permute-start(bf16[512,2048]{1,0:T(8,128)(2,1)} %collective-permute-done.1), channel_id=1, source_target_pairs={{0,1},{1,0},{2,3},{3,2},{4,5},{5,4},{6,7},{7,6},{8,9},{9,8},{10,11... | collective-permute-start | bytes 6291464 | tf_op jit(solution)/shard_map/ppermute | solution.py:66
  152.4 22.7 %collective-permute-start.6 = (bf16[512,2048]{1,0:T(8,128)(2,1)}, bf16[512,2048]{1,0:T(8,128)(2,1)}, u32[]{:S(2)}, u32[]{:S(2)}) collective-permute-start(bf16[512,2048]{1,0:T(8,128)(2,1)} %collective-permute-done.2), channel_id=1, source_target_pairs={{0,1},{1,0},{2,3},{3,2},{4,5},{5,4},{6,7},{7,6},{8,9},{9,8},{10,11... | collective-permute-start | bytes 6291464 | tf_op jit(solution)/shard_map/ppermute | solution.py:66
  202.5 32.6 %copy-start.7 = (f32[256]{0:T(256)S(1)}, f32[256]{0:T(256)}, u32[]{:S(2)}) copy-start(f32[256]{0:T(256)} %param.19) | copy-start | bytes 3076
  208.1 13.5 %all-to-all-start.2 = ((f32[3,32,32]{2,0,1:T(4,128)}), f32[3,32,32]{2,0,1:T(4,128)S(1)}, u32[]{:S(2)}, u32[]{:S(2)}) async-start(f32[3,32,32]{2,0,1:T(4,128)} %pad_maximum_fusion), calls=%async_computation.2 | async-start | bytes 131072 | tf_op jit(solution)/shard_map/all_to_all | solution.py:110
  235.0 1.2 copy-start.8
Sparse Core Ops, SparseCore 0:
  58.0 91.7 all-gather.1

commit v3 on v2

--- a/solution.py
+++ b/solution.py
@@ -1,6 +1,8 @@
 import jax
 import jax.numpy as jnp
 from jax import lax
+from jax.experimental import pallas as pl
+from jax.experimental.pallas import tpu as pltpu
 from jax.sharding import PartitionSpec as P
 
 kl_coef = 0.1
@@ -15,6 +17,51 @@
     same = dest[..., None, :] == dest[..., :, None]
     earlier = idx[None, :] < idx[:, None]
     return jnp.sum(jnp.logical_and(same, earlier).astype(jnp.int32), axis=-1)
+
+
+def stats_kernel(pieces, tile_n, target_ref, rows_ref, *refs):
+    weight_refs = refs[:pieces]
+    max_ref, total_ref, target_logit_ref = refs[pieces:]
+    width = weight_refs[0].shape[0]
+    logits = jnp.dot(rows_ref[:, 0:width], weight_refs[0][...], preferred_element_type=jnp.float32)
+    for k in range(1, pieces):
+        logits = logits + jnp.dot(
+            rows_ref[:, k * width : (k + 1) * width],
+            weight_refs[k][...],
+            preferred_element_type=jnp.float32,
+        )
+    row_max = jnp.max(logits, axis=1, keepdims=True)
+    total = jnp.sum(jnp.exp(logits - row_max), axis=1, keepdims=True)
+    column = lax.broadcasted_iota(jnp.int32, logits.shape, 1) + pl.program_id(0) * tile_n
+    target_logit = jnp.sum(jnp.where(column == target_ref[...], logits, 0.0), axis=1, keepdims=True)
+    max_ref[0] = row_max
+    total_ref[0] = total
+    target_logit_ref[0] = target_logit
+
+
+def logit_stats(rows, pieces, local_target, tile_m=256, tile_n=1024):
+    count, width_full = rows.shape
+    width, vocab = pieces[0].shape
+    grid = (vocab // tile_n, count // tile_m)
+    stat_shape = jax.ShapeDtypeStruct((grid[0], count, 1), jnp.float32)
+    stat_spec = pl.BlockSpec((1, tile_m, 1), lambda j, i: (j, i, 0))
+    return pl.pallas_call(
+        lambda *refs: stats_kernel(len(pieces), tile_n, *refs),
+        grid=grid,
+        in_specs=[
+            pl.BlockSpec((tile_m, 1), lambda j, i: (i, 0)),
+            pl.BlockSpec((tile_m, width_full), lambda j, i: (i, 0)),
+        ]
+        + [pl.BlockSpec((width, tile_n), lambda j, i: (0, j)) for _ in pieces],
+        out_specs=[stat_spec, stat_spec, stat_spec],
+        out_shape=[stat_shape, stat_shape, stat_shape],
+        compiler_params=pltpu.CompilerParams(vmem_limit_bytes=48 * 1024 * 1024),
+        cost_estimate=pl.CostEstimate(
+            flops=2 * count * width_full * vocab,
+            transcendentals=count * vocab,
+            bytes_accessed=2 * width_full * vocab + 2 * count * width_full * grid[0],
+        ),
+    )(local_target.reshape(count, 1), rows, *pieces)
 
 
 def body(
@@ -64,7 +111,6 @@
         for shift in range(1, chips)
     ]
     mate_core = [lax.ppermute(block, "mp", [(i, i ^ 1) for i in range(ways)]) for block in own_core]
-    weight = jnp.concatenate(own_core + mate_core, axis=0)
     chip, core = part // 2, part % 2
     order = jnp.arange(ways, dtype=jnp.int32)
     source_chip = (chip - order % chips) % chips
@@ -100,12 +146,13 @@
     hits = key[None, :] == jnp.arange(shards * sub_len, dtype=jnp.int32)[:, None]
     targets = jnp.sum(jnp.where(hits, tok4.reshape(-1)[None, :], 0), axis=1)
 
-    logits = jnp.dot(block_rows, weight, preferred_element_type=jnp.float32)
     vocab_dev = head_weight.shape[1]
-    row_max = jnp.max(logits, axis=1)
-    exp_total = jnp.sum(jnp.exp(logits - row_max[:, None]), axis=1)
-    column = jnp.arange(vocab_dev, dtype=jnp.int32)[None, :] + me * vocab_dev
-    target_logit = jnp.sum(jnp.where(column == targets[:, None], logits, 0.0), axis=1)
+    tile_max, tile_total, tile_target = logit_stats(
+        block_rows, own_core + mate_core, targets - me * vocab_dev
+    )
+    row_max = jnp.max(tile_max[:, :, 0], axis=0)
+    exp_total = jnp.sum(tile_total[:, :, 0] * jnp.exp(tile_max[:, :, 0] - row_max[None, :]), axis=0)
+    target_logit = jnp.sum(tile_target[:, :, 0], axis=0)
     stats = jnp.stack([row_max, exp_total, target_logit]).reshape(3, shards, sub_len)
     stats = lax.all_to_all(stats, "dp", 1, 1, tiled=True)
     joint_max = jnp.max(stats[0], axis=0)

time: 244 us -> 220 us (0.902)
  waiting for transfers between devices: 56.3 us -> 99.9 us
  starting transfers between devices: 62.7 us -> 21.6 us
  Pallas kernels: 0 us -> 25.6 us
  matrix products: 26.1 us -> 0.91 us
  local copies, waits for them, and re-layouts: 32 us -> 8.23 us
  other arithmetic: 9.72 us -> 6.07 us
    ppermute x3, waiting for transfers between devices: 40.7 us -> 84.4 us  [body(): lax.ppermute(head_weight, 'mp', [(i, (i + 2 * shift) % ways) for i in ran...]
    ppermute x4, starting transfers between devices: 48.6 us -> 8.2 us  [body(): lax.ppermute(block, 'mp', [(i, i ^ 1) for i in range(ways)])]
    pallas_call x0 -> x1, Pallas kernels: none -> 25.6 us  [logit_stats(): pl.pallas_call(lambda *refs: stats_kernel(len(pieces), tile_n, *refs), gr...]
    dot_general x1 -> x0, matrix products: 24.2 us -> none  [body(): logits = jnp.dot(block_rows, weight, preferred_element_type=jnp.float32)]
    unnamed x32 -> x29, local copies, waits for them, and re-layouts: 24.7 us -> 4.57 us
    reduce_sum x1 -> x2, other arithmetic: 4.64 us -> 0.24 us  [the longest x1 0.21 us: body(): target_logit = jnp.sum(tile_target[:, :, 0], axis=0)]
    concatenate x1 -> x0, local copies, waits for them, and re-layouts: 3.17 us -> none  [body(): weight = jnp.concatenate(own_core + mate_core, axis=0)]
  transfers between devices with their start and end apart: 10 -> 10, of which waited for: 3 -> 5; matrix products, arithmetic and copies ran while one was open for 11% -> 2% of each run, Pallas kernels for 0% -> 0%
where the time goes in v3:
time: 220 us
  waiting for transfers between devices  99.9 us (45%)
  blocking collectives  42.5 us (19%)
  Pallas kernels  25.6 us (12%)
  starting transfers between devices  21.6 us (10%)
  between operations  15.1 us (7%)
  local copies, waits for them, and re-layouts  8.23 us (4%)
  other arithmetic  6.07 us (3%)
    ppermute x3, waiting for transfers between devices, body(): lax.ppermute(head_weight, 'mp', [(i, (i + 2 * shift) % ways) for i in ran...  84.4 us
    all_to_all x1, blocking collectives, body(): lax.all_to_all(send, 'dp', 0, 0, tiled=True)  28.1 us
    pallas_call x1, Pallas kernels, logit_stats(): pl.pallas_call(lambda *refs: stats_kernel(len(pieces), tile_n, *refs), gr...  25.6 us
    unnamed x1, blocking collectives  14.4 us
    all_to_all x1, waiting for transfers between devices, body(): stats = lax.all_to_all(stats, 'dp', 1, 1, tiled=True)  8.8 us
    ppermute x4, starting transfers between devices, body(): lax.ppermute(block, 'mp', [(i, i ^ 1) for i in range(ways)])  8.2 us
    all_to_all x1, starting transfers between devices, body(): lax.all_to_all(ref_packed.reshape(ways, sub_len, width_dev), 'mp', 0, 0,...  6.89 us
    all_to_all x1, waiting for transfers between devices, body(): lax.all_to_all(ref_packed.reshape(ways, sub_len, width_dev), 'mp', 0, 0,...  6.45 us
  transfers between devices with their start and end apart: 10, of which 5 were waited for; matrix products, arithmetic and copies ran while one was open for 2% of the time, Pallas kernels for 0%

profile of v3, /device:TPU:1, one launch (start us, length us, event | category | flops | bytes accessed | tf_op | source)
XLA Modules:
  0.0 220.0 jit_solution(1600843790641450256)
XLA Ops:
  7.2 0.8 broadcast_multiply_fusion
  8.0 0.2 convert_reduce_fusion.1
  8.2 0.8 subtract_multiply_fusion.1
  9.1 0.1 select_n.141
  9.2 1.3 copy.33
  10.5 0.2 reshape.249
  10.7 0.3 copy.34
  10.9 0.2 reshape.250
  11.1 0.3 convolution_convert_fusion.2
  11.4 0.3 convolution_convert_fusion.1
  11.8 28.1 %all_to_all.15 = bf16[32,8,1024]{2,1,0:T(8,128)(2,1)S(1)} all-to-all(bf16[32,8,1024]{2,1,0:T(8,128)(2,1)S(1)} %maximum_bitcast_fusion), channel_id=1, replica_groups=mesh['dp'=32,'mp'=8] {'dp'}, dimensions={0} | all-to-all | bytes 1048576 | tf_op jit(solution)/shard_map/all_to_all | solution.py:104
  39.9 0.7 slice.89
  40.6 6.9 %all-to-all-start.1 = ((bf16[8,32,512]{2,1,0:T(8,128)(2,1)}), bf16[8,32,512]{2,1,0:T(8,128)(2,1)S(1)}, u32[]{:S(2)}, u32[]{:S(2)}) async-start(bf16[8,32,512]{2,1,0:T(8,128)(2,1)} %bitcast.4), calls=%async_computation.1 | async-start | bytes 524288 | tf_op jit(solution)/shard_map/all_to_all | solution.py:122
  47.5 6.5 %all-to-all-done.1 = bf16[8,32,512]{2,1,0:T(8,128)(2,1)S(1)} async-done(((bf16[8,32,512]{2,1,0:T(8,128)(2,1)}), bf16[8,32,512]{2,1,0:T(8,128)(2,1)S(1)}, u32[]{:S(2)}, u32[]{:S(2)}) %all-to-all-start.1) | async-done | bytes 262176 | tf_op jit(solution)/shard_map/all_to_all | solution.py:122
  54.0 0.3 convolution_convert_fusion
  54.3 0.8 copy.39
  55.1 1.0 collective-permute-start.2
  56.1 1.2 collective-permute-start.1
  57.3 1.6 collective-permute-start.3
  59.3 0.2 reduce_window_sum.11
  59.5 0.1 select_reduce_fusion.1
  59.7 41.8 %collective-permute-done.2.refs_5_ = bf16[512,2048]{1,0:T(8,128)(2,1)} collective-permute-done((bf16[512,2048]{1,0:T(8,128)(2,1)S(1)}, bf16[512,2048]{1,0:T(8,128)(2,1)}, u32[]{:S(2)}, u32[]{:S(2)}) %collective-permute-start.2) | collective-permute-done | bytes 2097184 | tf_op jit(solution)/shard_map/ppermute | solution.py:110
  101.4 3.4 %collective-permute-start.6 = (bf16[512,2048]{1,0:T(8,128)(2,1)}, bf16[512,2048]{1,0:T(8,128)(2,1)}, u32[]{:S(2)}, u32[]{:S(2)}) collective-permute-start(bf16[512,2048]{1,0:T(8,128)(2,1)} %collective-permute-done.2.refs_5_), channel_id=1, source_target_pairs={{0,1},{1,0},{2,3},{3,2},{4,5},{5,4},{6,7},{7,6},{8,9},{9,8},{10,11... | collective-permute-start | bytes 6291464 | tf_op jit(solution)/shard_map/ppermute | solution.py:113
  104.8 2.7 %collective-permute-start.5 = (bf16[512,2048]{1,0:T(8,128)(2,1)}, bf16[512,2048]{1,0:T(8,128)(2,1)}, u32[]{:S(2)}, u32[]{:S(2)}) collective-permute-start(bf16[512,2048]{1,0:T(8,128)(2,1)} %collective-permute-done.1.refs_4_), channel_id=1, source_target_pairs={{0,1},{1,0},{2,3},{3,2},{4,5},{5,4},{6,7},{7,6},{8,9},{9,8},{10,11... | collective-permute-start | bytes 6291464 | tf_op jit(solution)/shard_map/ppermute | solution.py:113
  107.5 42.6 %collective-permute-done.refs_3_ = bf16[512,2048]{1,0:T(8,128)(2,1)} collective-permute-done((bf16[512,2048]{1,0:T(8,128)(2,1)S(1)}, bf16[512,2048]{1,0:T(8,128)(2,1)}, u32[]{:S(2)}, u32[]{:S(2)}) %collective-permute-start) | collective-permute-done | bytes 2097184 | tf_op jit(solution)/shard_map/ppermute | solution.py:110
  150.2 0.5 collective-permute-start.4
  150.9 0.1 copy.32
  151.0 0.2 broadcast_in_dim.76
  151.3 0.2 convert_reduce_fusion
  151.6 0.2 add_select_fusion
  151.7 0.2 select_n.132
  151.9 0.8 select_reduce_fusion
  152.8 0.2 copy.36.refs_0_
  153.0 0.6 dynamic-slice
  154.3 0.2 fusion
  154.5 0.3 collective-permute-done.4.refs_7_
  154.8 1.6 copy-done.2
  156.4 25.6 %shard_map.113 = (f32[2,1024,1]{2,1,0:T(8,128)S(1)}, f32[2,1024,1]{2,1,0:T(8,128)S(1)}, f32[2,1024,1]{2,1,0:T(8,128)S(1)}) custom-call(s32[1024,1]{1,0:T(8,128)S(1)} %copy.36.refs_0_, bf16[1024,4096]{1,0:T(8,128)(2,1)} %all-gather.2.cloned.1.call-done.refs_1_, bf16[512,2048]{1,0:T(8,128)(2,1)S(1)} %copy-done.2, ...), custom_call_target="tpu_custom_call" | custom-call | flops 17179869184 | bytes 33554432 | tf_op jit(solution)/shard_map/pallas_call | solution.py:48
  182.0 0.5 fusion.19
  182.6 0.3 reduce.4
  183.1 0.2 reduce_sum.103
  183.4 0.7 pad_maximum_fusion
  184.1 4.4 %all-to-all-start.2 = ((f32[3,32,32]{2,0,1:T(4,128)}), f32[3,32,32]{2,0,1:T(4,128)S(1)}, u32[]{:S(2)}, u32[]{:S(2)}) async-start(f32[3,32,32]{2,0,1:T(4,128)} %pad_maximum_fusion), calls=%async_computation.2 | async-start | bytes 131072 | tf_op jit(solution)/shard_map/all_to_all | solution.py:157
  188.5 8.8 %all-to-all-done.2 = f32[3,32,32]{2,0,1:T(4,128)S(1)} async-done(((f32[3,32,32]{2,0,1:T(4,128)}), f32[3,32,32]{2,0,1:T(4,128)S(1)}, u32[]{:S(2)}, u32[]{:S(2)}) %all-to-all-start.2) | async-done | bytes 12320 | tf_op jit(solution)/shard_map/all_to_all | solution.py:157
  197.4 0.1 subtract_dynamic-update-slice_fusion
  197.5 14.4 %all-reduce.1 = (f32[256]{0:T(256)S(1)}, f32[3,256]{1,0:T(4,128)S(1)}) all-reduce(f32[256]{0:T(256)S(1)} %subtract_dynamic-update-slice_fusion, f32[3,256]{1,0:T(4,128)S(1)} %pad_maximum_fusion.1), channel_id=1, replica_groups=mesh['dp'=32,'mp'=8] {'mp'}, use_global_device_ids=true, to_apply=%add | all-reduce | flops 1024 | bytes 8192
  212.2 0.1 slice_add_fusion.6
  212.4 0.7 reshape.257
  (65 shorter events, 1.8 us)
Async XLA Ops:
  7.2 143.7 %copy-start = (s32[2048,7]{0,1:T(8,128)S(1)}, s32[2048,7]{0,1:T(8,128)}, u32[]{:S(2)}) copy-start(s32[2048,7]{0,1:T(8,128)} %param.10) | copy-start | bytes 172036
  7.2 3.5 %copy-start.3 = (bf16[64,7,512]{2,0,1:T(8,128)(2,1)S(1)}, bf16[64,7,512]{2,0,1:T(8,128)(2,1)}, u32[]{:S(2)}) copy-start(bf16[64,7,512]{2,0,1:T(8,128)(2,1)} %param.14) | copy-start | bytes 1376260
  11.7 43.4 %copy-start.1 = (bf16[512,2048]{1,0:T(8,128)(2,1)S(1)}, bf16[512,2048]{1,0:T(8,128)(2,1)}, u32[]{:S(2)}) copy-start(bf16[512,2048]{1,0:T(8,128)(2,1)} %refs_2_.1) | copy-start | bytes 6291460
  11.7 47.1 %copy-start.4 = (s32[2048]{0:T(1024)S(1)}, s32[2048]{0:T(1024)}, u32[]{:S(2)}) copy-start(s32[2048]{0:T(1024)} %param.11) | copy-start | bytes 24580
  11.8 47.2 %copy-start.5 = (s32[2048]{0:T(1024)S(1)}, s32[2048]{0:T(1024)}, u32[]{:S(2)}) copy-start(s32[2048]{0:T(1024)} %param.12) | copy-start | bytes 24580
  39.9 113.1 %copy-start.11 = (u32[256]{0:T(256)S(1)}, u32[256]{0:T(256)}, u32[]{:S(2)}) copy-start(u32[256]{0:T(256)} %constant.99) | copy-start | bytes 3076
  39.9 114.3 %copy-start.6 = (f32[512]{0:T(512)S(1)}, f32[512]{0:T(512)}, u32[]{:S(2)}) copy-start(f32[512]{0:T(512)} %param.16) | copy-start | bytes 6148
  39.9 114.4 %copy-start.7 = (f32[512]{0:T(512)S(1)}, f32[512]{0:T(512)}, u32[]{:S(2)}) copy-start(f32[512]{0:T(512)} %param.17) | copy-start | bytes 6148
  39.9 114.4 %copy-start.8 = (f32[512]{0:T(512)S(1)}, f32[512]{0:T(512)}, u32[]{:S(2)}) copy-start(f32[512]{0:T(512)} %param.18) | copy-start | bytes 6148
  40.6 13.4 %all-to-all-start.1 = ((bf16[8,32,512]{2,1,0:T(8,128)(2,1)}), bf16[8,32,512]{2,1,0:T(8,128)(2,1)S(1)}, u32[]{:S(2)}, u32[]{:S(2)}) async-start(bf16[8,32,512]{2,1,0:T(8,128)(2,1)} %bitcast.4), calls=%async_computation.1 | async-start | bytes 524288 | tf_op jit(solution)/shard_map/all_to_all | solution.py:122
  47.5 107.3 %all-gather.2.cloned.1.call-start = ((), (), s32[]{:S(2)}) async-start(), calls=%async_computation.3 | async-start | bytes 8650752 | tf_op jit(solution)/shard_map/all_gather | solution.py:128
  55.1 46.3 %collective-permute-start.2 = (bf16[512,2048]{1,0:T(8,128)(2,1)S(1)}, bf16[512,2048]{1,0:T(8,128)(2,1)}, u32[]{:S(2)}, u32[]{:S(2)}) collective-permute-start(bf16[512,2048]{1,0:T(8,128)(2,1)S(1)} %copy-done.1), channel_id=1, source_target_pairs={{0,6},{1,7},{2,0},{3,1},{4,2},{5,3},{6,4},{7,5},{8,14},{9,15},{10,... | collective-permute-start | bytes 6291464 | tf_op jit(solution)/shard_map/ppermute | solution.py:110
  56.1 48.8 %collective-permute-start.1 = (bf16[512,2048]{1,0:T(8,128)(2,1)S(1)}, bf16[512,2048]{1,0:T(8,128)(2,1)}, u32[]{:S(2)}, u32[]{:S(2)}) collective-permute-start(bf16[512,2048]{1,0:T(8,128)(2,1)S(1)} %copy-done.1), channel_id=1, source_target_pairs={{0,4},{1,5},{2,6},{3,7},{4,0},{5,1},{6,2},{7,3},{8,12},{9,13},{10,... | collective-permute-start | bytes 6291464 | tf_op jit(solution)/shard_map/ppermute | solution.py:110
  57.3 92.9 %collective-permute-start = (bf16[512,2048]{1,0:T(8,128)(2,1)S(1)}, bf16[512,2048]{1,0:T(8,128)(2,1)}, u32[]{:S(2)}, u32[]{:S(2)}) collective-permute-start(bf16[512,2048]{1,0:T(8,128)(2,1)S(1)} %copy-done.1), channel_id=1, source_target_pairs={{0,2},{1,3},{2,4},{3,5},{4,6},{5,7},{6,0},{7,1},{8,10},{9,11},{10,... | collective-permute-start | bytes 6291464 | tf_op jit(solution)/shard_map/ppermute | solution.py:110
  57.3 97.2 %collective-permute-start.3 = (bf16[512,2048]{1,0:T(8,128)(2,1)S(1)}, bf16[512,2048]{1,0:T(8,128)(2,1)}, u32[]{:S(2)}, u32[]{:S(2)}) collective-permute-start(bf16[512,2048]{1,0:T(8,128)(2,1)S(1)} %copy-done.1), channel_id=1, source_target_pairs={{0,1},{1,0},{2,3},{3,2},{4,5},{5,4},{6,7},{7,6},{8,9},{9,8},{10,11... | collective-permute-start | bytes 6291464 | tf_op jit(solution)/shard_map/ppermute | solution.py:113
  101.4 53.1 %collective-permute-start.6 = (bf16[512,2048]{1,0:T(8,128)(2,1)}, bf16[512,2048]{1,0:T(8,128)(2,1)}, u32[]{:S(2)}, u32[]{:S(2)}) collective-permute-start(bf16[512,2048]{1,0:T(8,128)(2,1)} %collective-permute-done.2.refs_5_), channel_id=1, source_target_pairs={{0,1},{1,0},{2,3},{3,2},{4,5},{5,4},{6,7},{7,6},{8,9},{9,8},{10,11... | collective-permute-start | bytes 6291464 | tf_op jit(solution)/shard_map/ppermute | solution.py:113
  104.8 49.7 %collective-permute-start.5 = (bf16[512,2048]{1,0:T(8,128)(2,1)}, bf16[512,2048]{1,0:T(8,128)(2,1)}, u32[]{:S(2)}, u32[]{:S(2)}) collective-permute-start(bf16[512,2048]{1,0:T(8,128)(2,1)} %collective-permute-done.1.refs_4_), channel_id=1, source_target_pairs={{0,1},{1,0},{2,3},{3,2},{4,5},{5,4},{6,7},{7,6},{8,9},{9,8},{10,11... | collective-permute-start | bytes 6291464 | tf_op jit(solution)/shard_map/ppermute | solution.py:113
  150.2 4.6 %collective-permute-start.4 = (bf16[512,2048]{1,0:T(8,128)(2,1)}, bf16[512,2048]{1,0:T(8,128)(2,1)}, u32[]{:S(2)}, u32[]{:S(2)}) collective-permute-start(bf16[512,2048]{1,0:T(8,128)(2,1)} %collective-permute-done.refs_3_), channel_id=1, source_target_pairs={{0,1},{1,0},{2,3},{3,2},{4,5},{5,4},{6,7},{7,6},{8,9},{9,8},{10,11... | collective-permute-start | bytes 6291464 | tf_op jit(solution)/shard_map/ppermute | solution.py:113
  154.8 1.6 copy-start.2
  182.0 30.0 %copy-start.9 = (f32[256]{0:T(256)S(1)}, f32[256]{0:T(256)}, u32[]{:S(2)}) copy-start(f32[256]{0:T(256)} %param.19) | copy-start | bytes 3076
  184.1 13.2 %all-to-all-start.2 = ((f32[3,32,32]{2,0,1:T(4,128)}), f32[3,32,32]{2,0,1:T(4,128)S(1)}, u32[]{:S(2)}, u32[]{:S(2)}) async-start(f32[3,32,32]{2,0,1:T(4,128)} %pad_maximum_fusion), calls=%async_computation.2 | async-start | bytes 131072 | tf_op jit(solution)/shard_map/all_to_all | solution.py:157
  211.9 1.2 copy-start.10
Sparse Core Ops, SparseCore 0:
  55.2 91.9 all-gather.1

commit v4 on v3

--- a/solution.py
+++ b/solution.py
@@ -100,10 +100,9 @@
     reward_send = jnp.dot(
         onehot, reward_hidden.reshape(req_dev * max_len, width_dev), preferred_element_type=jnp.float32
     ).astype(jnp.bfloat16)
-    send = jnp.concatenate([ref_send, reward_send], axis=1).reshape(shards, pair_len, 2 * width_dev)
-    got = lax.all_to_all(send, "dp", 0, 0, tiled=True).reshape(slot_dev, 2 * width_dev)
-    ref_packed = got[:, :width_dev]
-    reward_packed = got[:, width_dev:]
+    reward_packed = lax.all_to_all(
+        reward_send.reshape(shards, pair_len, width_dev), "dp", 0, 0, tiled=True
+    ).reshape(slot_dev, width_dev)
 
     chips = ways // 2
     own_core = [head_weight] + [
@@ -119,32 +118,26 @@
         (source_chip * 2 + source_core)[:, None] == jnp.arange(ways, dtype=jnp.int32)[None, :]
     ).astype(jnp.bfloat16)
 
-    parts_rows = lax.all_to_all(
-        ref_packed.reshape(ways, sub_len, width_dev), "mp", 0, 0, tiled=True
-    )
+    parts_rows = lax.all_to_all(ref_send.reshape(ways, sub_len, width_dev), "mp", 0, 0, tiled=True)
     own_rows = jnp.einsum(
         "msf,nm->snf", parts_rows, pick, preferred_element_type=jnp.float32
     ).astype(jnp.bfloat16).reshape(sub_len, width_full)
     block_rows = lax.all_gather(own_rows, "dp", axis=0, tiled=True)
 
-    first_src = part * blocks
-    dest4 = lax.dynamic_slice_in_dim(pack_dest, first_src * req_dev, blocks * req_dev).reshape(
-        blocks, req_dev
-    )
-    size4 = lax.dynamic_slice_in_dim(lengths, first_src * req_dev, blocks * req_dev).reshape(
-        blocks, req_dev
-    )
-    tok4 = lax.dynamic_slice_in_dim(token_ids, first_src * req_dev, blocks * req_dev, axis=0)
-    rank4 = pair_rank(dest4)
+    dest_all = pack_dest.reshape(shards, req_dev)
+    size_all = lengths.reshape(shards, req_dev)
+    rank_all = pair_rank(dest_all)
     key = (
-        dest4[:, :, None] * sub_len
-        + jnp.arange(blocks, dtype=jnp.int32)[:, None, None] * pair_len
+        dest_all[:, :, None] * pair_len
         + steps[None, None, :]
-        + rank4[:, :, None] * (pair_len - size4[:, :, None])
-    )
-    key = jnp.where(steps[None, None, :] < size4[:, :, None], key, -1).reshape(-1)
-    hits = key[None, :] == jnp.arange(shards * sub_len, dtype=jnp.int32)[:, None]
-    targets = jnp.sum(jnp.where(hits, tok4.reshape(-1)[None, :], 0), axis=1)
+        + rank_all[:, :, None] * (pair_len - size_all[:, :, None])
+        - part * sub_len
+    )
+    key = jnp.where(steps[None, None, :] < size_all[:, :, None], key, -1).reshape(shards, 1, -1)
+    hits = key == jnp.arange(sub_len, dtype=jnp.int32)[None, :, None]
+    targets = jnp.sum(
+        jnp.where(hits, token_ids.reshape(shards, 1, -1), 0), axis=2
+    ).reshape(-1)
 
     vocab_dev = head_weight.shape[1]
     tile_max, tile_total, tile_target = logit_stats(
@@ -153,13 +146,21 @@
     row_max = jnp.max(tile_max[:, :, 0], axis=0)
     exp_total = jnp.sum(tile_total[:, :, 0] * jnp.exp(tile_max[:, :, 0] - row_max[None, :]), axis=0)
     target_logit = jnp.sum(tile_target[:, :, 0], axis=0)
-    stats = jnp.stack([row_max, exp_total, target_logit]).reshape(3, shards, sub_len)
-    stats = lax.all_to_all(stats, "dp", 1, 1, tiled=True)
-    joint_max = jnp.max(stats[0], axis=0)
-    joint_total = jnp.sum(stats[1] * jnp.exp(stats[0] - joint_max[None, :]), axis=0)
-    joint_target = jnp.sum(stats[2], axis=0)
-    block_logprob = joint_target - joint_max - jnp.log(joint_total)
-    ref_logprob = lax.all_gather(block_logprob, "mp", axis=0, tiled=True)
+    stats = jnp.stack([row_max, exp_total, target_logit]).reshape(3, shards, blocks, pair_len)
+    to_shard = jnp.arange(shards, dtype=jnp.int32)[:, None] == (
+        part * blocks + jnp.arange(blocks, dtype=jnp.int32)
+    )[None, :]
+    routed = jnp.sum(
+        jnp.where(to_shard[:, None, None, :, None], stats[None], 0.0), axis=3
+    )
+    routed = lax.all_to_all(routed, "dp", 0, 0, tiled=True)
+    joint_max = jnp.max(routed[:, 0], axis=0)
+    joint_total = jnp.sum(routed[:, 1] * jnp.exp(routed[:, 0] - joint_max[None]), axis=0)
+    joint_target = jnp.sum(routed[:, 2], axis=0)
+    holder = me // blocks == part
+    block_logprob = jnp.where(
+        holder, joint_target - joint_max - jnp.log(joint_total), 0.0
+    ).reshape(-1)
 
     hidden_f = reward_packed.astype(jnp.float32)
     sums = jnp.stack(
@@ -169,7 +170,9 @@
             jnp.sum(hidden_f * (norm_gain * value_weight), axis=1),
         ]
     )
-    squares, score_dot, value_dot = lax.psum(sums, "mp")
+    ref_logprob, squares, score_dot, value_dot = lax.psum(
+        jnp.concatenate([block_logprob[None], sums]), "mp"
+    )
     inv_rms = lax.rsqrt(squares / width_full + norm_eps)
     score = score_dot * inv_rms
     value_est = value_dot * inv_rms

time: 220 us -> 205 us (0.932)
  starting transfers between devices: 21.6 us -> 78.7 us
  waiting for transfers between devices: 99.9 us -> 51.3 us
  blocking collectives: 42.5 us -> 13.6 us
  local copies, waits for them, and re-layouts: 8.23 us -> 10.8 us
    ppermute x3, waiting for transfers between devices: 84.4 us -> 31.3 us  [body(): lax.ppermute(head_weight, 'mp', [(i, (i + 2 * shift) % ways) for i in ran...]
    ppermute x4, starting transfers between devices: 8.2 us -> 48.4 us  [body(): lax.ppermute(block, 'mp', [(i, i ^ 1) for i in range(ways)])]
    all_to_all x1 -> x0, blocking collectives: 28.1 us -> none  [body(): lax.all_to_all(send, 'dp', 0, 0, tiled=True)]
    all_to_all x2 -> x3, starting transfers between devices: 11.3 us -> 27.4 us  [the longest x1 10.5 us: body(): routed = lax.all_to_all(routed, 'dp', 0, 0, tiled=True)]
    unnamed x1 -> x0, blocking collectives: 14.4 us -> none
    psum x0 -> x1, blocking collectives: none -> 13.6 us  [body(): lax.psum(jnp.concatenate([block_logprob[None], sums]), 'mp')]
    ppermute x4, waiting for transfers between devices: 0.27 us -> 5.15 us  [body(): lax.ppermute(block, 'mp', [(i, i ^ 1) for i in range(ways)])]
    unnamed x29 -> x34, local copies, waits for them, and re-layouts: 4.57 us -> 5.48 us
  transfers between devices with their start and end apart: 10 -> 11, of which waited for: 5 -> 5; matrix products, arithmetic and copies ran while one was open for 2% -> 5% of each run, Pallas kernels for 0% -> 13%
where the time goes in v4:
time: 205 us; the launch traced here: 204 us
  starting transfers between devices  78.7 us (38%)
  waiting for transfers between devices  51.3 us (25%)
  Pallas kernels  25.6 us (12%)
  between operations  14.5 us (7%)
  blocking collectives  13.6 us (7%)
  local copies, waits for them, and re-layouts  10.8 us (5%)
  other arithmetic  7.21 us (4%)
  matrix products  2.32 us (1%)
    ppermute x4, starting transfers between devices, body(): lax.ppermute(block, 'mp', [(i, i ^ 1) for i in range(ways)])  48.4 us
    ppermute x3, waiting for transfers between devices, body(): lax.ppermute(head_weight, 'mp', [(i, (i + 2 * shift) % ways) for i in ran...  31.3 us
    pallas_call x1, Pallas kernels, logit_stats(): pl.pallas_call(lambda *refs: stats_kernel(len(pieces), tile_n, *refs), gr...  25.6 us
    psum x1, blocking collectives, body(): lax.psum(jnp.concatenate([block_logprob[None], sums]), 'mp')  13.6 us
    all_to_all x1, starting transfers between devices, body(): routed = lax.all_to_all(routed, 'dp', 0, 0, tiled=True)  10.5 us
    all_to_all x1, starting transfers between devices, body(): lax.all_to_all(reward_send.reshape(shards, pair_len, width_dev), 'dp', 0,...  10.4 us
    all_to_all x1, waiting for transfers between devices, body(): routed = lax.all_to_all(routed, 'dp', 0, 0, tiled=True)  8.43 us
    all_to_all x1, starting transfers between devices, body(): lax.all_to_all(ref_send.reshape(ways, sub_len, width_dev), 'mp', 0, 0, ti...  6.51 us
  transfers between devices with their start and end apart: 11, of which 5 were waited for; matrix products, arithmetic and copies ran while one was open for 5% of the time, Pallas kernels for 13%

profile of v4, /device:TPU:1, one launch (start us, length us, event | category | flops | bytes accessed | tf_op | source)
XLA Modules:
  0.0 204.1 jit_solution(4050360445433909353)
XLA Ops:
  7.2 0.8 broadcast_multiply_fusion.1
  7.9 0.2 convert_reduce_fusion.1
  8.1 0.8 subtract_multiply_fusion.1
  9.0 0.1 add.194
  9.2 0.1 lt.129
  9.4 0.1 add.191
  9.7 1.4 copy.77
  11.1 0.2 reshape.293
  11.3 1.0 convolution_convert_fusion.2
  12.3 6.5 %all-to-all-start = ((bf16[8,32,512]{2,1,0:T(8,128)(2,1)}), bf16[8,32,512]{2,1,0:T(8,128)(2,1)S(1)}, u32[]{:S(2)}, u32[]{:S(2)}) async-start(bf16[8,32,512]{2,1,0:T(8,128)(2,1)} %bitcast.1), calls=%async_computation | async-start | bytes 524288 | tf_op jit(solution)/shard_map/all_to_all | solution.py:121
  18.9 6.5 %all-to-all-done = bf16[8,32,512]{2,1,0:T(8,128)(2,1)S(1)} async-done(((bf16[8,32,512]{2,1,0:T(8,128)(2,1)}), bf16[8,32,512]{2,1,0:T(8,128)(2,1)S(1)}, u32[]{:S(2)}, u32[]{:S(2)}) %all-to-all-start) | async-done | bytes 262176 | tf_op jit(solution)/shard_map/all_to_all | solution.py:121
  25.4 0.3 convolution_convert_fusion.1
  25.7 0.8 copy.87
  26.5 0.4 collective-permute-start
  26.9 1.8 collective-permute-start.1
  28.6 0.7 collective-permute-start.2
  29.4 1.6 collective-permute-start.3
  31.0 0.3 copy.85
  31.2 0.2 reshape.296
  31.4 1.0 fusion
  32.4 10.4 %all-to-all-start.2 = ((bf16[32,8,512]{2,1,0:T(8,128)(2,1)}), bf16[32,8,512]{2,1,0:T(8,128)(2,1)S(1)}, u32[]{:S(2)}, u32[]{:S(2)}) async-start(bf16[32,8,512]{2,1,0:T(8,128)(2,1)} %fusion), calls=%async_computation.2 | async-start | bytes 524288 | tf_op jit(solution)/shard_map/all_to_all | solution.py:103
  43.1 0.2 reduce_window_sum.11
  43.4 31.3 %collective-permute-done.refs_3_ = bf16[512,2048]{1,0:T(8,128)(2,1)} collective-permute-done((bf16[512,2048]{1,0:T(8,128)(2,1)S(1)}, bf16[512,2048]{1,0:T(8,128)(2,1)}, u32[]{:S(2)}, u32[]{:S(2)}) %collective-permute-start) | collective-permute-done | bytes 2097184 | tf_op jit(solution)/shard_map/ppermute | solution.py:109
  74.6 46.2 %collective-permute-start.4 = (bf16[512,2048]{1,0:T(8,128)(2,1)}, bf16[512,2048]{1,0:T(8,128)(2,1)}, u32[]{:S(2)}, u32[]{:S(2)}) collective-permute-start(bf16[512,2048]{1,0:T(8,128)(2,1)} %collective-permute-done.refs_3_), channel_id=1, source_target_pairs={{0,1},{1,0},{2,3},{3,2},{4,5},{5,4},{6,7},{7,6},{8,9},{9,8},{10,11... | collective-permute-start | bytes 6291464 | tf_op jit(solution)/shard_map/ppermute | solution.py:112
  120.9 0.6 collective-permute-start.6
  121.5 0.9 convert_reduce_fusion
  122.4 0.6 select_reduce_fusion.2
  123.7 0.4 copy.76
  124.1 0.5 broadcast_in_dim.105
  124.6 0.6 select_reduce_fusion
  125.2 0.5 sub.135.refs_0_
  125.9 2.1 %collective-permute-done.5.refs_8_ = bf16[512,2048]{1,0:T(8,128)(2,1)} collective-permute-done((bf16[512,2048]{1,0:T(8,128)(2,1)}, bf16[512,2048]{1,0:T(8,128)(2,1)}, u32[]{:S(2)}, u32[]{:S(2)}) %collective-permute-start.5) | collective-permute-done | bytes 2097184 | tf_op jit(solution)/shard_map/ppermute | solution.py:112
  128.0 3.0 %collective-permute-done.6.refs_9_ = bf16[512,2048]{1,0:T(8,128)(2,1)} collective-permute-done((bf16[512,2048]{1,0:T(8,128)(2,1)}, bf16[512,2048]{1,0:T(8,128)(2,1)}, u32[]{:S(2)}, u32[]{:S(2)}) %collective-permute-start.6) | collective-permute-done | bytes 2097184 | tf_op jit(solution)/shard_map/ppermute | solution.py:112
  131.0 1.6 copy-done.1
  132.6 25.6 %shard_map.113 = (f32[2,1024,1]{2,1,0:T(8,128)S(1)}, f32[2,1024,1]{2,1,0:T(8,128)S(1)}, f32[2,1024,1]{2,1,0:T(8,128)S(1)}) custom-call(s32[1024,1]{1,0:T(8,128)S(1)} %sub.135.refs_0_, bf16[1024,4096]{1,0:T(8,128)(2,1)} %all-gather.2.cloned.1.call-done.refs_1_, bf16[512,2048]{1,0:T(8,128)(2,1)S(1)} %copy-done.1, ...), custom_call_target="tpu_custom_call" | custom-call | flops 17179869184 | bytes 33554432 | tf_op jit(solution)/shard_map/pallas_call | solution.py:48
  158.2 0.5 fusion.23
  158.8 0.3 reduce.7
  159.5 0.2 reduce_sum.112
  160.0 0.3 select_reduce_fusion.1
  160.2 0.8 reshape.303
  161.1 10.5 %all-to-all-start.1 = ((f32[32,1,768]{2,1,0:T(1,128)}), f32[32,1,768]{2,1,0:T(1,128)S(1)}, u32[]{:S(2)}, u32[]{:S(2)}) async-start(f32[32,1,768]{2,1,0:T(1,128)} %reshape.303), calls=%async_computation.1 | async-start | bytes 196608 | tf_op jit(solution)/shard_map/all_to_all | solution.py:156
  171.7 0.2 fusion.1
  172.2 8.4 %all-to-all-done.1 = f32[32,1,768]{2,1,0:T(1,128)S(1)} async-done(((f32[32,1,768]{2,1,0:T(1,128)}), f32[32,1,768]{2,1,0:T(1,128)S(1)}, u32[]{:S(2)}, u32[]{:S(2)}) %all-to-all-start.1) | async-done | bytes 98336 | tf_op jit(solution)/shard_map/all_to_all | solution.py:156
  180.6 0.5 broadcast.306
  181.1 0.9 reduce.10
  182.0 0.1 reshape.304
  182.5 13.6 %psum.7 = f32[4,256]{1,0:T(4,128)S(1)} all-reduce(f32[4,256]{1,0:T(4,128)S(1)} %pad_maximum_fusion), channel_id=1, replica_groups=mesh['dp'=32,'mp'=8] {'mp'}, use_global_device_ids=true, to_apply=%region_13.14 | all-reduce | flops 1024 | bytes 8192 | tf_op jit(solution)/shard_map/psum | solution.py:173
  196.6 0.7 reshape.299
  (91 shorter events, 3.1 us)
Async XLA Ops:
  9.7 16.8 %copy-start = (bf16[512,2048]{1,0:T(8,128)(2,1)S(1)}, bf16[512,2048]{1,0:T(8,128)(2,1)}, u32[]{:S(2)}) copy-start(bf16[512,2048]{1,0:T(8,128)(2,1)} %refs_2_.1) | copy-start | bytes 6291460
  9.7 21.3 %copy-start.2 = (bf16[64,7,512]{2,0,1:T(8,128)(2,1)S(1)}, bf16[64,7,512]{2,0,1:T(8,128)(2,1)}, u32[]{:S(2)}) copy-start(bf16[64,7,512]{2,0,1:T(8,128)(2,1)} %param.14) | copy-start | bytes 1376260
  11.3 1.0 copy-start.10
  12.3 13.0 %all-to-all-start = ((bf16[8,32,512]{2,1,0:T(8,128)(2,1)}), bf16[8,32,512]{2,1,0:T(8,128)(2,1)S(1)}, u32[]{:S(2)}, u32[]{:S(2)}) async-start(bf16[8,32,512]{2,1,0:T(8,128)(2,1)} %bitcast.1), calls=%async_computation | async-start | bytes 524288 | tf_op jit(solution)/shard_map/all_to_all | solution.py:121
  18.9 12.5 %copy-start.11 = (s32[448]{0:T(512)S(1)}, s32[448]{0:T(512)}, u32[]{:S(2)}) copy-start(s32[448]{0:T(512)} %copy-done.10) | copy-start | bytes 5380
  18.9 112.1 %all-gather.2.cloned.1.call-start = ((), (), s32[]{:S(2)}) async-start(), calls=%async_computation.3 | async-start | bytes 8650752 | tf_op jit(solution)/shard_map/all_gather | solution.py:125
  25.7 17.2 %copy-start.4 = (s32[2048]{0:T(1024)S(1)}, s32[2048]{0:T(1024)}, u32[]{:S(2)}) copy-start(s32[2048]{0:T(1024)} %param.12) | copy-start | bytes 24580
  25.7 17.3 %copy-start.5 = (s32[2048]{0:T(1024)S(1)}, s32[2048]{0:T(1024)}, u32[]{:S(2)}) copy-start(s32[2048]{0:T(1024)} %param.11) | copy-start | bytes 24580
  26.5 48.1 %collective-permute-start = (bf16[512,2048]{1,0:T(8,128)(2,1)S(1)}, bf16[512,2048]{1,0:T(8,128)(2,1)}, u32[]{:S(2)}, u32[]{:S(2)}) collective-permute-start(bf16[512,2048]{1,0:T(8,128)(2,1)S(1)} %copy-done), channel_id=1, source_target_pairs={{0,2},{1,3},{2,4},{3,5},{4,6},{5,7},{6,0},{7,1},{8,10},{9,11},{10,... | collective-permute-start | bytes 6291464 | tf_op jit(solution)/shard_map/ppermute | solution.py:109
  26.9 94.0 %collective-permute-start.1 = (bf16[512,2048]{1,0:T(8,128)(2,1)S(1)}, bf16[512,2048]{1,0:T(8,128)(2,1)}, u32[]{:S(2)}, u32[]{:S(2)}) collective-permute-start(bf16[512,2048]{1,0:T(8,128)(2,1)S(1)} %copy-done), channel_id=1, source_target_pairs={{0,4},{1,5},{2,6},{3,7},{4,0},{5,1},{6,2},{7,3},{8,12},{9,13},{10,... | collective-permute-start | bytes 6291464 | tf_op jit(solution)/shard_map/ppermute | solution.py:109
  28.6 92.3 %collective-permute-start.2 = (bf16[512,2048]{1,0:T(8,128)(2,1)S(1)}, bf16[512,2048]{1,0:T(8,128)(2,1)}, u32[]{:S(2)}, u32[]{:S(2)}) collective-permute-start(bf16[512,2048]{1,0:T(8,128)(2,1)S(1)} %copy-done), channel_id=1, source_target_pairs={{0,6},{1,7},{2,0},{3,1},{4,2},{5,3},{6,4},{7,5},{8,14},{9,15},{10,... | collective-permute-start | bytes 6291464 | tf_op jit(solution)/shard_map/ppermute | solution.py:109
  29.4 96.5 %collective-permute-start.3 = (bf16[512,2048]{1,0:T(8,128)(2,1)S(1)}, bf16[512,2048]{1,0:T(8,128)(2,1)}, u32[]{:S(2)}, u32[]{:S(2)}) collective-permute-start(bf16[512,2048]{1,0:T(8,128)(2,1)S(1)} %copy-done), channel_id=1, source_target_pairs={{0,1},{1,0},{2,3},{3,2},{4,5},{5,4},{6,7},{7,6},{8,9},{9,8},{10,11... | collective-permute-start | bytes 6291464 | tf_op jit(solution)/shard_map/ppermute | solution.py:112
  32.4 128.6 %all-to-all-start.2 = ((bf16[32,8,512]{2,1,0:T(8,128)(2,1)}), bf16[32,8,512]{2,1,0:T(8,128)(2,1)S(1)}, u32[]{:S(2)}, u32[]{:S(2)}) async-start(bf16[32,8,512]{2,1,0:T(8,128)(2,1)} %fusion), calls=%async_computation.2 | async-start | bytes 524288 | tf_op jit(solution)/shard_map/all_to_all | solution.py:103
  42.9 80.8 %copy-start.3 = (s32[2048,7]{0,1:T(8,128)S(1)}, s32[2048,7]{0,1:T(8,128)}, u32[]{:S(2)}) copy-start(s32[2048,7]{0,1:T(8,128)} %param.10) | copy-start | bytes 172036
  74.6 51.2 %collective-permute-start.4 = (bf16[512,2048]{1,0:T(8,128)(2,1)}, bf16[512,2048]{1,0:T(8,128)(2,1)}, u32[]{:S(2)}, u32[]{:S(2)}) collective-permute-start(bf16[512,2048]{1,0:T(8,128)(2,1)} %collective-permute-done.refs_3_), channel_id=1, source_target_pairs={{0,1},{1,0},{2,3},{3,2},{4,5},{5,4},{6,7},{7,6},{8,9},{9,8},{10,11... | collective-permute-start | bytes 6291464 | tf_op jit(solution)/shard_map/ppermute | solution.py:112
  120.9 7.1 %collective-permute-start.5 = (bf16[512,2048]{1,0:T(8,128)(2,1)}, bf16[512,2048]{1,0:T(8,128)(2,1)}, u32[]{:S(2)}, u32[]{:S(2)}) collective-permute-start(bf16[512,2048]{1,0:T(8,128)(2,1)} %collective-permute-done.1.refs_4_), channel_id=1, source_target_pairs={{0,1},{1,0},{2,3},{3,2},{4,5},{5,4},{6,7},{7,6},{8,9},{9,8},{10,11... | collective-permute-start | bytes 6291464 | tf_op jit(solution)/shard_map/ppermute | solution.py:112
  120.9 10.1 %collective-permute-start.6 = (bf16[512,2048]{1,0:T(8,128)(2,1)}, bf16[512,2048]{1,0:T(8,128)(2,1)}, u32[]{:S(2)}, u32[]{:S(2)}) collective-permute-start(bf16[512,2048]{1,0:T(8,128)(2,1)} %collective-permute-done.2.refs_5_), channel_id=1, source_target_pairs={{0,1},{1,0},{2,3},{3,2},{4,5},{5,4},{6,7},{7,6},{8,9},{9,8},{10,11... | collective-permute-start | bytes 6291464 | tf_op jit(solution)/shard_map/ppermute | solution.py:112
  123.4 2.4 %copy-start.7 = (f32[512]{0:T(512)S(1)}, f32[512]{0:T(512)}, u32[]{:S(2)}) copy-start(f32[512]{0:T(512)} %param.16) | copy-start | bytes 6148
  123.4 2.4 %copy-start.8 = (f32[512]{0:T(512)S(1)}, f32[512]{0:T(512)}, u32[]{:S(2)}) copy-start(f32[512]{0:T(512)} %param.18) | copy-start | bytes 6148
  123.4 2.4 %copy-start.9 = (f32[512]{0:T(512)S(1)}, f32[512]{0:T(512)}, u32[]{:S(2)}) copy-start(f32[512]{0:T(512)} %param.17) | copy-start | bytes 6148
  123.6 2.2 %copy-start.13 = (s32[32]{0:T(128)S(1)}, s32[32]{0:T(128)}, u32[]{:S(2)}) copy-start(s32[32]{0:T(128)} %get-tuple-element.25) | copy-start | bytes 388
  131.0 1.6 copy-start.1
  159.5 36.7 %copy-start.12 = (f32[256]{0:T(256)S(1)}, f32[256]{0:T(256)}, u32[]{:S(2)}) copy-start(f32[256]{0:T(256)} %param.19) | copy-start | bytes 3076
  161.1 19.6 %all-to-all-start.1 = ((f32[32,1,768]{2,1,0:T(1,128)}), f32[32,1,768]{2,1,0:T(1,128)S(1)}, u32[]{:S(2)}, u32[]{:S(2)}) async-start(f32[32,1,768]{2,1,0:T(1,128)} %reshape.303), calls=%async_computation.1 | async-start | bytes 196608 | tf_op jit(solution)/shard_map/all_to_all | solution.py:156
  196.1 1.2 copy-start.6
Sparse Core Ops, SparseCore 0:
  26.6 99.3 all-gather.1

commit v5 on v4

--- a/solution.py
+++ b/solution.py
@@ -122,7 +122,12 @@
     own_rows = jnp.einsum(
         "msf,nm->snf", parts_rows, pick, preferred_element_type=jnp.float32
     ).astype(jnp.bfloat16).reshape(sub_len, width_full)
-    block_rows = lax.all_gather(own_rows, "dp", axis=0, tiled=True)
+    halves = 2
+    half_len = sub_len // halves
+    half_rows = [
+        lax.all_gather(own_rows[h * half_len : (h + 1) * half_len], "dp", axis=0, tiled=True)
+        for h in range(halves)
+    ]
 
     dest_all = pack_dest.reshape(shards, req_dev)
     size_all = lengths.reshape(shards, req_dev)
@@ -140,12 +145,18 @@
     ).reshape(-1)
 
     vocab_dev = head_weight.shape[1]
-    tile_max, tile_total, tile_target = logit_stats(
-        block_rows, own_core + mate_core, targets - me * vocab_dev
-    )
-    row_max = jnp.max(tile_max[:, :, 0], axis=0)
-    exp_total = jnp.sum(tile_total[:, :, 0] * jnp.exp(tile_max[:, :, 0] - row_max[None, :]), axis=0)
-    target_logit = jnp.sum(tile_target[:, :, 0], axis=0)
+    local_target = (targets - me * vocab_dev).reshape(shards, halves, half_len)
+    parts_stats = []
+    for h in range(halves):
+        tile_max, tile_total, tile_target = logit_stats(
+            half_rows[h], own_core + mate_core, local_target[:, h].reshape(-1)
+        )
+        half_max = jnp.max(tile_max[:, :, 0], axis=0)
+        half_total = jnp.sum(tile_total[:, :, 0] * jnp.exp(tile_max[:, :, 0] - half_max[None, :]), axis=0)
+        half_target = jnp.sum(tile_target[:, :, 0], axis=0)
+        parts_stats.append(jnp.stack([half_max, half_total, half_target]).reshape(3, shards, half_len))
+    joint_stats = jnp.concatenate(parts_stats, axis=2)
+    row_max, exp_total, target_logit = joint_stats[0], joint_stats[1], joint_stats[2]
     stats = jnp.stack([row_max, exp_total, target_logit]).reshape(3, shards, blocks, pair_len)
     to_shard = jnp.arange(shards, dtype=jnp.int32)[:, None] == (
         part * blocks + jnp.arange(blocks, dtype=jnp.int32)

time: 205 us -> 249 us (1.21)
  waiting for transfers between devices: 51.3 us -> 89.7 us
  Pallas kernels: 25.6 us -> 30.4 us
  starting transfers between devices: 78.7 us -> 74.4 us
  blocking collectives: 13.6 us -> 16.5 us
    all_gather x1 -> x2, waiting for transfers between devices: 0.01 us -> 38.9 us  [body(): lax.all_gather(own_rows[h * half_len:(h + 1) * half_len], 'dp', axis=0, t...]
    pallas_call x1 -> x2, Pallas kernels: 25.6 us -> 30.4 us  [logit_stats(): pl.pallas_call(lambda *refs: stats_kernel(len(pieces), tile_n, *refs), gr...]
    all_to_all x1, starting transfers between devices: 10.5 us -> 5.99 us  [body(): routed = lax.all_to_all(routed, 'dp', 0, 0, tiled=True)]
    psum x1, blocking collectives: 13.6 us -> 16.5 us  [body(): lax.psum(jnp.concatenate([block_logprob[None], sums]), 'mp')]
    unnamed x34 -> x35, local copies, waits for them, and re-layouts: 5.48 us -> 7.5 us
  transfers between devices with their start and end apart: 11 -> 12, of which waited for: 5 -> 7; matrix products, arithmetic and copies ran while one was open for 5% -> 4% of each run, Pallas kernels for 13% -> 12%
where the time goes in v5:
time: 249 us
  waiting for transfers between devices  89.7 us (36%)
  starting transfers between devices  74.4 us (30%)
  Pallas kernels  30.4 us (12%)
  blocking collectives  16.5 us (7%)
  between operations  14.5 us (6%)
  local copies, waits for them, and re-layouts  12.8 us (5%)
  other arithmetic  7.96 us (3%)
    ppermute x4, starting transfers between devices, body(): lax.ppermute(block, 'mp', [(i, i ^ 1) for i in range(ways)])  48.4 us
    all_gather x2, waiting for transfers between devices, body(): lax.all_gather(own_rows[h * half_len:(h + 1) * half_len], 'dp', axis=0, t...  38.9 us
    pallas_call x2, Pallas kernels, logit_stats(): pl.pallas_call(lambda *refs: stats_kernel(len(pieces), tile_n, *refs), gr...  30.4 us
    ppermute x3, waiting for transfers between devices, body(): lax.ppermute(head_weight, 'mp', [(i, (i + 2 * shift) % ways) for i in ran...  30.3 us
    psum x1, blocking collectives, body(): lax.psum(jnp.concatenate([block_logprob[None], sums]), 'mp')  16.5 us
    all_to_all x1, starting transfers between devices, body(): lax.all_to_all(reward_send.reshape(shards, pair_len, width_dev), 'dp', 0,...  10.6 us
    unnamed x35, local copies, waits for them, and re-layouts  7.5 us
    all_to_all x1, waiting for transfers between devices, body(): routed = lax.all_to_all(routed, 'dp', 0, 0, tiled=True)  7.48 us
  transfers between devices with their start and end apart: 12, of which 7 were waited for; matrix products, arithmetic and copies ran while one was open for 4% of the time, Pallas kernels for 12%

profile of v5, /device:TPU:1, one launch (start us, length us, event | category | flops | bytes accessed | tf_op | source)
XLA Modules:
  0.0 248.7 jit_solution(12800347119069064762)
XLA Ops:
  7.2 0.8 broadcast_multiply_fusion.1
  7.9 0.2 convert_reduce_fusion.1
  8.1 0.8 subtract_multiply_fusion.1
  9.7 1.3 copy.86
  11.0 0.2 reshape.294
  11.2 1.0 convolution_convert_fusion.2
  12.2 6.5 %all-to-all-start = ((bf16[8,32,512]{2,1,0:T(8,128)(2,1)}), bf16[8,32,512]{2,1,0:T(8,128)(2,1)S(1)}, u32[]{:S(2)}, u32[]{:S(2)}) async-start(bf16[8,32,512]{2,1,0:T(8,128)(2,1)} %bitcast.2), calls=%async_computation | async-start | bytes 524288 | tf_op jit(solution)/shard_map/all_to_all | solution.py:121
  18.7 6.5 %all-to-all-done = bf16[8,32,512]{2,1,0:T(8,128)(2,1)S(1)} async-done(((bf16[8,32,512]{2,1,0:T(8,128)(2,1)}), bf16[8,32,512]{2,1,0:T(8,128)(2,1)S(1)}, u32[]{:S(2)}, u32[]{:S(2)}) %all-to-all-start) | async-done | bytes 262176 | tf_op jit(solution)/shard_map/all_to_all | solution.py:121
  25.2 0.3 fusion.1
  25.6 0.7 copy.97
  26.3 0.7 copy.96
  27.0 0.4 collective-permute-start
  27.4 1.8 collective-permute-start.1
  29.2 0.7 collective-permute-start.2
  29.9 1.6 collective-permute-start.3
  31.5 0.3 copy.94
  32.0 1.0 fusion
  33.0 10.6 %all-to-all-start.2 = ((bf16[32,8,512]{2,1,0:T(8,128)(2,1)}), bf16[32,8,512]{2,1,0:T(8,128)(2,1)}, u32[]{:S(2)}, u32[]{:S(2)}) async-start(bf16[32,8,512]{2,1,0:T(8,128)(2,1)} %fusion), calls=%async_computation.2 | async-start | bytes 524288 | tf_op jit(solution)/shard_map/all_to_all | solution.py:103
  43.7 0.2 reduce_window_sum.11
  44.0 0.9 convert_reduce_fusion
  44.9 30.3 %collective-permute-done.refs_3_ = bf16[512,2048]{1,0:T(8,128)(2,1)} collective-permute-done((bf16[512,2048]{1,0:T(8,128)(2,1)S(1)}, bf16[512,2048]{1,0:T(8,128)(2,1)}, u32[]{:S(2)}, u32[]{:S(2)}) %collective-permute-start) | collective-permute-done | bytes 2097184 | tf_op jit(solution)/shard_map/ppermute | solution.py:109
  75.2 46.2 %collective-permute-start.4 = (bf16[512,2048]{1,0:T(8,128)(2,1)}, bf16[512,2048]{1,0:T(8,128)(2,1)}, u32[]{:S(2)}, u32[]{:S(2)}) collective-permute-start(bf16[512,2048]{1,0:T(8,128)(2,1)} %collective-permute-done.refs_3_), channel_id=1, source_target_pairs={{0,1},{1,0},{2,3},{3,2},{4,5},{5,4},{6,7},{7,6},{8,9},{9,8},{10,11... | collective-permute-start | bytes 6291464 | tf_op jit(solution)/shard_map/ppermute | solution.py:112
  121.4 0.6 collective-permute-start.6
  122.3 0.4 copy.83
  122.6 0.5 broadcast_in_dim.106
  123.7 0.6 select_reduce_fusion
  124.5 0.2 reshape_reshape_squeeze.9.refs_0_
  124.8 0.2 reshape_reshape_squeeze.8.refs_0_
  125.1 0.5 collective-permute-done.4.refs_7_
  125.6 3.0 %collective-permute-done.5.refs_8_ = bf16[512,2048]{1,0:T(8,128)(2,1)} collective-permute-done((bf16[512,2048]{1,0:T(8,128)(2,1)}, bf16[512,2048]{1,0:T(8,128)(2,1)}, u32[]{:S(2)}, u32[]{:S(2)}) %collective-permute-start.5) | collective-permute-done | bytes 2097184 | tf_op jit(solution)/shard_map/ppermute | solution.py:112
  128.6 3.0 %collective-permute-done.6.refs_9_ = bf16[512,2048]{1,0:T(8,128)(2,1)} collective-permute-done((bf16[512,2048]{1,0:T(8,128)(2,1)}, bf16[512,2048]{1,0:T(8,128)(2,1)}, u32[]{:S(2)}, u32[]{:S(2)}) %collective-permute-start.6) | collective-permute-done | bytes 2097184 | tf_op jit(solution)/shard_map/ppermute | solution.py:112
  131.6 1.6 copy-done.1
  133.2 15.2 %shard_map.114 = (f32[2,512,1]{2,1,0:T(8,128)S(1)}, f32[2,512,1]{2,1,0:T(8,128)S(1)}, f32[2,512,1]{2,1,0:T(8,128)S(1)}) custom-call(s32[512,1]{1,0:T(8,128)S(1)} %reshape_reshape_squeeze.9.refs_0_, bf16[512,4096]{1,0:T(8,128)(2,1)} %all-gather.5.cloned.1.call-done.refs_1_, bf16[512,2048]{1,0:T(8,128)(2,1)S(1)} %copy-done.1, ...), custom_call_target="tpu_custom_call" | custom-call | flops 8589934592 | bytes 25165824 | tf_op jit(solution)/shard_map/pallas_call | solution.py:48
  148.4 38.9 %all-gather.3.cloned.1.call-done.refs_1_ = bf16[512,4096]{1,0:T(8,128)(2,1)} async-done(((bf16[16,4096]{1,0:T(8,128)(2,1)}), bf16[512,4096]{1,0:T(8,128)(2,1)}) %all-gather.3.cloned.1.call-update) | async-done | bytes 4194320 | tf_op jit(solution)/shard_map/all_gather | solution.py:128
  187.4 1.6 copy-done.2
  188.9 15.2 %shard_map.113 = (f32[2,512,1]{2,1,0:T(8,128)S(1)}, f32[2,512,1]{2,1,0:T(8,128)S(1)}, f32[2,512,1]{2,1,0:T(8,128)S(1)}) custom-call(s32[512,1]{1,0:T(8,128)S(1)} %reshape_reshape_squeeze.8.refs_0_, bf16[512,4096]{1,0:T(8,128)(2,1)} %all-gather.3.cloned.1.call-done.refs_1_, bf16[512,2048]{1,0:T(8,128)(2,1)S(1)} %copy-done.2, ...), custom_call_target="tpu_custom_call" | custom-call | flops 8589934592 | bytes 25165824 | tf_op jit(solution)/shard_map/pallas_call | solution.py:48
  204.1 0.5 fusion.24
  204.9 0.2 reduce.11
  205.5 0.2 reduce.9
  206.1 0.3 select_reduce_fusion.1
  206.4 0.8 reshape.305
  207.2 6.0 %all-to-all-start.1 = ((f32[32,1,768]{2,1,0:T(1,128)}), f32[32,1,768]{2,1,0:T(1,128)S(1)}, u32[]{:S(2)}, u32[]{:S(2)}) async-start(f32[32,1,768]{2,1,0:T(1,128)} %reshape.305), calls=%async_computation.1 | async-start | bytes 196608 | tf_op jit(solution)/shard_map/all_to_all | solution.py:167
  213.4 1.2 fusion.2
  214.8 7.5 %all-to-all-done.1 = f32[32,1,768]{2,1,0:T(1,128)S(1)} async-done(((f32[32,1,768]{2,1,0:T(1,128)}), f32[32,1,768]{2,1,0:T(1,128)S(1)}, u32[]{:S(2)}, u32[]{:S(2)}) %all-to-all-start.1) | async-done | bytes 98336 | tf_op jit(solution)/shard_map/all_to_all | solution.py:167
  222.3 0.5 broadcast.303
  222.8 0.9 reduce.15
  224.2 16.5 %psum.7 = f32[4,256]{1,0:T(4,128)S(1)} all-reduce(f32[4,256]{1,0:T(4,128)S(1)} %pad_maximum_fusion), channel_id=1, replica_groups=mesh['dp'=32,'mp'=8] {'mp'}, use_global_device_ids=true, to_apply=%region_16.17 | all-reduce | flops 1024 | bytes 8192 | tf_op jit(solution)/shard_map/psum | solution.py:184
  241.2 0.7 reshape.299
  (106 shorter events, 4.7 us)
Async XLA Ops:
  11.0 16.1 %copy-start = (bf16[512,2048]{1,0:T(8,128)(2,1)S(1)}, bf16[512,2048]{1,0:T(8,128)(2,1)}, u32[]{:S(2)}) copy-start(bf16[512,2048]{1,0:T(8,128)(2,1)} %refs_2_.3) | copy-start | bytes 6291460
  11.0 20.5 %copy-start.3 = (bf16[64,7,512]{2,0,1:T(8,128)(2,1)S(1)}, bf16[64,7,512]{2,0,1:T(8,128)(2,1)}, u32[]{:S(2)}) copy-start(bf16[64,7,512]{2,0,1:T(8,128)(2,1)} %param.14) | copy-start | bytes 1376260
  11.2 1.0 copy-start.11
  12.2 13.0 %all-to-all-start = ((bf16[8,32,512]{2,1,0:T(8,128)(2,1)}), bf16[8,32,512]{2,1,0:T(8,128)(2,1)S(1)}, u32[]{:S(2)}, u32[]{:S(2)}) async-start(bf16[8,32,512]{2,1,0:T(8,128)(2,1)} %bitcast.2), calls=%async_computation | async-start | bytes 524288 | tf_op jit(solution)/shard_map/all_to_all | solution.py:121
  18.7 13.2 %copy-start.12 = (s32[448]{0:T(512)S(1)}, s32[448]{0:T(512)}, u32[]{:S(2)}) copy-start(s32[448]{0:T(512)} %copy-done.11) | copy-start | bytes 5380
  18.7 112.8 %all-gather.5.cloned.1.call-start = ((), (), s32[]{:S(2)}) async-start(), calls=%async_computation.4 | async-start | bytes 4325376 | tf_op jit(solution)/shard_map/all_gather | solution.py:128
  25.5 18.0 %copy-start.5 = (s32[2048]{0:T(1024)S(1)}, s32[2048]{0:T(1024)}, u32[]{:S(2)}) copy-start(s32[2048]{0:T(1024)} %param.11) | copy-start | bytes 24580
  25.5 18.1 %copy-start.6 = (s32[2048]{0:T(1024)S(1)}, s32[2048]{0:T(1024)}, u32[]{:S(2)}) copy-start(s32[2048]{0:T(1024)} %param.12) | copy-start | bytes 24580
  26.2 96.0 %copy-start.4 = (s32[2048,7]{0,1:T(8,128)S(1)}, s32[2048,7]{0,1:T(8,128)}, u32[]{:S(2)}) copy-start(s32[2048,7]{0,1:T(8,128)} %param.10) | copy-start | bytes 172036
  26.3 161.1 %all-gather.3.cloned.1.call-start = ((), (), s32[]{:S(2)}) async-start(), calls=%async_computation.3 | async-start | bytes 4325376 | tf_op jit(solution)/shard_map/all_gather | solution.py:128
  27.0 48.1 %collective-permute-start = (bf16[512,2048]{1,0:T(8,128)(2,1)S(1)}, bf16[512,2048]{1,0:T(8,128)(2,1)}, u32[]{:S(2)}, u32[]{:S(2)}) collective-permute-start(bf16[512,2048]{1,0:T(8,128)(2,1)S(1)} %copy-done), channel_id=1, source_target_pairs={{0,2},{1,3},{2,4},{3,5},{4,6},{5,7},{6,0},{7,1},{8,10},{9,11},{10,... | collective-permute-start | bytes 6291464 | tf_op jit(solution)/shard_map/ppermute | solution.py:109
  27.4 94.0 %collective-permute-start.1 = (bf16[512,2048]{1,0:T(8,128)(2,1)S(1)}, bf16[512,2048]{1,0:T(8,128)(2,1)}, u32[]{:S(2)}, u32[]{:S(2)}) collective-permute-start(bf16[512,2048]{1,0:T(8,128)(2,1)S(1)} %copy-done), channel_id=1, source_target_pairs={{0,4},{1,5},{2,6},{3,7},{4,0},{5,1},{6,2},{7,3},{8,12},{9,13},{10,... | collective-permute-start | bytes 6291464 | tf_op jit(solution)/shard_map/ppermute | solution.py:109
  29.2 92.3 %collective-permute-start.2 = (bf16[512,2048]{1,0:T(8,128)(2,1)S(1)}, bf16[512,2048]{1,0:T(8,128)(2,1)}, u32[]{:S(2)}, u32[]{:S(2)}) collective-permute-start(bf16[512,2048]{1,0:T(8,128)(2,1)S(1)} %copy-done), channel_id=1, source_target_pairs={{0,6},{1,7},{2,0},{3,1},{4,2},{5,3},{6,4},{7,5},{8,14},{9,15},{10,... | collective-permute-start | bytes 6291464 | tf_op jit(solution)/shard_map/ppermute | solution.py:109
  29.9 95.1 %collective-permute-start.3 = (bf16[512,2048]{1,0:T(8,128)(2,1)S(1)}, bf16[512,2048]{1,0:T(8,128)(2,1)}, u32[]{:S(2)}, u32[]{:S(2)}) collective-permute-start(bf16[512,2048]{1,0:T(8,128)(2,1)S(1)} %copy-done), channel_id=1, source_target_pairs={{0,1},{1,0},{2,3},{3,2},{4,5},{5,4},{6,7},{7,6},{8,9},{9,8},{10,11... | collective-permute-start | bytes 6291464 | tf_op jit(solution)/shard_map/ppermute | solution.py:112
  33.0 174.2 %all-to-all-start.2 = ((bf16[32,8,512]{2,1,0:T(8,128)(2,1)}), bf16[32,8,512]{2,1,0:T(8,128)(2,1)}, u32[]{:S(2)}, u32[]{:S(2)}) async-start(bf16[32,8,512]{2,1,0:T(8,128)(2,1)} %fusion), calls=%async_computation.2 | async-start | bytes 524288 | tf_op jit(solution)/shard_map/all_to_all | solution.py:103
  75.2 50.4 %collective-permute-start.4 = (bf16[512,2048]{1,0:T(8,128)(2,1)}, bf16[512,2048]{1,0:T(8,128)(2,1)}, u32[]{:S(2)}, u32[]{:S(2)}) collective-permute-start(bf16[512,2048]{1,0:T(8,128)(2,1)} %collective-permute-done.refs_3_), channel_id=1, source_target_pairs={{0,1},{1,0},{2,3},{3,2},{4,5},{5,4},{6,7},{7,6},{8,9},{9,8},{10,11... | collective-permute-start | bytes 6291464 | tf_op jit(solution)/shard_map/ppermute | solution.py:112
  121.4 7.1 %collective-permute-start.5 = (bf16[512,2048]{1,0:T(8,128)(2,1)}, bf16[512,2048]{1,0:T(8,128)(2,1)}, u32[]{:S(2)}, u32[]{:S(2)}) collective-permute-start(bf16[512,2048]{1,0:T(8,128)(2,1)} %collective-permute-done.1.refs_4_), channel_id=1, source_target_pairs={{0,1},{1,0},{2,3},{3,2},{4,5},{5,4},{6,7},{7,6},{8,9},{9,8},{10,11... | collective-permute-start | bytes 6291464 | tf_op jit(solution)/shard_map/ppermute | solution.py:112
  121.4 10.1 %collective-permute-start.6 = (bf16[512,2048]{1,0:T(8,128)(2,1)}, bf16[512,2048]{1,0:T(8,128)(2,1)}, u32[]{:S(2)}, u32[]{:S(2)}) collective-permute-start(bf16[512,2048]{1,0:T(8,128)(2,1)} %collective-permute-done.2.refs_5_), channel_id=1, source_target_pairs={{0,1},{1,0},{2,3},{3,2},{4,5},{5,4},{6,7},{7,6},{8,9},{9,8},{10,11... | collective-permute-start | bytes 6291464 | tf_op jit(solution)/shard_map/ppermute | solution.py:112
  123.2 1.8 copy-start.8
  123.2 1.8 copy-start.9
  123.2 1.8 copy-start.10
  131.6 1.6 copy-start.1
  187.4 1.6 copy-start.2
  205.3 35.5 %copy-start.13 = (f32[256]{0:T(256)S(1)}, f32[256]{0:T(256)}, u32[]{:S(2)}) copy-start(f32[256]{0:T(256)} %param.19) | copy-start | bytes 3076
  207.2 15.1 %all-to-all-start.1 = ((f32[32,1,768]{2,1,0:T(1,128)}), f32[32,1,768]{2,1,0:T(1,128)S(1)}, u32[]{:S(2)}, u32[]{:S(2)}) async-start(f32[32,1,768]{2,1,0:T(1,128)} %reshape.305), calls=%async_computation.1 | async-start | bytes 196608 | tf_op jit(solution)/shard_map/all_to_all | solution.py:167
  240.7 1.2 copy-start.7
Sparse Core Ops, SparseCore 0:
  26.4 79.7 all-gather.4
  108.7 78.5 all-gather.2

commit v6 on v4

--- a/solution.py
+++ b/solution.py
@@ -4,6 +4,7 @@
 from jax.experimental import pallas as pl
 from jax.experimental.pallas import tpu as pltpu
 from jax.sharding import PartitionSpec as P
+
 
 kl_coef = 0.1
 discount = 0.99
@@ -170,9 +171,12 @@
             jnp.sum(hidden_f * (norm_gain * value_weight), axis=1),
         ]
     )
-    ref_logprob, squares, score_dot, value_dot = lax.psum(
-        jnp.concatenate([block_logprob[None], sums]), "mp"
-    )
+    squares, score_dot, value_dot = lax.psum(sums, "mp")
+    ref_logprob = block_logprob
+    for shift in range(1, ways):
+        ref_logprob = ref_logprob + lax.ppermute(
+            block_logprob, "mp", [(i, (i + shift) % ways) for i in range(ways)]
+        )
     inv_rms = lax.rsqrt(squares / width_full + norm_eps)
     score = score_dot * inv_rms
     value_est = value_dot * inv_rms

time: 205 us -> 216 us (1.054)
  starting transfers between devices: 78.7 us -> 84.5 us
  waiting for transfers between devices: 51.3 us -> 55.7 us
    ppermute x0 -> x7, starting transfers between devices: none -> 5.76 us  [body(): lax.ppermute(block_logprob, 'mp', [(i, (i + shift) % ways) for i in range...]
    ppermute x0 -> x7, waiting for transfers between devices: none -> 4.42 us  [body(): lax.ppermute(block_logprob, 'mp', [(i, (i + shift) % ways) for i in range...]
    unnamed x34 -> x32, local copies, waits for them, and re-layouts: 5.48 us -> 5.47 us
  transfers between devices with their start and end apart: 11 -> 18, of which waited for: 5 -> 8; matrix products, arithmetic and copies ran while one was open for 5% -> 4% of each run, Pallas kernels for 13% -> 12%
where the time goes in v6:
time: 216 us; the launch traced here: 215 us
  starting transfers between devices  84.5 us (39%)
  waiting for transfers between devices  55.7 us (26%)
  Pallas kernels  25.6 us (12%)
  between operations  14.5 us (7%)
  blocking collectives  14.1 us (7%)
  local copies, waits for them, and re-layouts  10.7 us (5%)
  other arithmetic  7.69 us (4%)
  matrix products  2.32 us (1%)
    ppermute x4, starting transfers between devices, body(): lax.ppermute(block, 'mp', [(i, i ^ 1) for i in range(ways)])  48.4 us
    ppermute x3, waiting for transfers between devices, body(): lax.ppermute(head_weight, 'mp', [(i, (i + 2 * shift) % ways) for i in ran...  30.4 us
    pallas_call x1, Pallas kernels, logit_stats(): pl.pallas_call(lambda *refs: stats_kernel(len(pieces), tile_n, *refs), gr...  25.6 us
    psum x1, blocking collectives, body(): squares, score_dot, value_dot = lax.psum(sums, 'mp')  14.1 us
    all_to_all x1, starting transfers between devices, body(): routed = lax.all_to_all(routed, 'dp', 0, 0, tiled=True)  10.5 us
    all_to_all x1, starting transfers between devices, body(): lax.all_to_all(reward_send.reshape(shards, pair_len, width_dev), 'dp', 0,...  10.4 us
    all_to_all x1, waiting for transfers between devices, body(): routed = lax.all_to_all(routed, 'dp', 0, 0, tiled=True)  8.59 us
    all_to_all x1, starting transfers between devices, body(): lax.all_to_all(ref_send.reshape(ways, sub_len, width_dev), 'mp', 0, 0, ti...  6.51 us
  transfers between devices with their start and end apart: 18, of which 8 were waited for; matrix products, arithmetic and copies ran while one was open for 4% of the time, Pallas kernels for 12%

profile of v6, /device:TPU:1, one launch (start us, length us, event | category | flops | bytes accessed | tf_op | source)
XLA Modules:
  0.0 215.3 jit_solution(4871543673607675576)
XLA Ops:
  7.2 0.8 broadcast_multiply_fusion.1
  8.1 0.8 subtract_multiply_fusion.1
  9.7 1.4 copy.77
  11.3 1.0 convolution_convert_fusion.2
  12.3 6.5 %all-to-all-start = ((bf16[8,32,512]{2,1,0:T(8,128)(2,1)}), bf16[8,32,512]{2,1,0:T(8,128)(2,1)S(1)}, u32[]{:S(2)}, u32[]{:S(2)}) async-start(bf16[8,32,512]{2,1,0:T(8,128)(2,1)} %bitcast.1), calls=%async_computation | async-start | bytes 524288 | tf_op jit(solution)/shard_map/all_to_all | solution.py:122
  18.9 6.5 %all-to-all-done = bf16[8,32,512]{2,1,0:T(8,128)(2,1)S(1)} async-done(((bf16[8,32,512]{2,1,0:T(8,128)(2,1)}), bf16[8,32,512]{2,1,0:T(8,128)(2,1)S(1)}, u32[]{:S(2)}, u32[]{:S(2)}) %all-to-all-start) | async-done | bytes 262176 | tf_op jit(solution)/shard_map/all_to_all | solution.py:122
  25.4 0.3 convolution_convert_fusion.1
  25.7 0.8 copy.87
  26.5 0.4 collective-permute-start
  26.9 1.8 collective-permute-start.1
  28.6 0.7 collective-permute-start.2
  29.4 1.6 collective-permute-start.3
  31.0 0.3 copy.85
  31.4 1.0 fusion
  32.4 10.4 %all-to-all-start.2 = ((bf16[32,8,512]{2,1,0:T(8,128)(2,1)}), bf16[32,8,512]{2,1,0:T(8,128)(2,1)S(1)}, u32[]{:S(2)}, u32[]{:S(2)}) async-start(bf16[32,8,512]{2,1,0:T(8,128)(2,1)} %fusion), calls=%async_computation.2 | async-start | bytes 524288 | tf_op jit(solution)/shard_map/all_to_all | solution.py:104
  43.1 0.2 reduce_window_sum.11
  43.3 0.9 convert_reduce_fusion
  44.2 30.4 %collective-permute-done.refs_3_ = bf16[512,2048]{1,0:T(8,128)(2,1)} collective-permute-done((bf16[512,2048]{1,0:T(8,128)(2,1)S(1)}, bf16[512,2048]{1,0:T(8,128)(2,1)}, u32[]{:S(2)}, u32[]{:S(2)}) %collective-permute-start) | collective-permute-done | bytes 2097184 | tf_op jit(solution)/shard_map/ppermute | solution.py:110
  74.6 46.2 %collective-permute-start.4 = (bf16[512,2048]{1,0:T(8,128)(2,1)}, bf16[512,2048]{1,0:T(8,128)(2,1)}, u32[]{:S(2)}, u32[]{:S(2)}) collective-permute-start(bf16[512,2048]{1,0:T(8,128)(2,1)} %collective-permute-done.refs_3_), channel_id=1, source_target_pairs={{0,1},{1,0},{2,3},{3,2},{4,5},{5,4},{6,7},{7,6},{8,9},{9,8},{10,11... | collective-permute-start | bytes 6291464 | tf_op jit(solution)/shard_map/ppermute | solution.py:113
  120.9 0.6 collective-permute-start.6
  121.5 0.6 subtract_multiply_fusion
  122.9 0.4 copy.76
  123.2 0.5 broadcast_in_dim.105
  123.7 0.6 select_reduce_fusion
  124.3 0.5 sub.123.refs_0_
  125.2 2.8 %collective-permute-done.5.refs_8_ = bf16[512,2048]{1,0:T(8,128)(2,1)} collective-permute-done((bf16[512,2048]{1,0:T(8,128)(2,1)}, bf16[512,2048]{1,0:T(8,128)(2,1)}, u32[]{:S(2)}, u32[]{:S(2)}) %collective-permute-start.5) | collective-permute-done | bytes 2097184 | tf_op jit(solution)/shard_map/ppermute | solution.py:113
  128.0 3.0 %collective-permute-done.6.refs_9_ = bf16[512,2048]{1,0:T(8,128)(2,1)} collective-permute-done((bf16[512,2048]{1,0:T(8,128)(2,1)}, bf16[512,2048]{1,0:T(8,128)(2,1)}, u32[]{:S(2)}, u32[]{:S(2)}) %collective-permute-start.6) | collective-permute-done | bytes 2097184 | tf_op jit(solution)/shard_map/ppermute | solution.py:113
  131.0 1.6 copy-done.1
  132.6 25.6 %shard_map.113 = (f32[2,1024,1]{2,1,0:T(8,128)S(1)}, f32[2,1024,1]{2,1,0:T(8,128)S(1)}, f32[2,1024,1]{2,1,0:T(8,128)S(1)}) custom-call(s32[1024,1]{1,0:T(8,128)S(1)} %sub.123.refs_0_, bf16[1024,4096]{1,0:T(8,128)(2,1)} %all-gather.2.cloned.1.call-done.refs_1_, bf16[512,2048]{1,0:T(8,128)(2,1)S(1)} %copy-done.1, ...), custom_call_target="tpu_custom_call" | custom-call | flops 17179869184 | bytes 33554432 | tf_op jit(solution)/shard_map/pallas_call | solution.py:49
  158.2 0.5 fusion.23
  158.8 0.3 reduce.7
  159.5 0.2 reduce_sum.112
  160.0 0.3 select_reduce_fusion.1
  160.2 0.8 reshape.274
  161.1 10.5 %all-to-all-start.1 = ((f32[32,1,768]{2,1,0:T(1,128)}), f32[32,1,768]{2,1,0:T(1,128)S(1)}, u32[]{:S(2)}, u32[]{:S(2)}) async-start(f32[32,1,768]{2,1,0:T(1,128)} %reshape.274), calls=%async_computation.1 | async-start | bytes 196608 | tf_op jit(solution)/shard_map/all_to_all | solution.py:157
  172.0 8.6 %all-to-all-done.1 = f32[32,1,768]{2,1,0:T(1,128)S(1)} async-done(((f32[32,1,768]{2,1,0:T(1,128)}), f32[32,1,768]{2,1,0:T(1,128)S(1)}, u32[]{:S(2)}, u32[]{:S(2)}) %all-to-all-start.1) | async-done | bytes 98336 | tf_op jit(solution)/shard_map/all_to_all | solution.py:157
  180.6 0.5 broadcast.294
  181.1 0.9 reduce.10
  182.6 1.0 collective-permute-start.11
  183.5 14.1 %psum.7 = f32[3,256]{1,0:T(4,128)S(1)} all-reduce(f32[3,256]{1,0:T(4,128)S(1)} %pad_maximum_fusion), channel_id=1, replica_groups=mesh['dp'=32,'mp'=8] {'mp'}, use_global_device_ids=true, to_apply=%region_15.16 | all-reduce | flops 768 | bytes 6144 | tf_op jit(solution)/shard_map/psum | solution.py:174
  197.7 2.0 collective-permute-start.12
  199.7 1.0 collective-permute-start.13
  200.7 1.6 collective-permute-start.7
  202.5 1.3 collective-permute-done.13
  203.8 2.1 collective-permute-done.8
  205.9 1.0 collective-permute-done.9
  206.9 0.6 fusion.18
  207.8 0.7 reshape.270
  (103 shorter events, 4.5 us)
Async XLA Ops:
  9.7 16.8 %copy-start = (bf16[512,2048]{1,0:T(8,128)(2,1)S(1)}, bf16[512,2048]{1,0:T(8,128)(2,1)}, u32[]{:S(2)}) copy-start(bf16[512,2048]{1,0:T(8,128)(2,1)} %refs_2_.1) | copy-start | bytes 6291460
  9.7 21.3 %copy-start.2 = (bf16[64,7,512]{2,0,1:T(8,128)(2,1)S(1)}, bf16[64,7,512]{2,0,1:T(8,128)(2,1)}, u32[]{:S(2)}) copy-start(bf16[64,7,512]{2,0,1:T(8,128)(2,1)} %param.14) | copy-start | bytes 1376260
  11.3 1.0 copy-start.9
  12.3 13.0 %all-to-all-start = ((bf16[8,32,512]{2,1,0:T(8,128)(2,1)}), bf16[8,32,512]{2,1,0:T(8,128)(2,1)S(1)}, u32[]{:S(2)}, u32[]{:S(2)}) async-start(bf16[8,32,512]{2,1,0:T(8,128)(2,1)} %bitcast.1), calls=%async_computation | async-start | bytes 524288 | tf_op jit(solution)/shard_map/all_to_all | solution.py:122
  18.9 12.5 %copy-start.10 = (s32[448]{0:T(512)S(1)}, s32[448]{0:T(512)}, u32[]{:S(2)}) copy-start(s32[448]{0:T(512)} %copy-done.9) | copy-start | bytes 5380
  18.9 112.1 %all-gather.2.cloned.1.call-start = ((), (), s32[]{:S(2)}) async-start(), calls=%async_computation.3 | async-start | bytes 8650752 | tf_op jit(solution)/shard_map/all_gather | solution.py:126
  25.7 17.2 %copy-start.4 = (s32[2048]{0:T(1024)S(1)}, s32[2048]{0:T(1024)}, u32[]{:S(2)}) copy-start(s32[2048]{0:T(1024)} %param.12) | copy-start | bytes 24580
  25.7 17.3 %copy-start.5 = (s32[2048]{0:T(1024)S(1)}, s32[2048]{0:T(1024)}, u32[]{:S(2)}) copy-start(s32[2048]{0:T(1024)} %param.11) | copy-start | bytes 24580
  26.5 48.1 %collective-permute-start = (bf16[512,2048]{1,0:T(8,128)(2,1)S(1)}, bf16[512,2048]{1,0:T(8,128)(2,1)}, u32[]{:S(2)}, u32[]{:S(2)}) collective-permute-start(bf16[512,2048]{1,0:T(8,128)(2,1)S(1)} %copy-done), channel_id=1, source_target_pairs={{0,2},{1,3},{2,4},{3,5},{4,6},{5,7},{6,0},{7,1},{8,10},{9,11},{10,... | collective-permute-start | bytes 6291464 | tf_op jit(solution)/shard_map/ppermute | solution.py:110
  26.9 94.0 %collective-permute-start.1 = (bf16[512,2048]{1,0:T(8,128)(2,1)S(1)}, bf16[512,2048]{1,0:T(8,128)(2,1)}, u32[]{:S(2)}, u32[]{:S(2)}) collective-permute-start(bf16[512,2048]{1,0:T(8,128)(2,1)S(1)} %copy-done), channel_id=1, source_target_pairs={{0,4},{1,5},{2,6},{3,7},{4,0},{5,1},{6,2},{7,3},{8,12},{9,13},{10,... | collective-permute-start | bytes 6291464 | tf_op jit(solution)/shard_map/ppermute | solution.py:110
  28.6 92.3 %collective-permute-start.2 = (bf16[512,2048]{1,0:T(8,128)(2,1)S(1)}, bf16[512,2048]{1,0:T(8,128)(2,1)}, u32[]{:S(2)}, u32[]{:S(2)}) collective-permute-start(bf16[512,2048]{1,0:T(8,128)(2,1)S(1)} %copy-done), channel_id=1, source_target_pairs={{0,6},{1,7},{2,0},{3,1},{4,2},{5,3},{6,4},{7,5},{8,14},{9,15},{10,... | collective-permute-start | bytes 6291464 | tf_op jit(solution)/shard_map/ppermute | solution.py:110
  29.4 95.8 %collective-permute-start.3 = (bf16[512,2048]{1,0:T(8,128)(2,1)S(1)}, bf16[512,2048]{1,0:T(8,128)(2,1)}, u32[]{:S(2)}, u32[]{:S(2)}) collective-permute-start(bf16[512,2048]{1,0:T(8,128)(2,1)S(1)} %copy-done), channel_id=1, source_target_pairs={{0,1},{1,0},{2,3},{3,2},{4,5},{5,4},{6,7},{7,6},{8,9},{9,8},{10,11... | collective-permute-start | bytes 6291464 | tf_op jit(solution)/shard_map/ppermute | solution.py:113
  32.4 128.6 %all-to-all-start.2 = ((bf16[32,8,512]{2,1,0:T(8,128)(2,1)}), bf16[32,8,512]{2,1,0:T(8,128)(2,1)S(1)}, u32[]{:S(2)}, u32[]{:S(2)}) async-start(bf16[32,8,512]{2,1,0:T(8,128)(2,1)} %fusion), calls=%async_computation.2 | async-start | bytes 524288 | tf_op jit(solution)/shard_map/all_to_all | solution.py:104
  42.9 80.0 %copy-start.3 = (s32[2048,7]{0,1:T(8,128)S(1)}, s32[2048,7]{0,1:T(8,128)}, u32[]{:S(2)}) copy-start(s32[2048,7]{0,1:T(8,128)} %param.10) | copy-start | bytes 172036
  74.6 50.6 %collective-permute-start.4 = (bf16[512,2048]{1,0:T(8,128)(2,1)}, bf16[512,2048]{1,0:T(8,128)(2,1)}, u32[]{:S(2)}, u32[]{:S(2)}) collective-permute-start(bf16[512,2048]{1,0:T(8,128)(2,1)} %collective-permute-done.refs_3_), channel_id=1, source_target_pairs={{0,1},{1,0},{2,3},{3,2},{4,5},{5,4},{6,7},{7,6},{8,9},{9,8},{10,11... | collective-permute-start | bytes 6291464 | tf_op jit(solution)/shard_map/ppermute | solution.py:113
  120.9 7.1 %collective-permute-start.5 = (bf16[512,2048]{1,0:T(8,128)(2,1)}, bf16[512,2048]{1,0:T(8,128)(2,1)}, u32[]{:S(2)}, u32[]{:S(2)}) collective-permute-start(bf16[512,2048]{1,0:T(8,128)(2,1)} %collective-permute-done.1.refs_4_), channel_id=1, source_target_pairs={{0,1},{1,0},{2,3},{3,2},{4,5},{5,4},{6,7},{7,6},{8,9},{9,8},{10,11... | collective-permute-start | bytes 6291464 | tf_op jit(solution)/shard_map/ppermute | solution.py:113
  120.9 10.1 %collective-permute-start.6 = (bf16[512,2048]{1,0:T(8,128)(2,1)}, bf16[512,2048]{1,0:T(8,128)(2,1)}, u32[]{:S(2)}, u32[]{:S(2)}) collective-permute-start(bf16[512,2048]{1,0:T(8,128)(2,1)} %collective-permute-done.2.refs_5_), channel_id=1, source_target_pairs={{0,1},{1,0},{2,3},{3,2},{4,5},{5,4},{6,7},{7,6},{8,9},{9,8},{10,11... | collective-permute-start | bytes 6291464 | tf_op jit(solution)/shard_map/ppermute | solution.py:113
  122.6 2.6 %copy-start.6 = (f32[512]{0:T(512)S(1)}, f32[512]{0:T(512)}, u32[]{:S(2)}) copy-start(f32[512]{0:T(512)} %param.16) | copy-start | bytes 6148
  122.6 2.6 %copy-start.7 = (f32[512]{0:T(512)S(1)}, f32[512]{0:T(512)}, u32[]{:S(2)}) copy-start(f32[512]{0:T(512)} %param.18) | copy-start | bytes 6148
  122.6 2.6 %copy-start.8 = (f32[512]{0:T(512)S(1)}, f32[512]{0:T(512)}, u32[]{:S(2)}) copy-start(f32[512]{0:T(512)} %param.17) | copy-start | bytes 6148
  122.7 2.2 %copy-start.12 = (s32[32]{0:T(128)S(1)}, s32[32]{0:T(128)}, u32[]{:S(2)}) copy-start(s32[32]{0:T(128)} %get-tuple-element.28) | copy-start | bytes 388
  131.0 1.6 copy-start.1
  159.4 47.5 %copy-start.11 = (f32[256]{0:T(256)S(1)}, f32[256]{0:T(256)}, u32[]{:S(2)}) copy-start(f32[256]{0:T(256)} %param.19) | copy-start | bytes 3076
  161.1 19.6 %all-to-all-start.1 = ((f32[32,1,768]{2,1,0:T(1,128)}), f32[32,1,768]{2,1,0:T(1,128)S(1)}, u32[]{:S(2)}, u32[]{:S(2)}) async-start(f32[32,1,768]{2,1,0:T(1,128)} %reshape.274), calls=%async_computation.1 | async-start | bytes 196608 | tf_op jit(solution)/shard_map/all_to_all | solution.py:157
  182.5 19.8 %collective-permute-start.10 = (f32[256]{0:T(256)S(1)}, f32[256]{0:T(256)S(1)}, u32[]{:S(2)}, u32[]{:S(2)}) collective-permute-start(f32[256]{0:T(256)S(1)} %select_n.151), channel_id=1, source_target_pairs={{0,4},{1,5},{2,6},{3,7},{4,0},{5,1},{6,2},{7,3},{8,12},{9,13},{10,... | collective-permute-start | bytes 3080 | tf_op jit(solution)/shard_map/ppermute | solution.py:177
  182.6 19.8 %collective-permute-start.11 = (f32[256]{0:T(256)S(1)}, f32[256]{0:T(256)S(1)}, u32[]{:S(2)}, u32[]{:S(2)}) collective-permute-start(f32[256]{0:T(256)S(1)} %select_n.151), channel_id=1, source_target_pairs={{0,5},{1,6},{2,7},{3,0},{4,1},{5,2},{6,3},{7,4},{8,13},{9,14},{10,... | collective-permute-start | bytes 3080 | tf_op jit(solution)/shard_map/ppermute | solution.py:177
  197.7 4.8 %collective-permute-start.12 = (f32[256]{0:T(256)S(1)}, f32[256]{0:T(256)S(1)}, u32[]{:S(2)}, u32[]{:S(2)}) collective-permute-start(f32[256]{0:T(256)S(1)} %select_n.151), channel_id=1, source_target_pairs={{0,6},{1,7},{2,0},{3,1},{4,2},{5,3},{6,4},{7,5},{8,14},{9,15},{10,... | collective-permute-start | bytes 3080 | tf_op jit(solution)/shard_map/ppermute | solution.py:177
  199.7 4.1 %collective-permute-start.13 = (f32[256]{0:T(256)S(1)}, f32[256]{0:T(256)S(1)}, u32[]{:S(2)}, u32[]{:S(2)}) collective-permute-start(f32[256]{0:T(256)S(1)} %select_n.151), channel_id=1, source_target_pairs={{0,7},{1,0},{2,1},{3,2},{4,3},{5,4},{6,5},{7,6},{8,15},{9,8},{10,9... | collective-permute-start | bytes 3080 | tf_op jit(solution)/shard_map/ppermute | solution.py:177
  200.7 3.2 %collective-permute-start.7 = (f32[256]{0:T(256)S(1)}, f32[256]{0:T(256)S(1)}, u32[]{:S(2)}, u32[]{:S(2)}) collective-permute-start(f32[256]{0:T(256)S(1)} %select_n.151), channel_id=1, source_target_pairs={{0,1},{1,2},{2,3},{3,4},{4,5},{5,6},{6,7},{7,0},{8,9},{9,10},{10,1... | collective-permute-start | bytes 3080 | tf_op jit(solution)/shard_map/ppermute | solution.py:177
  202.3 3.6 %collective-permute-start.8 = (f32[256]{0:T(256)S(1)}, f32[256]{0:T(256)S(1)}, u32[]{:S(2)}, u32[]{:S(2)}) collective-permute-start(f32[256]{0:T(256)S(1)} %select_n.151), channel_id=1, source_target_pairs={{0,2},{1,3},{2,4},{3,5},{4,6},{5,7},{6,0},{7,1},{8,10},{9,11},{10,... | collective-permute-start | bytes 3080 | tf_op jit(solution)/shard_map/ppermute | solution.py:177
  202.4 4.5 %collective-permute-start.9 = (f32[256]{0:T(256)S(1)}, f32[256]{0:T(256)S(1)}, u32[]{:S(2)}, u32[]{:S(2)}) collective-permute-start(f32[256]{0:T(256)S(1)} %select_n.151), channel_id=1, source_target_pairs={{0,3},{1,4},{2,5},{3,6},{4,7},{5,0},{6,1},{7,2},{8,11},{9,12},{10,... | collective-permute-start | bytes 3080 | tf_op jit(solution)/shard_map/ppermute | solution.py:177
Sparse Core Ops, SparseCore 0:
  26.6 99.3 all-gather.1

commit v7 on v4

--- a/solution.py
+++ b/solution.py
@@ -1,4 +1,7 @@
+import functools
+
 import jax
+import numpy as np
 import jax.numpy as jnp
 from jax import lax
 from jax.experimental import pallas as pl
@@ -19,17 +22,18 @@
     return jnp.sum(jnp.logical_and(same, earlier).astype(jnp.int32), axis=-1)
 
 
-def stats_kernel(pieces, tile_n, target_ref, rows_ref, *refs):
+def stats_kernel(heights, tile_n, target_ref, rows_ref, *refs):
+    pieces = len(heights)
     weight_refs = refs[:pieces]
     max_ref, total_ref, target_logit_ref = refs[pieces:]
-    width = weight_refs[0].shape[0]
-    logits = jnp.dot(rows_ref[:, 0:width], weight_refs[0][...], preferred_element_type=jnp.float32)
-    for k in range(1, pieces):
-        logits = logits + jnp.dot(
-            rows_ref[:, k * width : (k + 1) * width],
-            weight_refs[k][...],
-            preferred_element_type=jnp.float32,
+    logits = None
+    offset = 0
+    for k, height in enumerate(heights):
+        part = jnp.dot(
+            rows_ref[:, offset : offset + height], weight_refs[k][...], preferred_element_type=jnp.float32
         )
+        logits = part if logits is None else logits + part
+        offset += height
     row_max = jnp.max(logits, axis=1, keepdims=True)
     total = jnp.sum(jnp.exp(logits - row_max), axis=1, keepdims=True)
     column = lax.broadcasted_iota(jnp.int32, logits.shape, 1) + pl.program_id(0) * tile_n
@@ -41,18 +45,19 @@
 
 def logit_stats(rows, pieces, local_target, tile_m=256, tile_n=1024):
     count, width_full = rows.shape
-    width, vocab = pieces[0].shape
+    vocab = pieces[0].shape[1]
+    heights = tuple(piece.shape[0] for piece in pieces)
     grid = (vocab // tile_n, count // tile_m)
     stat_shape = jax.ShapeDtypeStruct((grid[0], count, 1), jnp.float32)
     stat_spec = pl.BlockSpec((1, tile_m, 1), lambda j, i: (j, i, 0))
     return pl.pallas_call(
-        lambda *refs: stats_kernel(len(pieces), tile_n, *refs),
+        lambda *refs: stats_kernel(heights, tile_n, *refs),
         grid=grid,
         in_specs=[
             pl.BlockSpec((tile_m, 1), lambda j, i: (i, 0)),
             pl.BlockSpec((tile_m, width_full), lambda j, i: (i, 0)),
         ]
-        + [pl.BlockSpec((width, tile_n), lambda j, i: (0, j)) for _ in pieces],
+        + [pl.BlockSpec((height, tile_n), lambda j, i: (0, j)) for height in heights],
         out_specs=[stat_spec, stat_spec, stat_spec],
         out_shape=[stat_shape, stat_shape, stat_shape],
         compiler_params=pltpu.CompilerParams(vmem_limit_bytes=48 * 1024 * 1024),
@@ -64,7 +69,16 @@
     )(local_target.reshape(count, 1), rows, *pieces)
 
 
+def ring_perm(places, step):
+    zs, xs = places.shape
+    where = {int(places[z, x]): (z, x) for z in range(zs) for x in range(xs)}
+    return [
+        (i, int(places[(z + step[0]) % zs, (x + step[1]) % xs])) for i, (z, x) in sorted(where.items())
+    ]
+
+
 def body(
+    places,
     token_ids,
     lengths,
     pack_dest,
@@ -105,14 +119,25 @@
     ).reshape(slot_dev, width_dev)
 
     chips = ways // 2
-    own_core = [head_weight] + [
-        lax.ppermute(head_weight, "mp", [(i, (i + 2 * shift) % ways) for i in range(ways)])
-        for shift in range(1, chips)
+    half = width_dev // 2
+
+    def along_y(x, shift):
+        return lax.ppermute(x, "mp", [(i, ((i // 2 + shift) % chips) * 2 + i % 2) for i in range(ways)])
+
+    from_prev = along_y(head_weight, 1)
+    from_next = along_y(head_weight, -1)
+    own_core = [
+        head_weight,
+        from_prev,
+        from_next,
+        along_y(from_prev[:half], 1),
+        along_y(from_next[half:], -1),
     ]
     mate_core = [lax.ppermute(block, "mp", [(i, i ^ 1) for i in range(ways)]) for block in own_core]
     chip, core = part // 2, part % 2
     order = jnp.arange(ways, dtype=jnp.int32)
-    source_chip = (chip - order % chips) % chips
+    chip_step = jnp.array([0, -1, 1, -2], jnp.int32)
+    source_chip = (chip + chip_step[order % chips]) % chips
     source_core = jnp.where(order < chips, core, 1 - core)
     pick = (
         (source_chip * 2 + source_core)[:, None] == jnp.arange(ways, dtype=jnp.int32)[None, :]
@@ -122,7 +147,34 @@
     own_rows = jnp.einsum(
         "msf,nm->snf", parts_rows, pick, preferred_element_type=jnp.float32
     ).astype(jnp.bfloat16).reshape(sub_len, width_full)
-    block_rows = lax.all_gather(own_rows, "dp", axis=0, tiled=True)
+
+    zs, xs = places.shape
+    x_fwd = lax.ppermute(own_rows, "dp", ring_perm(places, (0, 1)))
+    x_back = lax.ppermute(own_rows, "dp", ring_perm(places, (0, -1)))
+    x_far = lax.ppermute(x_fwd, "dp", ring_perm(places, (0, 1)))
+    x_steps = [0, -1, 1, -2]
+    group = jnp.stack([own_rows, x_fwd, x_back, x_far])
+    z_groups = [group]
+    z_steps = [0]
+    fwd, back = group, group
+    for hop in range(1, zs // 2):
+        fwd = lax.ppermute(fwd, "dp", ring_perm(places, (1, 0)))
+        back = lax.ppermute(back, "dp", ring_perm(places, (-1, 0)))
+        z_groups += [fwd, back]
+        z_steps += [-hop, hop]
+    split = len(x_steps) // 2
+    far_a = lax.ppermute(fwd[:split], "dp", ring_perm(places, (1, 0)))
+    far_b = lax.ppermute(back[split:], "dp", ring_perm(places, (-1, 0)))
+    z_groups.append(jnp.concatenate([far_a, far_b]))
+    z_steps.append(-(zs // 2))
+    block_rows = jnp.concatenate(z_groups).reshape(-1, width_full)
+    my_z = jnp.argmax(jnp.any(places == me, axis=1))
+    my_x = jnp.argmax(jnp.any(places == me, axis=0))
+    places_arr = jnp.asarray(places, jnp.int32)
+    source_shard = jnp.stack(
+        [places_arr[(my_z + dz) % zs, (my_x + dx) % xs] for dz in z_steps for dx in x_steps]
+    )
+    is_source = source_shard[:, None] == jnp.arange(shards, dtype=jnp.int32)[None, :]
 
     dest_all = pack_dest.reshape(shards, req_dev)
     size_all = lengths.reshape(shards, req_dev)
@@ -135,9 +187,8 @@
     )
     key = jnp.where(steps[None, None, :] < size_all[:, :, None], key, -1).reshape(shards, 1, -1)
     hits = key == jnp.arange(sub_len, dtype=jnp.int32)[None, :, None]
-    targets = jnp.sum(
-        jnp.where(hits, token_ids.reshape(shards, 1, -1), 0), axis=2
-    ).reshape(-1)
+    targets = jnp.sum(jnp.where(hits, token_ids.reshape(shards, 1, -1), 0), axis=2)
+    targets = jnp.sum(jnp.where(is_source[:, :, None], targets[None], 0), axis=1).reshape(-1)
 
     vocab_dev = head_weight.shape[1]
     tile_max, tile_total, tile_target = logit_stats(
@@ -146,7 +197,9 @@
     row_max = jnp.max(tile_max[:, :, 0], axis=0)
     exp_total = jnp.sum(tile_total[:, :, 0] * jnp.exp(tile_max[:, :, 0] - row_max[None, :]), axis=0)
     target_logit = jnp.sum(tile_target[:, :, 0], axis=0)
-    stats = jnp.stack([row_max, exp_total, target_logit]).reshape(3, shards, blocks, pair_len)
+    stats = jnp.stack([row_max, exp_total, target_logit]).reshape(3, shards, 1, sub_len)
+    stats = jnp.sum(jnp.where(is_source[None, :, :, None], stats, 0.0), axis=1)
+    stats = stats.reshape(3, shards, blocks, pair_len)
     to_shard = jnp.arange(shards, dtype=jnp.int32)[:, None] == (
         part * blocks + jnp.arange(blocks, dtype=jnp.int32)
     )[None, :]
@@ -199,8 +252,14 @@
 
 
 def solution(mesh):
+    dp_devices = mesh.devices[:, 0]
+    zs = sorted({d.coords[2] for d in dp_devices})
+    xs = sorted({d.coords[0] for d in dp_devices})
+    places = np.zeros((len(zs), len(xs)), np.int32)
+    for i, d in enumerate(dp_devices):
+        places[zs.index(d.coords[2]), xs.index(d.coords[0])] = i
     return jax.shard_map(
-        body,
+        functools.partial(body, places),
         mesh=mesh,
         in_specs=(
             P(),

time: 205 us -> 248 us (1.21)
  waiting for transfers between devices: 51.3 us -> 94 us
  local copies, waits for them, and re-layouts: 10.8 us -> 40.6 us
  starting transfers between devices: 78.7 us -> 49.8 us
  between operations: 14.5 us -> 11.8 us
    ppermute x3 -> x15, waiting for transfers between devices: 31.3 us -> 83.4 us  [the longest x3 55.5 us: body(): fwd = lax.ppermute(fwd, 'dp', ring_perm(places, (1, 0)))]
    ppermute x4 -> x5, starting transfers between devices: 48.4 us -> 9.61 us  [body(): lax.ppermute(block, 'mp', [(i, i ^ 1) for i in range(ways)])]
    another operation x6 -> x5, local copies, waits for them, and re-layouts: 0.6 us -> 21 us  [the longest x1 20.7 us: body(): jnp.stack([places_arr[(my_z + dz) % zs, (my_x + dx) % xs] for dz in z_ste...]
    ppermute x3 -> x15, starting transfers between devices: 2.87 us -> 20.4 us  [the longest x3 6.82 us: body(): back = lax.ppermute(back, 'dp', ring_perm(places, (-1, 0)))]
    all_to_all x1, waiting for transfers between devices: 6.48 us -> 0.01 us  [body(): lax.all_to_all(ref_send.reshape(ways, sub_len, width_dev), 'mp', 0, 0, ti...]
    all_to_all x1, starting transfers between devices: 10.5 us -> 7.1 us  [body(): routed = lax.all_to_all(routed, 'dp', 0, 0, tiled=True)]
    all_to_all x1, starting transfers between devices: 6.51 us -> 3.36 us  [body(): lax.all_to_all(ref_send.reshape(ways, sub_len, width_dev), 'mp', 0, 0, ti...]
    ppermute x4 -> x5, waiting for transfers between devices: 5.15 us -> 2.11 us  [body(): lax.ppermute(block, 'mp', [(i, i ^ 1) for i in range(ways)])]
  transfers between devices with their start and end apart: 11 -> 23, of which waited for: 5 -> 10; matrix products, arithmetic and copies ran while one was open for 5% -> 19% of each run, Pallas kernels for 13% -> 10%
where the time goes in v7:
time: 248 us; the launch traced here: 247 us
  waiting for transfers between devices  94 us (38%)
  starting transfers between devices  49.8 us (20%)
  local copies, waits for them, and re-layouts  40.6 us (16%)
  Pallas kernels  25.7 us (10%)
  blocking collectives  13.6 us (5%)
  between operations  11.8 us (5%)
  other arithmetic  9.54 us (4%)
    ppermute x3, waiting for transfers between devices, body(): fwd = lax.ppermute(fwd, 'dp', ring_perm(places, (1, 0)))  55.5 us
    pallas_call x1, Pallas kernels, logit_stats(): pl.pallas_call(lambda *refs: stats_kernel(heights, tile_n, *refs), grid=g...  25.7 us
    another operation x1, local copies, waits for them, and re-layouts, body(): jnp.stack([places_arr[(my_z + dz) % zs, (my_x + dx) % xs] for dz in z_ste...  20.7 us
    psum x1, blocking collectives, body(): lax.psum(jnp.concatenate([block_logprob[None], sums]), 'mp')  13.6 us
    ppermute x1, waiting for transfers between devices, body(): far_a = lax.ppermute(fwd[:split], 'dp', ring_perm(places, (1, 0)))  11.4 us
    ppermute x5, starting transfers between devices, body(): lax.ppermute(block, 'mp', [(i, i ^ 1) for i in range(ways)])  9.61 us
    all_to_all x1, starting transfers between devices, body(): lax.all_to_all(reward_send.reshape(shards, pair_len, width_dev), 'dp', 0,...  9.34 us
    all_to_all x1, waiting for transfers between devices, body(): routed = lax.all_to_all(routed, 'dp', 0, 0, tiled=True)  8.43 us
  transfers between devices with their start and end apart: 23, of which 10 were waited for; matrix products, arithmetic and copies ran while one was open for 19% of the time, Pallas kernels for 10%

profile of v7, /device:TPU:1, one launch (start us, length us, event | category | flops | bytes accessed | tf_op | source)
XLA Modules:
  0.0 247.3 jit_solution(7505501314868210265)
XLA Ops:
  0.7 2.2 collective-permute-start.11
  2.9 1.5 collective-permute-start.12
  4.4 2.8 %collective-permute-start.15 = (bf16[512,2048]{1,0:T(8,128)(2,1)}, bf16[512,2048]{1,0:T(8,128)(2,1)}, u32[]{:S(2)}, u32[]{:S(2)}) collective-permute-start(bf16[512,2048]{1,0:T(8,128)(2,1)} %refs_2_.1), channel_id=1, source_target_pairs={{0,1},{1,0},{2,3},{3,2},{4,5},{5,4},{6,7},{7,6},{8,9},{9,8},{10,11... | collective-permute-start | bytes 6291464 | tf_op jit(solution)/shard_map/ppermute | solution.py:136
  7.2 0.8 broadcast_multiply_fusion.1
  8.1 0.8 subtract_multiply_fusion.1
  9.7 1.3 copy.75
  11.2 1.0 convolution_convert_fusion.2
  12.2 3.4 %all-to-all-start = ((bf16[8,32,512]{2,1,0:T(8,128)(2,1)}), bf16[8,32,512]{2,1,0:T(8,128)(2,1)S(1)}, u32[]{:S(2)}, u32[]{:S(2)}) async-start(bf16[8,32,512]{2,1,0:T(8,128)(2,1)} %bitcast.34), calls=%async_computation | async-start | bytes 524288 | tf_op jit(solution)/shard_map/all_to_all | solution.py:146
  15.6 0.8 compare_reduce_fusion
  16.4 0.7 iota_reduce_fusion
  28.1 0.8 broadcast_in_dim_reshape.2
  28.9 0.8 lt.394
  29.8 2.7 %fusion.24 = (s32[1,1]{0,1:T(1,128)}, s32[1,1]{0,1:T(1,128)}, s32[1,1]{0,1:T(1,128)}, s32[1,1]{0,1:T(1,128)}, s32[1,1]{0,1:T(1,128)}, /*index=5*/s32[1,1]{0,1:T(...) fusion(s32[8,4]{0,1:T(4,128)} %constant.281.clone, ...), kind=kLoop, calls=%fused_computation.98 | loop fusion | bytes 304 | tf_op jit(solution)/shard_map/dynamic_slice | solution.py:175
  32.5 20.7 %stack.46 = s32[32]{0:T(128)S(1)} concatenate(s32[1]{0:T(128)} %bitcast, s32[1]{0:T(128)} %bitcast.1, s32[1]{0:T(128)} %bitcast.2, s32[1]{0:T(128)} %bitcast.3, s32[1]{0:T(128)} %bitcast.4, s32[1]{0:T(128)} %bitcast.5, s32[1]{0:T(128)} %bitcast.6, s32[1]{0:T(128)} %bitcast.7, s32[1]{0:T(128)} %bitcast.8, s32[1]{0:T(128)} %bitcast.9, s32[1]{0:T(128)} %bitcast.10, s32[1]{0:T(128)} %bitcast.11, ...), dimensions={0} | concatenate | bytes 256 | tf_op jit(solution)/shard_map/stack | solution.py:174
  53.5 0.9 convert_reduce_fusion
  55.2 1.2 copy.74
  57.3 1.0 fusion
  59.7 9.3 %all-to-all-start.2 = ((bf16[32,8,512]{2,1,0:T(8,128)(2,1)}), bf16[32,8,512]{2,1,0:T(8,128)(2,1)S(1)}, u32[]{:S(2)}, u32[]{:S(2)}) async-start(bf16[32,8,512]{2,1,0:T(8,128)(2,1)} %fusion), calls=%async_computation.2 | async-start | bytes 524288 | tf_op jit(solution)/shard_map/all_to_all | solution.py:117
  69.4 1.3 collective-permute-start
  71.0 1.5 collective-permute-start.1
  72.5 8.4 %collective-permute-done = bf16[32,4096]{1,0:T(8,128)(2,1)S(1)} collective-permute-done((bf16[32,4096]{1,0:T(8,128)(2,1)S(1)}, bf16[32,4096]{1,0:T(8,128)(2,1)S(1)}, u32[]{:S(2)}, u32[]{:S(2)}) %collective-permute-start) | collective-permute-done | bytes 262176 | tf_op jit(solution)/shard_map/ppermute | solution.py:152
  81.6 7.3 %collective-permute-done.2 = bf16[32,4096]{1,0:T(8,128)(2,1)S(1)} collective-permute-done((bf16[32,4096]{1,0:T(8,128)(2,1)S(1)}, bf16[32,4096]{1,0:T(8,128)(2,1)S(1)}, u32[]{:S(2)}, u32[]{:S(2)}) %collective-permute-start.2) | collective-permute-done | bytes 262176 | tf_op jit(solution)/shard_map/ppermute | solution.py:154
  89.0 1.4 collective-permute-start.3
  90.4 1.5 collective-permute-start.4
  92.0 21.3 %collective-permute-done.3 = bf16[4,32,4096]{2,1,0:T(8,128)(2,1)S(1)} collective-permute-done((bf16[4,32,4096]{2,1,0:T(8,128)(2,1)S(1)}, bf16[4,32,4096]{2,1,0:T(8,128)(2,1)S(1)}, u32[]{:S(2)}, u32[]{:S(2)}) %collective-permute-start.3) | collective-permute-done | bytes 1048608 | tf_op jit(solution)/shard_map/ppermute | solution.py:161
  113.3 2.6 %collective-permute-start.6 = (bf16[4,32,4096]{2,1,0:T(8,128)(2,1)S(1)}, bf16[4,32,4096]{2,1,0:T(8,128)(2,1)S(1)}, u32[]{:S(2)}, u32[]{:S(2)}) collective-permute-start(bf16[4,32,4096]{2,1,0:T(8,128)(2,1)S(1)} %collective-permute-done.4), channel_id=1, source_target_pairs={{0,224},{8,232},{16,240},{24,248},{32,0},{40,8},{48,16},{56,24},{6... | collective-permute-start | bytes 3145736 | tf_op jit(solution)/shard_map/ppermute | solution.py:162
  116.0 1.3 slice.101
  118.0 1.3 slice.102
  119.3 2.2 collective-permute-start.14
  121.5 14.9 %collective-permute-done.5 = bf16[4,32,4096]{2,1,0:T(8,128)(2,1)S(1)} collective-permute-done((bf16[4,32,4096]{2,1,0:T(8,128)(2,1)S(1)}, bf16[4,32,4096]{2,1,0:T(8,128)(2,1)S(1)}, u32[]{:S(2)}, u32[]{:S(2)}) %collective-permute-start.5) | collective-permute-done | bytes 1048608 | tf_op jit(solution)/shard_map/ppermute | solution.py:161
  136.4 2.7 %collective-permute-start.8 = (bf16[4,32,4096]{2,1,0:T(8,128)(2,1)S(1)}, bf16[4,32,4096]{2,1,0:T(8,128)(2,1)S(1)}, u32[]{:S(2)}, u32[]{:S(2)}) collective-permute-start(bf16[4,32,4096]{2,1,0:T(8,128)(2,1)S(1)} %collective-permute-done.6), channel_id=1, source_target_pairs={{0,224},{8,232},{16,240},{24,248},{32,0},{40,8},{48,16},{56,24},{6... | collective-permute-start | bytes 3145736 | tf_op jit(solution)/shard_map/ppermute | solution.py:162
  139.3 19.3 %collective-permute-done.7 = bf16[4,32,4096]{2,1,0:T(8,128)(2,1)S(1)} collective-permute-done((bf16[4,32,4096]{2,1,0:T(8,128)(2,1)S(1)}, bf16[4,32,4096]{2,1,0:T(8,128)(2,1)S(1)}, u32[]{:S(2)}, u32[]{:S(2)}) %collective-permute-start.7) | collective-permute-done | bytes 1048608 | tf_op jit(solution)/shard_map/ppermute | solution.py:161
  158.6 4.5 %collective-permute-start.16 = (bf16[512,2048]{1,0:T(8,128)(2,1)}, bf16[512,2048]{1,0:T(8,128)(2,1)S(1)}, u32[]{:S(2)}, u32[]{:S(2)}) collective-permute-start(bf16[512,2048]{1,0:T(8,128)(2,1)} %collective-permute-done.11.refs_3_), channel_id=1, source_target_pairs={{0,1},{1,0},{2,3},{3,2},{4,5},{5,4},{6,7},{7,6},{8,9},{9,8},{10,11... | collective-permute-start | bytes 6291464 | tf_op jit(solution)/shard_map/ppermute | solution.py:136
  163.4 1.9 collective-permute-start.9
  165.2 0.9 collective-permute-start.10
  166.3 11.4 %collective-permute-done.9 = bf16[2,32,4096]{2,1,0:T(8,128)(2,1)S(1)} collective-permute-done((bf16[2,32,4096]{2,1,0:T(8,128)(2,1)S(1)}, bf16[2,32,4096]{2,1,0:T(8,128)(2,1)S(1)}, u32[]{:S(2)}, u32[]{:S(2)}) %collective-permute-start.9) | collective-permute-done | bytes 524320 | tf_op jit(solution)/shard_map/ppermute | solution.py:166
  177.6 1.3 collective-permute-start.18
  179.0 0.9 collective-permute-done.10
  179.9 0.9 collective-permute-start.19
  181.3 1.8 collective-permute-done.19.refs_11_
  183.1 1.1 copy-done.2
  184.1 1.9 copy-done.9
  186.0 25.7 %shard_map.140 = (f32[2,1024,1]{2,1,0:T(8,128)S(1)}, f32[2,1024,1]{2,1,0:T(8,128)S(1)}, f32[2,1024,1]{2,1,0:T(8,128)S(1)}) custom-call(s32[1024,1]{1,0:T(8,128)S(1)} %sub.123.refs_0_, bf16[1024,4096]{1,0:T(8,128)(2,1)} %bitcast.95, bf16[512,2048]{1,0:T(8,128)(2,1)} %refs_2_.1, bf16[512,2048]{1,0:T(8,128)(2,1)} %collective-permute-done.11.refs_3_, ...), custom_call_target="tpu_custom_call" | custom-call | flops 17179869184 | bytes 33554432 | tf_op jit(solution)/shard_map/pallas_call | solution.py:53
  213.6 0.8 reshape.384
  214.5 7.1 %all-to-all-start.1 = ((f32[32,1,768]{2,1,0:T(1,128)}), f32[32,1,768]{2,1,0:T(1,128)S(1)}, u32[]{:S(2)}, u32[]{:S(2)}) async-start(f32[32,1,768]{2,1,0:T(1,128)} %reshape.384), calls=%async_computation.1 | async-start | bytes 196608 | tf_op jit(solution)/shard_map/all_to_all | solution.py:209
  222.2 8.4 %all-to-all-done.1 = f32[32,1,768]{2,1,0:T(1,128)S(1)} async-done(((f32[32,1,768]{2,1,0:T(1,128)}), f32[32,1,768]{2,1,0:T(1,128)S(1)}, u32[]{:S(2)}, u32[]{:S(2)}) %all-to-all-start.1) | async-done | bytes 98336 | tf_op jit(solution)/shard_map/all_to_all | solution.py:209
  231.2 0.9 reduce.48
  232.5 13.6 %psum.7 = f32[4,256]{1,0:T(4,128)S(1)} all-reduce(f32[4,256]{1,0:T(4,128)S(1)} %pad_maximum_fusion.1), channel_id=1, replica_groups=mesh['dp'=32,'mp'=8] {'mp'}, use_global_device_ids=true, to_apply=%region_19.20 | all-reduce | flops 1024 | bytes 8192 | tf_op jit(solution)/shard_map/psum | solution.py:226
  (137 shorter events, 12.9 us)
Async XLA Ops:
  0.6 57.7 %copy-start = (s32[4]{0:T(128)S(1)}, s32[4]{0:T(128)}, u32[]{:S(2)}) copy-start(s32[4]{0:T(128)} %constant.280.clone) | copy-start | bytes 52
  0.6 56.2 %copy-start.1 = (bf16[64,7,512]{2,0,1:T(8,128)(2,1)S(1)}, bf16[64,7,512]{2,0,1:T(8,128)(2,1)}, u32[]{:S(2)}) copy-start(bf16[64,7,512]{2,0,1:T(8,128)(2,1)} %param.17) | copy-start | bytes 1376260
  0.7 80.8 %copy-start.4 = (f32[512]{0:T(512)S(1)}, f32[512]{0:T(512)}, u32[]{:S(2)}) copy-start(f32[512]{0:T(512)} %param.19) | copy-start | bytes 6148
  0.7 80.8 %copy-start.6 = (f32[512]{0:T(512)S(1)}, f32[512]{0:T(512)}, u32[]{:S(2)}) copy-start(f32[512]{0:T(512)} %param.20) | copy-start | bytes 6148
  0.7 80.8 %copy-start.5 = (f32[512]{0:T(512)S(1)}, f32[512]{0:T(512)}, u32[]{:S(2)}) copy-start(f32[512]{0:T(512)} %param.21) | copy-start | bytes 6148
  0.7 115.3 %collective-permute-start.11 = (bf16[512,2048]{1,0:T(8,128)(2,1)}, bf16[512,2048]{1,0:T(8,128)(2,1)}, u32[]{:S(2)}, u32[]{:S(2)}) collective-permute-start(bf16[512,2048]{1,0:T(8,128)(2,1)} %refs_2_.1), channel_id=1, source_target_pairs={{0,2},{1,3},{2,4},{3,5},{4,6},{5,7},{6,0},{7,1},{8,10},{9,11},{10,... | collective-permute-start | bytes 6291464 | tf_op jit(solution)/shard_map/ppermute | solution.py:125
  2.9 115.1 %collective-permute-start.12 = (bf16[512,2048]{1,0:T(8,128)(2,1)}, bf16[512,2048]{1,0:T(8,128)(2,1)}, u32[]{:S(2)}, u32[]{:S(2)}) collective-permute-start(bf16[512,2048]{1,0:T(8,128)(2,1)} %refs_2_.1), channel_id=1, source_target_pairs={{0,6},{1,7},{2,0},{3,1},{4,2},{5,3},{6,4},{7,5},{8,14},{9,15},{10,... | collective-permute-start | bytes 6291464 | tf_op jit(solution)/shard_map/ppermute | solution.py:125
  4.4 176.5 %collective-permute-start.15 = (bf16[512,2048]{1,0:T(8,128)(2,1)}, bf16[512,2048]{1,0:T(8,128)(2,1)}, u32[]{:S(2)}, u32[]{:S(2)}) collective-permute-start(bf16[512,2048]{1,0:T(8,128)(2,1)} %refs_2_.1), channel_id=1, source_target_pairs={{0,1},{1,0},{2,3},{3,2},{4,5},{5,4},{6,7},{7,6},{8,9},{9,8},{10,11... | collective-permute-start | bytes 6291464 | tf_op jit(solution)/shard_map/ppermute | solution.py:136
  12.2 47.5 %all-to-all-start = ((bf16[8,32,512]{2,1,0:T(8,128)(2,1)}), bf16[8,32,512]{2,1,0:T(8,128)(2,1)S(1)}, u32[]{:S(2)}, u32[]{:S(2)}) async-start(bf16[8,32,512]{2,1,0:T(8,128)(2,1)} %bitcast.34), calls=%async_computation | async-start | bytes 524288 | tf_op jit(solution)/shard_map/all_to_all | solution.py:146
  59.7 154.8 %all-to-all-start.2 = ((bf16[32,8,512]{2,1,0:T(8,128)(2,1)}), bf16[32,8,512]{2,1,0:T(8,128)(2,1)S(1)}, u32[]{:S(2)}, u32[]{:S(2)}) async-start(bf16[32,8,512]{2,1,0:T(8,128)(2,1)} %fusion), calls=%async_computation.2 | async-start | bytes 524288 | tf_op jit(solution)/shard_map/all_to_all | solution.py:117
  69.4 11.5 %collective-permute-start = (bf16[32,4096]{1,0:T(8,128)(2,1)S(1)}, bf16[32,4096]{1,0:T(8,128)(2,1)S(1)}, u32[]{:S(2)}, u32[]{:S(2)}) collective-permute-start(bf16[32,4096]{1,0:T(8,128)(2,1)S(1)} %bitcast.91), channel_id=1, source_target_pairs={{0,8},{8,16},{16,24},{24,0},{32,40},{40,48},{48,56},{56,32},{64,72... | collective-permute-start | bytes 786440 | tf_op jit(solution)/shard_map/ppermute | solution.py:152
  71.0 10.6 %collective-permute-start.1 = (bf16[32,4096]{1,0:T(8,128)(2,1)S(1)}, bf16[32,4096]{1,0:T(8,128)(2,1)S(1)}, u32[]{:S(2)}, u32[]{:S(2)}) collective-permute-start(bf16[32,4096]{1,0:T(8,128)(2,1)S(1)} %bitcast.92), channel_id=1, source_target_pairs={{0,24},{8,0},{16,8},{24,16},{32,56},{40,32},{48,40},{56,48},{64,88... | collective-permute-start | bytes 786440 | tf_op jit(solution)/shard_map/ppermute | solution.py:153
  80.9 8.0 %collective-permute-start.2 = (bf16[32,4096]{1,0:T(8,128)(2,1)S(1)}, bf16[32,4096]{1,0:T(8,128)(2,1)S(1)}, u32[]{:S(2)}, u32[]{:S(2)}) collective-permute-start(bf16[32,4096]{1,0:T(8,128)(2,1)S(1)} %collective-permute-done), channel_id=1, source_target_pairs={{0,8},{8,16},{16,24},{24,0},{32,40},{40,48},{48,56},{56,32},{64,72... | collective-permute-start | bytes 786440 | tf_op jit(solution)/shard_map/ppermute | solution.py:154
  89.0 24.2 %collective-permute-start.3 = (bf16[4,32,4096]{2,1,0:T(8,128)(2,1)S(1)}, bf16[4,32,4096]{2,1,0:T(8,128)(2,1)S(1)}, u32[]{:S(2)}, u32[]{:S(2)}) collective-permute-start(bf16[4,32,4096]{2,1,0:T(8,128)(2,1)S(1)} %pad_maximum_fusion), channel_id=1, source_target_pairs={{0,32},{8,40},{16,48},{24,56},{32,64},{40,72},{48,80},{56,88},{64,... | collective-permute-start | bytes 3145736 | tf_op jit(solution)/shard_map/ppermute | solution.py:161
  90.4 22.8 %collective-permute-start.4 = (bf16[4,32,4096]{2,1,0:T(8,128)(2,1)S(1)}, bf16[4,32,4096]{2,1,0:T(8,128)(2,1)S(1)}, u32[]{:S(2)}, u32[]{:S(2)}) collective-permute-start(bf16[4,32,4096]{2,1,0:T(8,128)(2,1)S(1)} %pad_maximum_fusion), channel_id=1, source_target_pairs={{0,224},{8,232},{16,240},{24,248},{32,0},{40,8},{48,16},{56,24},{6... | collective-permute-start | bytes 3145736 | tf_op jit(solution)/shard_map/ppermute | solution.py:162
  113.2 23.1 %collective-permute-start.5 = (bf16[4,32,4096]{2,1,0:T(8,128)(2,1)S(1)}, bf16[4,32,4096]{2,1,0:T(8,128)(2,1)S(1)}, u32[]{:S(2)}, u32[]{:S(2)}) collective-permute-start(bf16[4,32,4096]{2,1,0:T(8,128)(2,1)S(1)} %collective-permute-done.3), channel_id=1, source_target_pairs={{0,32},{8,40},{16,48},{24,56},{32,64},{40,72},{48,80},{56,88},{64,... | collective-permute-start | bytes 3145736 | tf_op jit(solution)/shard_map/ppermute | solution.py:161
  113.3 23.1 %collective-permute-start.6 = (bf16[4,32,4096]{2,1,0:T(8,128)(2,1)S(1)}, bf16[4,32,4096]{2,1,0:T(8,128)(2,1)S(1)}, u32[]{:S(2)}, u32[]{:S(2)}) collective-permute-start(bf16[4,32,4096]{2,1,0:T(8,128)(2,1)S(1)} %collective-permute-done.4), channel_id=1, source_target_pairs={{0,224},{8,232},{16,240},{24,248},{32,0},{40,8},{48,16},{56,24},{6... | collective-permute-start | bytes 3145736 | tf_op jit(solution)/shard_map/ppermute | solution.py:162
  117.3 46.0 %collective-permute-start.13 = (bf16[256,2048]{1,0:T(8,128)(2,1)S(1)}, bf16[256,2048]{1,0:T(8,128)(2,1)S(1)}, u32[]{:S(2)}, u32[]{:S(2)}) collective-permute-start(bf16[256,2048]{1,0:T(8,128)(2,1)S(1)} %slice.101), channel_id=1, source_target_pairs={{0,2},{1,3},{2,4},{3,5},{4,6},{5,7},{6,0},{7,1},{8,10},{9,11},{10,... | collective-permute-start | bytes 3145736 | tf_op jit(solution)/shard_map/ppermute | solution.py:125
  119.3 45.9 %collective-permute-start.14 = (bf16[256,2048]{1,0:T(8,128)(2,1)S(1)}, bf16[256,2048]{1,0:T(8,128)(2,1)S(1)}, u32[]{:S(2)}, u32[]{:S(2)}) collective-permute-start(bf16[256,2048]{1,0:T(8,128)(2,1)S(1)} %slice.102), channel_id=1, source_target_pairs={{0,6},{1,7},{2,0},{3,1},{4,2},{5,3},{6,4},{7,5},{8,14},{9,15},{10,... | collective-permute-start | bytes 3145736 | tf_op jit(solution)/shard_map/ppermute | solution.py:125
  136.4 22.3 %collective-permute-start.7 = (bf16[4,32,4096]{2,1,0:T(8,128)(2,1)S(1)}, bf16[4,32,4096]{2,1,0:T(8,128)(2,1)S(1)}, u32[]{:S(2)}, u32[]{:S(2)}) collective-permute-start(bf16[4,32,4096]{2,1,0:T(8,128)(2,1)S(1)} %collective-permute-done.5), channel_id=1, source_target_pairs={{0,32},{8,40},{16,48},{24,56},{32,64},{40,72},{48,80},{56,88},{64,... | collective-permute-start | bytes 3145736 | tf_op jit(solution)/shard_map/ppermute | solution.py:161
  136.4 26.8 %collective-permute-start.8 = (bf16[4,32,4096]{2,1,0:T(8,128)(2,1)S(1)}, bf16[4,32,4096]{2,1,0:T(8,128)(2,1)S(1)}, u32[]{:S(2)}, u32[]{:S(2)}) collective-permute-start(bf16[4,32,4096]{2,1,0:T(8,128)(2,1)S(1)} %collective-permute-done.6), channel_id=1, source_target_pairs={{0,224},{8,232},{16,240},{24,248},{32,0},{40,8},{48,16},{56,24},{6... | collective-permute-start | bytes 3145736 | tf_op jit(solution)/shard_map/ppermute | solution.py:162
  158.6 24.4 %collective-permute-start.16 = (bf16[512,2048]{1,0:T(8,128)(2,1)}, bf16[512,2048]{1,0:T(8,128)(2,1)S(1)}, u32[]{:S(2)}, u32[]{:S(2)}) collective-permute-start(bf16[512,2048]{1,0:T(8,128)(2,1)} %collective-permute-done.11.refs_3_), channel_id=1, source_target_pairs={{0,1},{1,0},{2,3},{3,2},{4,5},{5,4},{6,7},{7,6},{8,9},{9,8},{10,11... | collective-permute-start | bytes 6291464 | tf_op jit(solution)/shard_map/ppermute | solution.py:136
  163.2 19.9 %collective-permute-start.17 = (bf16[512,2048]{1,0:T(8,128)(2,1)}, bf16[512,2048]{1,0:T(8,128)(2,1)S(1)}, u32[]{:S(2)}, u32[]{:S(2)}) collective-permute-start(bf16[512,2048]{1,0:T(8,128)(2,1)} %collective-permute-done.12.refs_4_), channel_id=1, source_target_pairs={{0,1},{1,0},{2,3},{3,2},{4,5},{5,4},{6,7},{7,6},{8,9},{9,8},{10,11... | collective-permute-start | bytes 6291464 | tf_op jit(solution)/shard_map/ppermute | solution.py:136
  163.4 14.3 %collective-permute-start.9 = (bf16[2,32,4096]{2,1,0:T(8,128)(2,1)S(1)}, bf16[2,32,4096]{2,1,0:T(8,128)(2,1)S(1)}, u32[]{:S(2)}, u32[]{:S(2)}) collective-permute-start(bf16[2,32,4096]{2,1,0:T(8,128)(2,1)S(1)} %slice.99), channel_id=1, source_target_pairs={{0,32},{8,40},{16,48},{24,56},{32,64},{40,72},{48,80},{56,88},{64,... | collective-permute-start | bytes 1572872 | tf_op jit(solution)/shard_map/ppermute | solution.py:166
  165.2 14.7 %collective-permute-start.10 = (bf16[2,32,4096]{2,1,0:T(8,128)(2,1)S(1)}, bf16[2,32,4096]{2,1,0:T(8,128)(2,1)S(1)}, u32[]{:S(2)}, u32[]{:S(2)}) collective-permute-start(bf16[2,32,4096]{2,1,0:T(8,128)(2,1)S(1)} %slice.100), channel_id=1, source_target_pairs={{0,224},{8,232},{16,240},{24,248},{32,0},{40,8},{48,16},{56,24},{6... | collective-permute-start | bytes 1572872 | tf_op jit(solution)/shard_map/ppermute | solution.py:167
  177.6 3.6 %collective-permute-start.18 = (bf16[256,2048]{1,0:T(8,128)(2,1)S(1)}, bf16[256,2048]{1,0:T(8,128)(2,1)S(1)}, u32[]{:S(2)}, u32[]{:S(2)}) collective-permute-start(bf16[256,2048]{1,0:T(8,128)(2,1)S(1)} %collective-permute-done.13.refs_5_), channel_id=1, source_target_pairs={{0,1},{1,0},{2,3},{3,2},{4,5},{5,4},{6,7},{7,6},{8,9},{9,8},{10,11... | collective-permute-start | bytes 3145736 | tf_op jit(solution)/shard_map/ppermute | solution.py:136
  179.9 3.1 %collective-permute-start.19 = (bf16[256,2048]{1,0:T(8,128)(2,1)S(1)}, bf16[256,2048]{1,0:T(8,128)(2,1)S(1)}, u32[]{:S(2)}, u32[]{:S(2)}) collective-permute-start(bf16[256,2048]{1,0:T(8,128)(2,1)S(1)} %collective-permute-done.14.refs_6_), channel_id=1, source_target_pairs={{0,1},{1,0},{2,3},{3,2},{4,5},{5,4},{6,7},{7,6},{8,9},{9,8},{10,11... | collective-permute-start | bytes 3145736 | tf_op jit(solution)/shard_map/ppermute | solution.py:136
  180.9 3.2 %copy-start.2 = (bf16[32,32,4096]{2,1,0:T(8,128)(2,1)}, bf16[32,32,4096]{2,1,0:T(8,128)(2,1)S(1)}, u32[]{:S(2)}) copy-start(bf16[32,32,4096]{2,1,0:T(8,128)(2,1)S(1)} %constant_dynamic-update-slice_fusion) | copy-start | bytes 25165828
  181.3 4.8 %copy-start.10 = (bf16[256,2048]{1,0:T(8,128)(2,1)}, bf16[256,2048]{1,0:T(8,128)(2,1)S(1)}, u32[]{:S(2)}) copy-start(bf16[256,2048]{1,0:T(8,128)(2,1)S(1)} %collective-permute-done.18.refs_10_) | copy-start | bytes 3145732
  183.0 3.0 %copy-start.11 = (bf16[256,2048]{1,0:T(8,128)(2,1)}, bf16[256,2048]{1,0:T(8,128)(2,1)S(1)}, u32[]{:S(2)}) copy-start(bf16[256,2048]{1,0:T(8,128)(2,1)S(1)} %collective-permute-done.19.refs_11_) | copy-start | bytes 3145732
  183.1 3.0 %copy-start.8 = (bf16[512,2048]{1,0:T(8,128)(2,1)}, bf16[512,2048]{1,0:T(8,128)(2,1)S(1)}, u32[]{:S(2)}) copy-start(bf16[512,2048]{1,0:T(8,128)(2,1)S(1)} %collective-permute-done.16.refs_8_) | copy-start | bytes 6291460
  184.1 1.9 copy-start.9
  186.0 60.2 %copy-start.7 = (f32[256]{0:T(256)S(1)}, f32[256]{0:T(256)}, u32[]{:S(2)}) copy-start(f32[256]{0:T(256)} %param.22) | copy-start | bytes 3076
  214.5 16.2 %all-to-all-start.1 = ((f32[32,1,768]{2,1,0:T(1,128)}), f32[32,1,768]{2,1,0:T(1,128)S(1)}, u32[]{:S(2)}, u32[]{:S(2)}) async-start(f32[32,1,768]{2,1,0:T(1,128)} %reshape.384), calls=%async_computation.1 | async-start | bytes 196608 | tf_op jit(solution)/shard_map/all_to_all | solution.py:209
  246.1 1.2 copy-start.3

commit v8 on v4

--- a/solution.py
+++ b/solution.py
@@ -19,17 +19,18 @@
     return jnp.sum(jnp.logical_and(same, earlier).astype(jnp.int32), axis=-1)
 
 
-def stats_kernel(pieces, tile_n, target_ref, rows_ref, *refs):
+def stats_kernel(heights, tile_n, target_ref, rows_ref, *refs):
+    pieces = len(heights)
     weight_refs = refs[:pieces]
     max_ref, total_ref, target_logit_ref = refs[pieces:]
-    width = weight_refs[0].shape[0]
-    logits = jnp.dot(rows_ref[:, 0:width], weight_refs[0][...], preferred_element_type=jnp.float32)
-    for k in range(1, pieces):
-        logits = logits + jnp.dot(
-            rows_ref[:, k * width : (k + 1) * width],
-            weight_refs[k][...],
-            preferred_element_type=jnp.float32,
+    logits = None
+    offset = 0
+    for k, height in enumerate(heights):
+        part = jnp.dot(
+            rows_ref[:, offset : offset + height], weight_refs[k][...], preferred_element_type=jnp.float32
         )
+        logits = part if logits is None else logits + part
+        offset += height
     row_max = jnp.max(logits, axis=1, keepdims=True)
     total = jnp.sum(jnp.exp(logits - row_max), axis=1, keepdims=True)
     column = lax.broadcasted_iota(jnp.int32, logits.shape, 1) + pl.program_id(0) * tile_n
@@ -41,18 +42,19 @@
 
 def logit_stats(rows, pieces, local_target, tile_m=256, tile_n=1024):
     count, width_full = rows.shape
-    width, vocab = pieces[0].shape
+    vocab = pieces[0].shape[1]
+    heights = tuple(piece.shape[0] for piece in pieces)
     grid = (vocab // tile_n, count // tile_m)
     stat_shape = jax.ShapeDtypeStruct((grid[0], count, 1), jnp.float32)
     stat_spec = pl.BlockSpec((1, tile_m, 1), lambda j, i: (j, i, 0))
     return pl.pallas_call(
-        lambda *refs: stats_kernel(len(pieces), tile_n, *refs),
+        lambda *refs: stats_kernel(heights, tile_n, *refs),
         grid=grid,
         in_specs=[
             pl.BlockSpec((tile_m, 1), lambda j, i: (i, 0)),
             pl.BlockSpec((tile_m, width_full), lambda j, i: (i, 0)),
         ]
-        + [pl.BlockSpec((width, tile_n), lambda j, i: (0, j)) for _ in pieces],
+        + [pl.BlockSpec((height, tile_n), lambda j, i: (0, j)) for height in heights],
         out_specs=[stat_spec, stat_spec, stat_spec],
         out_shape=[stat_shape, stat_shape, stat_shape],
         compiler_params=pltpu.CompilerParams(vmem_limit_bytes=48 * 1024 * 1024),
@@ -105,14 +107,25 @@
     ).reshape(slot_dev, width_dev)
 
     chips = ways // 2
-    own_core = [head_weight] + [
-        lax.ppermute(head_weight, "mp", [(i, (i + 2 * shift) % ways) for i in range(ways)])
-        for shift in range(1, chips)
+    half = width_dev // 2
+
+    def along_y(x, shift):
+        return lax.ppermute(x, "mp", [(i, ((i // 2 + shift) % chips) * 2 + i % 2) for i in range(ways)])
+
+    from_prev = along_y(head_weight, 1)
+    from_next = along_y(head_weight, -1)
+    own_core = [
+        head_weight,
+        from_prev,
+        from_next,
+        along_y(from_prev[:half], 1),
+        along_y(from_next[half:], -1),
     ]
     mate_core = [lax.ppermute(block, "mp", [(i, i ^ 1) for i in range(ways)]) for block in own_core]
     chip, core = part // 2, part % 2
     order = jnp.arange(ways, dtype=jnp.int32)
-    source_chip = (chip - order % chips) % chips
+    chip_step = jnp.array([0, -1, 1, -2], jnp.int32)
+    source_chip = (chip + chip_step[order % chips]) % chips
     source_core = jnp.where(order < chips, core, 1 - core)
     pick = (
         (source_chip * 2 + source_core)[:, None] == jnp.arange(ways, dtype=jnp.int32)[None, :]

time: 205 us -> 197 us (0.961)
  starting transfers between devices: 78.7 us -> 35.3 us
  waiting for transfers between devices: 51.3 us -> 78.3 us
  local copies, waits for them, and re-layouts: 10.8 us -> 18.7 us
    ppermute x4 -> x5, starting transfers between devices: 48.4 us -> 7.58 us  [body(): lax.ppermute(block, 'mp', [(i, i ^ 1) for i in range(ways)])]
    all_gather x1, waiting for transfers between devices: 0.01 us -> 18.7 us  [body(): block_rows = lax.all_gather(own_rows, 'dp', axis=0, tiled=True)]
    ppermute x3 -> x4, waiting for transfers between devices: 31.3 us -> 44.6 us  [along_y(): lax.ppermute(x, 'mp', [(i, (i // 2 + shift) % chips * 2 + i % 2) for i in...]
    all_to_all x1, starting transfers between devices: 10.5 us -> 5.35 us  [body(): routed = lax.all_to_all(routed, 'dp', 0, 0, tiled=True)]
    slice x0 -> x2, local copies, waits for them, and re-layouts: none -> 4.64 us  [the longest x1 2.32 us: body(): from_prev[:half]]
    ppermute x4 -> x5, waiting for transfers between devices: 5.15 us -> 0.75 us  [body(): lax.ppermute(block, 'mp', [(i, i ^ 1) for i in range(ways)])]
    unnamed x34, local copies, waits for them, and re-layouts: 5.48 us -> 8.15 us
    ppermute x3 -> x4, starting transfers between devices: 2.87 us -> 5.43 us  [along_y(): lax.ppermute(x, 'mp', [(i, (i // 2 + shift) % chips * 2 + i % 2) for i in...]
  transfers between devices with their start and end apart: 11 -> 13, of which waited for: 5 -> 6; matrix products, arithmetic and copies ran while one was open for 5% -> 7% of each run, Pallas kernels for 13% -> 13%
where the time goes in v8:
time: 197 us; the launch traced here: 196 us
  waiting for transfers between devices  78.3 us (40%)
  starting transfers between devices  35.3 us (18%)
  Pallas kernels  25.6 us (13%)
  local copies, waits for them, and re-layouts  18.7 us (9%)
  blocking collectives  14.6 us (7%)
  between operations  14.5 us (7%)
  other arithmetic  6.7 us (3%)
  matrix products  2.32 us (1%)
    ppermute x4, waiting for transfers between devices, along_y(): lax.ppermute(x, 'mp', [(i, (i // 2 + shift) % chips * 2 + i % 2) for i in...  44.6 us
    pallas_call x1, Pallas kernels, logit_stats(): pl.pallas_call(lambda *refs: stats_kernel(heights, tile_n, *refs), grid=g...  25.6 us
    all_gather x1, waiting for transfers between devices, body(): block_rows = lax.all_gather(own_rows, 'dp', axis=0, tiled=True)  18.7 us
    psum x1, blocking collectives, body(): lax.psum(jnp.concatenate([block_logprob[None], sums]), 'mp')  14.6 us
    all_to_all x1, starting transfers between devices, body(): lax.all_to_all(reward_send.reshape(shards, pair_len, width_dev), 'dp', 0,...  10.5 us
    all_to_all x1, waiting for transfers between devices, body(): routed = lax.all_to_all(routed, 'dp', 0, 0, tiled=True)  8.44 us
    unnamed x34, local copies, waits for them, and re-layouts  8.15 us
    ppermute x5, starting transfers between devices, body(): lax.ppermute(block, 'mp', [(i, i ^ 1) for i in range(ways)])  7.58 us
  transfers between devices with their start and end apart: 13, of which 6 were waited for; matrix products, arithmetic and copies ran while one was open for 7% of the time, Pallas kernels for 13%

profile of v8, /device:TPU:1, one launch (start us, length us, event | category | flops | bytes accessed | tf_op | source)
XLA Modules:
  0.0 196.1 jit_solution(12099852923305939104)
XLA Ops:
  7.2 0.8 broadcast_multiply_fusion.1
  8.1 0.8 subtract_multiply_fusion.1
  9.7 1.3 copy.78
  11.2 1.0 convolution_convert_fusion.2
  12.2 6.5 %all-to-all-start = ((bf16[8,32,512]{2,1,0:T(8,128)(2,1)}), bf16[8,32,512]{2,1,0:T(8,128)(2,1)S(1)}, u32[]{:S(2)}, u32[]{:S(2)}) async-start(bf16[8,32,512]{2,1,0:T(8,128)(2,1)} %bitcast.2), calls=%async_computation | async-start | bytes 524288 | tf_op jit(solution)/shard_map/all_to_all | solution.py:134
  18.7 0.6 gather_fusion
  19.4 5.8 %all-to-all-done = bf16[8,32,512]{2,1,0:T(8,128)(2,1)S(1)} async-done(((bf16[8,32,512]{2,1,0:T(8,128)(2,1)}), bf16[8,32,512]{2,1,0:T(8,128)(2,1)S(1)}, u32[]{:S(2)}, u32[]{:S(2)}) %all-to-all-start) | async-done | bytes 262176 | tf_op jit(solution)/shard_map/all_to_all | solution.py:134
  25.2 0.3 convolution_convert_fusion.1
  25.5 0.8 copy.88
  26.3 0.4 collective-permute-start
  26.7 2.4 %collective-permute-start.1 = (bf16[512,2048]{1,0:T(8,128)(2,1)}, bf16[512,2048]{1,0:T(8,128)(2,1)}, u32[]{:S(2)}, u32[]{:S(2)}) collective-permute-start(bf16[512,2048]{1,0:T(8,128)(2,1)} %refs_2_.1), channel_id=1, source_target_pairs={{0,6},{1,7},{2,0},{3,1},{4,2},{5,3},{6,4},{7,5},{8,14},{9,15},{10,... | collective-permute-start | bytes 6291464 | tf_op jit(solution)/shard_map/ppermute | solution.py:113
  29.1 1.6 collective-permute-start.4
  30.7 0.3 copy.86
  31.1 1.0 fusion
  32.1 10.5 %all-to-all-start.2 = ((bf16[32,8,512]{2,1,0:T(8,128)(2,1)}), bf16[32,8,512]{2,1,0:T(8,128)(2,1)S(1)}, u32[]{:S(2)}, u32[]{:S(2)}) async-start(bf16[32,8,512]{2,1,0:T(8,128)(2,1)} %fusion), calls=%async_computation.2 | async-start | bytes 524288 | tf_op jit(solution)/shard_map/all_to_all | solution.py:105
  42.7 31.4 %collective-permute-done.refs_3_ = bf16[512,2048]{1,0:T(8,128)(2,1)} collective-permute-done((bf16[512,2048]{1,0:T(8,128)(2,1)}, bf16[512,2048]{1,0:T(8,128)(2,1)}, u32[]{:S(2)}, u32[]{:S(2)}) %collective-permute-start) | collective-permute-done | bytes 2097184 | tf_op jit(solution)/shard_map/ppermute | solution.py:113
  74.1 2.3 %slice.91 = bf16[256,2048]{1,0:T(8,128)(2,1)} slice(bf16[512,2048]{1,0:T(8,128)(2,1)} %collective-permute-done.refs_3_), slice={[0:256], [0:2048]} | slice | bytes 2097152 | tf_op jit(solution)/shard_map/slice | solution.py:121
  76.4 2.3 %slice.92 = bf16[256,2048]{1,0:T(8,128)(2,1)} slice(bf16[512,2048]{1,0:T(8,128)(2,1)} %collective-permute-done.1.refs_4_), slice={[256:512], [0:2048]} | slice | bytes 2097152 | tf_op jit(solution)/shard_map/slice | solution.py:122
  78.7 2.7 %collective-permute-start.3 = (bf16[256,2048]{1,0:T(8,128)(2,1)}, bf16[256,2048]{1,0:T(8,128)(2,1)S(1)}, u32[]{:S(2)}, u32[]{:S(2)}) collective-permute-start(bf16[256,2048]{1,0:T(8,128)(2,1)} %slice.92), channel_id=1, source_target_pairs={{0,6},{1,7},{2,0},{3,1},{4,2},{5,3},{6,4},{7,5},{8,14},{9,15},{10,... | collective-permute-start | bytes 3145736 | tf_op jit(solution)/shard_map/ppermute | solution.py:113
  81.5 0.2 reduce_window_sum.11
  81.8 2.5 %collective-permute-start.5 = (bf16[512,2048]{1,0:T(8,128)(2,1)}, bf16[512,2048]{1,0:T(8,128)(2,1)}, u32[]{:S(2)}, u32[]{:S(2)}) collective-permute-start(bf16[512,2048]{1,0:T(8,128)(2,1)} %collective-permute-done.refs_3_), channel_id=1, source_target_pairs={{0,1},{1,0},{2,3},{3,2},{4,5},{5,4},{6,7},{7,6},{8,9},{9,8},{10,11... | collective-permute-start | bytes 6291464 | tf_op jit(solution)/shard_map/ppermute | solution.py:124
  84.4 0.9 convert_reduce_fusion
  86.1 0.4 copy.77
  86.4 0.5 broadcast_in_dim.106
  86.9 0.6 select_reduce_fusion
  87.5 13.2 %collective-permute-done.2.refs_5_ = bf16[256,2048]{1,0:T(8,128)(2,1)S(1)} collective-permute-done((bf16[256,2048]{1,0:T(8,128)(2,1)}, bf16[256,2048]{1,0:T(8,128)(2,1)S(1)}, u32[]{:S(2)}, u32[]{:S(2)}) %collective-permute-start.2) | collective-permute-done | bytes 1048608 | tf_op jit(solution)/shard_map/ppermute | solution.py:113
  100.7 2.6 %collective-permute-start.7 = (bf16[256,2048]{1,0:T(8,128)(2,1)S(1)}, bf16[256,2048]{1,0:T(8,128)(2,1)}, u32[]{:S(2)}, u32[]{:S(2)}) collective-permute-start(bf16[256,2048]{1,0:T(8,128)(2,1)S(1)} %collective-permute-done.2.refs_5_), channel_id=1, source_target_pairs={{0,1},{1,0},{2,3},{3,2},{4,5},{5,4},{6,7},{7,6},{8,9},{9,8},{10,11... | collective-permute-start | bytes 3145736 | tf_op jit(solution)/shard_map/ppermute | solution.py:124
  103.4 1.0 copy-done
  104.4 0.7 collective-permute-start.8
  105.1 1.0 copy-done.2
  106.1 0.5 sub.123.refs_0_
  106.7 0.7 collective-permute-done.8.refs_11_
  107.5 18.7 %all-gather.2.cloned.1.call-done.refs_1_ = bf16[1024,4096]{1,0:T(8,128)(2,1)} async-done(((bf16[32,4096]{1,0:T(8,128)(2,1)}), bf16[1024,4096]{1,0:T(8,128)(2,1)}) %all-gather.2.cloned.1.call-update) | async-done | bytes 8388624 | tf_op jit(solution)/shard_map/all_gather | solution.py:138
  126.2 1.2 copy-done.1
  127.4 1.2 copy-done.3
  128.7 25.6 %shard_map.122 = (f32[2,1024,1]{2,1,0:T(8,128)S(1)}, f32[2,1024,1]{2,1,0:T(8,128)S(1)}, f32[2,1024,1]{2,1,0:T(8,128)S(1)}) custom-call(s32[1024,1]{1,0:T(8,128)S(1)} %sub.123.refs_0_, bf16[1024,4096]{1,0:T(8,128)(2,1)} %all-gather.2.cloned.1.call-done.refs_1_, bf16[512,2048]{1,0:T(8,128)(2,1)} %refs_2_.1, bf16[512,2048]{1,0:T(8,128)(2,1)} %collective-permute-done.refs_3_, ...), custom_call_target="tpu_custom_call" | custom-call | flops 17179869184 | bytes 33554432 | tf_op jit(solution)/shard_map/pallas_call | solution.py:50
  154.3 0.5 fusion.23
  154.9 0.3 reduce.7
  155.6 0.2 reduce_sum.112
  156.0 0.3 select_reduce_fusion.1
  156.3 0.8 reshape.337
  157.1 5.4 %all-to-all-start.1 = ((f32[32,1,768]{2,1,0:T(1,128)}), f32[32,1,768]{2,1,0:T(1,128)S(1)}, u32[]{:S(2)}, u32[]{:S(2)}) async-start(f32[32,1,768]{2,1,0:T(1,128)} %reshape.337), calls=%async_computation.1 | async-start | bytes 196608 | tf_op jit(solution)/shard_map/all_to_all | solution.py:169
  162.7 0.2 fusion.1
  163.1 8.4 %all-to-all-done.1 = f32[32,1,768]{2,1,0:T(1,128)S(1)} async-done(((f32[32,1,768]{2,1,0:T(1,128)}), f32[32,1,768]{2,1,0:T(1,128)S(1)}, u32[]{:S(2)}, u32[]{:S(2)}) %all-to-all-start.1) | async-done | bytes 98336 | tf_op jit(solution)/shard_map/all_to_all | solution.py:169
  171.6 0.5 broadcast.341
  172.1 0.9 reduce.10
  173.5 14.6 %psum.7 = f32[4,256]{1,0:T(4,128)S(1)} all-reduce(f32[4,256]{1,0:T(4,128)S(1)} %pad_maximum_fusion), channel_id=1, replica_groups=mesh['dp'=32,'mp'=8] {'mp'}, use_global_device_ids=true, to_apply=%region_13.14 | all-reduce | flops 1024 | bytes 8192 | tf_op jit(solution)/shard_map/psum | solution.py:186
  188.6 0.7 reshape.325
  (100 shorter events, 4.4 us)
Async XLA Ops:
  7.2 11.6 %copy-start.4 = (s32[4]{0:T(128)S(1)}, s32[4]{0:T(128)}, u32[]{:S(2)}) copy-start(s32[4]{0:T(128)} %constant.105.clone) | copy-start | bytes 52
  11.0 19.7 %copy-start.5 = (bf16[64,7,512]{2,0,1:T(8,128)(2,1)S(1)}, bf16[64,7,512]{2,0,1:T(8,128)(2,1)}, u32[]{:S(2)}) copy-start(bf16[64,7,512]{2,0,1:T(8,128)(2,1)} %param.15) | copy-start | bytes 1376260
  12.2 13.0 %all-to-all-start = ((bf16[8,32,512]{2,1,0:T(8,128)(2,1)}), bf16[8,32,512]{2,1,0:T(8,128)(2,1)S(1)}, u32[]{:S(2)}, u32[]{:S(2)}) async-start(bf16[8,32,512]{2,1,0:T(8,128)(2,1)} %bitcast.2), calls=%async_computation | async-start | bytes 524288 | tf_op jit(solution)/shard_map/all_to_all | solution.py:134
  18.7 107.5 %all-gather.2.cloned.1.call-start = ((), (), s32[]{:S(2)}) async-start(), calls=%async_computation.3 | async-start | bytes 8650752 | tf_op jit(solution)/shard_map/all_gather | solution.py:138
  25.5 17.1 %copy-start.7 = (s32[2048]{0:T(1024)S(1)}, s32[2048]{0:T(1024)}, u32[]{:S(2)}) copy-start(s32[2048]{0:T(1024)} %param.13) | copy-start | bytes 24580
  26.3 47.8 %collective-permute-start = (bf16[512,2048]{1,0:T(8,128)(2,1)}, bf16[512,2048]{1,0:T(8,128)(2,1)}, u32[]{:S(2)}, u32[]{:S(2)}) collective-permute-start(bf16[512,2048]{1,0:T(8,128)(2,1)} %refs_2_.1), channel_id=1, source_target_pairs={{0,2},{1,3},{2,4},{3,5},{4,6},{5,7},{6,0},{7,1},{8,10},{9,11},{10,... | collective-permute-start | bytes 6291464 | tf_op jit(solution)/shard_map/ppermute | solution.py:113
  26.7 49.7 %collective-permute-start.1 = (bf16[512,2048]{1,0:T(8,128)(2,1)}, bf16[512,2048]{1,0:T(8,128)(2,1)}, u32[]{:S(2)}, u32[]{:S(2)}) collective-permute-start(bf16[512,2048]{1,0:T(8,128)(2,1)} %refs_2_.1), channel_id=1, source_target_pairs={{0,6},{1,7},{2,0},{3,1},{4,2},{5,3},{6,4},{7,5},{8,14},{9,15},{10,... | collective-permute-start | bytes 6291464 | tf_op jit(solution)/shard_map/ppermute | solution.py:113
  29.1 77.7 %collective-permute-start.4 = (bf16[512,2048]{1,0:T(8,128)(2,1)}, bf16[512,2048]{1,0:T(8,128)(2,1)}, u32[]{:S(2)}, u32[]{:S(2)}) collective-permute-start(bf16[512,2048]{1,0:T(8,128)(2,1)} %refs_2_.1), channel_id=1, source_target_pairs={{0,1},{1,0},{2,3},{3,2},{4,5},{5,4},{6,7},{7,6},{8,9},{9,8},{10,11... | collective-permute-start | bytes 6291464 | tf_op jit(solution)/shard_map/ppermute | solution.py:124
  32.1 125.0 %all-to-all-start.2 = ((bf16[32,8,512]{2,1,0:T(8,128)(2,1)}), bf16[32,8,512]{2,1,0:T(8,128)(2,1)S(1)}, u32[]{:S(2)}, u32[]{:S(2)}) async-start(bf16[32,8,512]{2,1,0:T(8,128)(2,1)} %fusion), calls=%async_computation.2 | async-start | bytes 524288 | tf_op jit(solution)/shard_map/all_to_all | solution.py:105
  42.7 38.7 %copy-start.8 = (s32[2048]{0:T(1024)S(1)}, s32[2048]{0:T(1024)}, u32[]{:S(2)}) copy-start(s32[2048]{0:T(1024)} %param.12) | copy-start | bytes 24580
  76.4 24.3 %collective-permute-start.2 = (bf16[256,2048]{1,0:T(8,128)(2,1)}, bf16[256,2048]{1,0:T(8,128)(2,1)S(1)}, u32[]{:S(2)}, u32[]{:S(2)}) collective-permute-start(bf16[256,2048]{1,0:T(8,128)(2,1)} %slice.91), channel_id=1, source_target_pairs={{0,2},{1,3},{2,4},{3,5},{4,6},{5,7},{6,0},{7,1},{8,10},{9,11},{10,... | collective-permute-start | bytes 3145736 | tf_op jit(solution)/shard_map/ppermute | solution.py:113
  78.7 7.4 %copy-start.6 = (s32[2048,7]{0,1:T(8,128)S(1)}, s32[2048,7]{0,1:T(8,128)}, u32[]{:S(2)}) copy-start(s32[2048,7]{0,1:T(8,128)} %param.11) | copy-start | bytes 172036
  78.7 25.6 %collective-permute-start.3 = (bf16[256,2048]{1,0:T(8,128)(2,1)}, bf16[256,2048]{1,0:T(8,128)(2,1)S(1)}, u32[]{:S(2)}, u32[]{:S(2)}) collective-permute-start(bf16[256,2048]{1,0:T(8,128)(2,1)} %slice.92), channel_id=1, source_target_pairs={{0,6},{1,7},{2,0},{3,1},{4,2},{5,3},{6,4},{7,5},{8,14},{9,15},{10,... | collective-permute-start | bytes 3145736 | tf_op jit(solution)/shard_map/ppermute | solution.py:113
  81.8 25.7 %collective-permute-start.5 = (bf16[512,2048]{1,0:T(8,128)(2,1)}, bf16[512,2048]{1,0:T(8,128)(2,1)}, u32[]{:S(2)}, u32[]{:S(2)}) collective-permute-start(bf16[512,2048]{1,0:T(8,128)(2,1)} %collective-permute-done.refs_3_), channel_id=1, source_target_pairs={{0,1},{1,0},{2,3},{3,2},{4,5},{5,4},{6,7},{7,6},{8,9},{9,8},{10,11... | collective-permute-start | bytes 6291464 | tf_op jit(solution)/shard_map/ppermute | solution.py:124
  84.3 23.2 %collective-permute-start.6 = (bf16[512,2048]{1,0:T(8,128)(2,1)}, bf16[512,2048]{1,0:T(8,128)(2,1)}, u32[]{:S(2)}, u32[]{:S(2)}) collective-permute-start(bf16[512,2048]{1,0:T(8,128)(2,1)} %collective-permute-done.1.refs_4_), channel_id=1, source_target_pairs={{0,1},{1,0},{2,3},{3,2},{4,5},{5,4},{6,7},{7,6},{8,9},{9,8},{10,11... | collective-permute-start | bytes 6291464 | tf_op jit(solution)/shard_map/ppermute | solution.py:124
  85.8 20.9 %copy-start.10 = (f32[512]{0:T(512)S(1)}, f32[512]{0:T(512)}, u32[]{:S(2)}) copy-start(f32[512]{0:T(512)} %param.17) | copy-start | bytes 6148
  85.8 20.9 %copy-start.11 = (f32[512]{0:T(512)S(1)}, f32[512]{0:T(512)}, u32[]{:S(2)}) copy-start(f32[512]{0:T(512)} %param.19) | copy-start | bytes 6148
  85.8 20.9 %copy-start.12 = (f32[512]{0:T(512)S(1)}, f32[512]{0:T(512)}, u32[]{:S(2)}) copy-start(f32[512]{0:T(512)} %param.18) | copy-start | bytes 6148
  100.7 6.0 %collective-permute-start.7 = (bf16[256,2048]{1,0:T(8,128)(2,1)S(1)}, bf16[256,2048]{1,0:T(8,128)(2,1)}, u32[]{:S(2)}, u32[]{:S(2)}) collective-permute-start(bf16[256,2048]{1,0:T(8,128)(2,1)S(1)} %collective-permute-done.2.refs_5_), channel_id=1, source_target_pairs={{0,1},{1,0},{2,3},{3,2},{4,5},{5,4},{6,7},{7,6},{8,9},{9,8},{10,11... | collective-permute-start | bytes 3145736 | tf_op jit(solution)/shard_map/ppermute | solution.py:124
  103.4 1.0 copy-start
  104.4 3.1 %collective-permute-start.8 = (bf16[256,2048]{1,0:T(8,128)(2,1)S(1)}, bf16[256,2048]{1,0:T(8,128)(2,1)}, u32[]{:S(2)}, u32[]{:S(2)}) collective-permute-start(bf16[256,2048]{1,0:T(8,128)(2,1)S(1)} %collective-permute-done.3.refs_6_), channel_id=1, source_target_pairs={{0,1},{1,0},{2,3},{3,2},{4,5},{5,4},{6,7},{7,6},{8,9},{9,8},{10,11... | collective-permute-start | bytes 3145736 | tf_op jit(solution)/shard_map/ppermute | solution.py:124
  105.1 1.0 copy-start.2
  126.2 1.2 copy-start.1
  127.4 1.2 copy-start.3
  155.6 32.6 %copy-start.13 = (f32[256]{0:T(256)S(1)}, f32[256]{0:T(256)}, u32[]{:S(2)}) copy-start(f32[256]{0:T(256)} %param.20) | copy-start | bytes 3076
  157.1 14.5 %all-to-all-start.1 = ((f32[32,1,768]{2,1,0:T(1,128)}), f32[32,1,768]{2,1,0:T(1,128)S(1)}, u32[]{:S(2)}, u32[]{:S(2)}) async-start(f32[32,1,768]{2,1,0:T(1,128)} %reshape.337), calls=%async_computation.1 | async-start | bytes 196608 | tf_op jit(solution)/shard_map/all_to_all | solution.py:169
  188.1 1.2 copy-start.9
Sparse Core Ops, SparseCore 0:
  26.4 99.7 all-gather.1

commit v9 on v8

--- a/solution.py
+++ b/solution.py
@@ -40,7 +40,7 @@
     target_logit_ref[0] = target_logit
 
 
-def logit_stats(rows, pieces, local_target, tile_m=256, tile_n=1024):
+def logit_stats(rows, pieces, local_target, tile_m=512, tile_n=1024):
     count, width_full = rows.shape
     vocab = pieces[0].shape[1]
     heights = tuple(piece.shape[0] for piece in pieces)

time: 197 us -> 195 us (0.990)
  transfers between devices with their start and end apart: 13 -> 13, of which waited for: 6 -> 6; matrix products, arithmetic and copies ran while one was open for 7% -> 7% of each run, Pallas kernels for 13% -> 12%
where the time goes in v9:
time: 195 us; the launch traced here: 194 us
  waiting for transfers between devices  78.3 us (40%)
  starting transfers between devices  35.3 us (18%)
  Pallas kernels  23.9 us (12%)
  local copies, waits for them, and re-layouts  18.7 us (10%)
  blocking collectives  14.6 us (7%)
  between operations  14.5 us (7%)
  other arithmetic  6.7 us (3%)
  matrix products  2.32 us (1%)
    ppermute x4, waiting for transfers between devices, along_y(): lax.ppermute(x, 'mp', [(i, (i // 2 + shift) % chips * 2 + i % 2) for i in...  44.6 us
    pallas_call x1, Pallas kernels, logit_stats(): pl.pallas_call(lambda *refs: stats_kernel(heights, tile_n, *refs), grid=g...  23.9 us
    all_gather x1, waiting for transfers between devices, body(): block_rows = lax.all_gather(own_rows, 'dp', axis=0, tiled=True)  18.7 us
    psum x1, blocking collectives, body(): lax.psum(jnp.concatenate([block_logprob[None], sums]), 'mp')  14.6 us
    all_to_all x1, starting transfers between devices, body(): lax.all_to_all(reward_send.reshape(shards, pair_len, width_dev), 'dp', 0,...  10.5 us
    all_to_all x1, waiting for transfers between devices, body(): routed = lax.all_to_all(routed, 'dp', 0, 0, tiled=True)  8.44 us
    unnamed x34, local copies, waits for them, and re-layouts  8.15 us
    ppermute x5, starting transfers between devices, body(): lax.ppermute(block, 'mp', [(i, i ^ 1) for i in range(ways)])  7.58 us
  transfers between devices with their start and end apart: 13, of which 6 were waited for; matrix products, arithmetic and copies ran while one was open for 7% of the time, Pallas kernels for 12%

profile of v9, /device:TPU:1, one launch (start us, length us, event | category | flops | bytes accessed | tf_op | source)
XLA Modules:
  0.0 194.4 jit_solution(18017969854162268088)
XLA Ops:
  7.2 0.8 broadcast_multiply_fusion.1
  8.1 0.8 subtract_multiply_fusion.1
  9.7 1.3 copy.78
  11.2 1.0 convolution_convert_fusion.2
  12.2 6.5 %all-to-all-start = ((bf16[8,32,512]{2,1,0:T(8,128)(2,1)}), bf16[8,32,512]{2,1,0:T(8,128)(2,1)S(1)}, u32[]{:S(2)}, u32[]{:S(2)}) async-start(bf16[8,32,512]{2,1,0:T(8,128)(2,1)} %bitcast.2), calls=%async_computation | async-start | bytes 524288 | tf_op jit(solution)/shard_map/all_to_all | solution.py:134
  18.7 0.6 gather_fusion
  19.4 5.8 %all-to-all-done = bf16[8,32,512]{2,1,0:T(8,128)(2,1)S(1)} async-done(((bf16[8,32,512]{2,1,0:T(8,128)(2,1)}), bf16[8,32,512]{2,1,0:T(8,128)(2,1)S(1)}, u32[]{:S(2)}, u32[]{:S(2)}) %all-to-all-start) | async-done | bytes 262176 | tf_op jit(solution)/shard_map/all_to_all | solution.py:134
  25.2 0.3 convolution_convert_fusion.1
  25.5 0.8 copy.88
  26.3 0.4 collective-permute-start
  26.7 2.4 %collective-permute-start.1 = (bf16[512,2048]{1,0:T(8,128)(2,1)}, bf16[512,2048]{1,0:T(8,128)(2,1)}, u32[]{:S(2)}, u32[]{:S(2)}) collective-permute-start(bf16[512,2048]{1,0:T(8,128)(2,1)} %refs_2_.1), channel_id=1, source_target_pairs={{0,6},{1,7},{2,0},{3,1},{4,2},{5,3},{6,4},{7,5},{8,14},{9,15},{10,... | collective-permute-start | bytes 6291464 | tf_op jit(solution)/shard_map/ppermute | solution.py:113
  29.1 1.6 collective-permute-start.4
  30.7 0.3 copy.86
  31.1 1.0 fusion
  32.1 10.5 %all-to-all-start.2 = ((bf16[32,8,512]{2,1,0:T(8,128)(2,1)}), bf16[32,8,512]{2,1,0:T(8,128)(2,1)S(1)}, u32[]{:S(2)}, u32[]{:S(2)}) async-start(bf16[32,8,512]{2,1,0:T(8,128)(2,1)} %fusion), calls=%async_computation.2 | async-start | bytes 524288 | tf_op jit(solution)/shard_map/all_to_all | solution.py:105
  42.7 31.4 %collective-permute-done.refs_3_ = bf16[512,2048]{1,0:T(8,128)(2,1)} collective-permute-done((bf16[512,2048]{1,0:T(8,128)(2,1)}, bf16[512,2048]{1,0:T(8,128)(2,1)}, u32[]{:S(2)}, u32[]{:S(2)}) %collective-permute-start) | collective-permute-done | bytes 2097184 | tf_op jit(solution)/shard_map/ppermute | solution.py:113
  74.1 2.3 %slice.91 = bf16[256,2048]{1,0:T(8,128)(2,1)} slice(bf16[512,2048]{1,0:T(8,128)(2,1)} %collective-permute-done.refs_3_), slice={[0:256], [0:2048]} | slice | bytes 2097152 | tf_op jit(solution)/shard_map/slice | solution.py:121
  76.4 2.3 %slice.92 = bf16[256,2048]{1,0:T(8,128)(2,1)} slice(bf16[512,2048]{1,0:T(8,128)(2,1)} %collective-permute-done.1.refs_4_), slice={[256:512], [0:2048]} | slice | bytes 2097152 | tf_op jit(solution)/shard_map/slice | solution.py:122
  78.7 2.7 %collective-permute-start.3 = (bf16[256,2048]{1,0:T(8,128)(2,1)}, bf16[256,2048]{1,0:T(8,128)(2,1)S(1)}, u32[]{:S(2)}, u32[]{:S(2)}) collective-permute-start(bf16[256,2048]{1,0:T(8,128)(2,1)} %slice.92), channel_id=1, source_target_pairs={{0,6},{1,7},{2,0},{3,1},{4,2},{5,3},{6,4},{7,5},{8,14},{9,15},{10,... | collective-permute-start | bytes 3145736 | tf_op jit(solution)/shard_map/ppermute | solution.py:113
  81.5 0.2 reduce_window_sum.11
  81.8 2.5 %collective-permute-start.5 = (bf16[512,2048]{1,0:T(8,128)(2,1)}, bf16[512,2048]{1,0:T(8,128)(2,1)}, u32[]{:S(2)}, u32[]{:S(2)}) collective-permute-start(bf16[512,2048]{1,0:T(8,128)(2,1)} %collective-permute-done.refs_3_), channel_id=1, source_target_pairs={{0,1},{1,0},{2,3},{3,2},{4,5},{5,4},{6,7},{7,6},{8,9},{9,8},{10,11... | collective-permute-start | bytes 6291464 | tf_op jit(solution)/shard_map/ppermute | solution.py:124
  84.4 0.9 convert_reduce_fusion
  86.1 0.4 copy.77
  86.4 0.5 broadcast_in_dim.106
  86.9 0.6 select_reduce_fusion
  87.5 13.2 %collective-permute-done.2.refs_5_ = bf16[256,2048]{1,0:T(8,128)(2,1)S(1)} collective-permute-done((bf16[256,2048]{1,0:T(8,128)(2,1)}, bf16[256,2048]{1,0:T(8,128)(2,1)S(1)}, u32[]{:S(2)}, u32[]{:S(2)}) %collective-permute-start.2) | collective-permute-done | bytes 1048608 | tf_op jit(solution)/shard_map/ppermute | solution.py:113
  100.7 2.6 %collective-permute-start.7 = (bf16[256,2048]{1,0:T(8,128)(2,1)S(1)}, bf16[256,2048]{1,0:T(8,128)(2,1)}, u32[]{:S(2)}, u32[]{:S(2)}) collective-permute-start(bf16[256,2048]{1,0:T(8,128)(2,1)S(1)} %collective-permute-done.2.refs_5_), channel_id=1, source_target_pairs={{0,1},{1,0},{2,3},{3,2},{4,5},{5,4},{6,7},{7,6},{8,9},{9,8},{10,11... | collective-permute-start | bytes 3145736 | tf_op jit(solution)/shard_map/ppermute | solution.py:124
  103.4 1.0 copy-done
  104.4 0.7 collective-permute-start.8
  105.1 1.0 copy-done.2
  106.1 0.5 sub.123.refs_0_
  106.7 0.7 collective-permute-done.8.refs_11_
  107.5 18.7 %all-gather.2.cloned.1.call-done.refs_1_ = bf16[1024,4096]{1,0:T(8,128)(2,1)} async-done(((bf16[32,4096]{1,0:T(8,128)(2,1)}), bf16[1024,4096]{1,0:T(8,128)(2,1)}) %all-gather.2.cloned.1.call-update) | async-done | bytes 8388624 | tf_op jit(solution)/shard_map/all_gather | solution.py:138
  126.2 1.2 copy-done.1
  127.4 1.2 copy-done.3
  128.7 23.9 %shard_map.122 = (f32[2,1024,1]{2,1,0:T(8,128)S(1)}, f32[2,1024,1]{2,1,0:T(8,128)S(1)}, f32[2,1024,1]{2,1,0:T(8,128)S(1)}) custom-call(s32[1024,1]{1,0:T(8,128)S(1)} %sub.123.refs_0_, bf16[1024,4096]{1,0:T(8,128)(2,1)} %all-gather.2.cloned.1.call-done.refs_1_, bf16[512,2048]{1,0:T(8,128)(2,1)} %refs_2_.1, bf16[512,2048]{1,0:T(8,128)(2,1)} %collective-permute-done.refs_3_, ...), custom_call_target="tpu_custom_call" | custom-call | flops 17179869184 | bytes 33554432 | tf_op jit(solution)/shard_map/pallas_call | solution.py:50
  152.6 0.5 fusion.23
  153.2 0.3 reduce.7
  153.9 0.2 reduce_sum.112
  154.3 0.3 select_reduce_fusion.1
  154.6 0.8 reshape.337
  155.4 5.4 %all-to-all-start.1 = ((f32[32,1,768]{2,1,0:T(1,128)}), f32[32,1,768]{2,1,0:T(1,128)S(1)}, u32[]{:S(2)}, u32[]{:S(2)}) async-start(f32[32,1,768]{2,1,0:T(1,128)} %reshape.337), calls=%async_computation.1 | async-start | bytes 196608 | tf_op jit(solution)/shard_map/all_to_all | solution.py:169
  161.0 0.2 fusion.1
  161.4 8.4 %all-to-all-done.1 = f32[32,1,768]{2,1,0:T(1,128)S(1)} async-done(((f32[32,1,768]{2,1,0:T(1,128)}), f32[32,1,768]{2,1,0:T(1,128)S(1)}, u32[]{:S(2)}, u32[]{:S(2)}) %all-to-all-start.1) | async-done | bytes 98336 | tf_op jit(solution)/shard_map/all_to_all | solution.py:169
  169.9 0.5 broadcast.341
  170.4 0.9 reduce.10
  171.8 14.6 %psum.7 = f32[4,256]{1,0:T(4,128)S(1)} all-reduce(f32[4,256]{1,0:T(4,128)S(1)} %pad_maximum_fusion), channel_id=1, replica_groups=mesh['dp'=32,'mp'=8] {'mp'}, use_global_device_ids=true, to_apply=%region_13.14 | all-reduce | flops 1024 | bytes 8192 | tf_op jit(solution)/shard_map/psum | solution.py:186
  186.9 0.7 reshape.325
  (100 shorter events, 4.4 us)
Async XLA Ops:
  7.2 11.6 %copy-start.4 = (s32[4]{0:T(128)S(1)}, s32[4]{0:T(128)}, u32[]{:S(2)}) copy-start(s32[4]{0:T(128)} %constant.105.clone) | copy-start | bytes 52
  11.0 19.7 %copy-start.5 = (bf16[64,7,512]{2,0,1:T(8,128)(2,1)S(1)}, bf16[64,7,512]{2,0,1:T(8,128)(2,1)}, u32[]{:S(2)}) copy-start(bf16[64,7,512]{2,0,1:T(8,128)(2,1)} %param.15) | copy-start | bytes 1376260
  12.2 13.0 %all-to-all-start = ((bf16[8,32,512]{2,1,0:T(8,128)(2,1)}), bf16[8,32,512]{2,1,0:T(8,128)(2,1)S(1)}, u32[]{:S(2)}, u32[]{:S(2)}) async-start(bf16[8,32,512]{2,1,0:T(8,128)(2,1)} %bitcast.2), calls=%async_computation | async-start | bytes 524288 | tf_op jit(solution)/shard_map/all_to_all | solution.py:134
  18.7 107.5 %all-gather.2.cloned.1.call-start = ((), (), s32[]{:S(2)}) async-start(), calls=%async_computation.3 | async-start | bytes 8650752 | tf_op jit(solution)/shard_map/all_gather | solution.py:138
  25.5 17.1 %copy-start.7 = (s32[2048]{0:T(1024)S(1)}, s32[2048]{0:T(1024)}, u32[]{:S(2)}) copy-start(s32[2048]{0:T(1024)} %param.13) | copy-start | bytes 24580
  26.3 47.8 %collective-permute-start = (bf16[512,2048]{1,0:T(8,128)(2,1)}, bf16[512,2048]{1,0:T(8,128)(2,1)}, u32[]{:S(2)}, u32[]{:S(2)}) collective-permute-start(bf16[512,2048]{1,0:T(8,128)(2,1)} %refs_2_.1), channel_id=1, source_target_pairs={{0,2},{1,3},{2,4},{3,5},{4,6},{5,7},{6,0},{7,1},{8,10},{9,11},{10,... | collective-permute-start | bytes 6291464 | tf_op jit(solution)/shard_map/ppermute | solution.py:113
  26.7 49.7 %collective-permute-start.1 = (bf16[512,2048]{1,0:T(8,128)(2,1)}, bf16[512,2048]{1,0:T(8,128)(2,1)}, u32[]{:S(2)}, u32[]{:S(2)}) collective-permute-start(bf16[512,2048]{1,0:T(8,128)(2,1)} %refs_2_.1), channel_id=1, source_target_pairs={{0,6},{1,7},{2,0},{3,1},{4,2},{5,3},{6,4},{7,5},{8,14},{9,15},{10,... | collective-permute-start | bytes 6291464 | tf_op jit(solution)/shard_map/ppermute | solution.py:113
  29.1 77.7 %collective-permute-start.4 = (bf16[512,2048]{1,0:T(8,128)(2,1)}, bf16[512,2048]{1,0:T(8,128)(2,1)}, u32[]{:S(2)}, u32[]{:S(2)}) collective-permute-start(bf16[512,2048]{1,0:T(8,128)(2,1)} %refs_2_.1), channel_id=1, source_target_pairs={{0,1},{1,0},{2,3},{3,2},{4,5},{5,4},{6,7},{7,6},{8,9},{9,8},{10,11... | collective-permute-start | bytes 6291464 | tf_op jit(solution)/shard_map/ppermute | solution.py:124
  32.1 123.3 %all-to-all-start.2 = ((bf16[32,8,512]{2,1,0:T(8,128)(2,1)}), bf16[32,8,512]{2,1,0:T(8,128)(2,1)S(1)}, u32[]{:S(2)}, u32[]{:S(2)}) async-start(bf16[32,8,512]{2,1,0:T(8,128)(2,1)} %fusion), calls=%async_computation.2 | async-start | bytes 524288 | tf_op jit(solution)/shard_map/all_to_all | solution.py:105
  42.7 38.7 %copy-start.8 = (s32[2048]{0:T(1024)S(1)}, s32[2048]{0:T(1024)}, u32[]{:S(2)}) copy-start(s32[2048]{0:T(1024)} %param.12) | copy-start | bytes 24580
  76.4 24.3 %collective-permute-start.2 = (bf16[256,2048]{1,0:T(8,128)(2,1)}, bf16[256,2048]{1,0:T(8,128)(2,1)S(1)}, u32[]{:S(2)}, u32[]{:S(2)}) collective-permute-start(bf16[256,2048]{1,0:T(8,128)(2,1)} %slice.91), channel_id=1, source_target_pairs={{0,2},{1,3},{2,4},{3,5},{4,6},{5,7},{6,0},{7,1},{8,10},{9,11},{10,... | collective-permute-start | bytes 3145736 | tf_op jit(solution)/shard_map/ppermute | solution.py:113
  78.7 7.4 %copy-start.6 = (s32[2048,7]{0,1:T(8,128)S(1)}, s32[2048,7]{0,1:T(8,128)}, u32[]{:S(2)}) copy-start(s32[2048,7]{0,1:T(8,128)} %param.11) | copy-start | bytes 172036
  78.7 25.6 %collective-permute-start.3 = (bf16[256,2048]{1,0:T(8,128)(2,1)}, bf16[256,2048]{1,0:T(8,128)(2,1)S(1)}, u32[]{:S(2)}, u32[]{:S(2)}) collective-permute-start(bf16[256,2048]{1,0:T(8,128)(2,1)} %slice.92), channel_id=1, source_target_pairs={{0,6},{1,7},{2,0},{3,1},{4,2},{5,3},{6,4},{7,5},{8,14},{9,15},{10,... | collective-permute-start | bytes 3145736 | tf_op jit(solution)/shard_map/ppermute | solution.py:113
  81.8 25.7 %collective-permute-start.5 = (bf16[512,2048]{1,0:T(8,128)(2,1)}, bf16[512,2048]{1,0:T(8,128)(2,1)}, u32[]{:S(2)}, u32[]{:S(2)}) collective-permute-start(bf16[512,2048]{1,0:T(8,128)(2,1)} %collective-permute-done.refs_3_), channel_id=1, source_target_pairs={{0,1},{1,0},{2,3},{3,2},{4,5},{5,4},{6,7},{7,6},{8,9},{9,8},{10,11... | collective-permute-start | bytes 6291464 | tf_op jit(solution)/shard_map/ppermute | solution.py:124
  84.3 23.2 %collective-permute-start.6 = (bf16[512,2048]{1,0:T(8,128)(2,1)}, bf16[512,2048]{1,0:T(8,128)(2,1)}, u32[]{:S(2)}, u32[]{:S(2)}) collective-permute-start(bf16[512,2048]{1,0:T(8,128)(2,1)} %collective-permute-done.1.refs_4_), channel_id=1, source_target_pairs={{0,1},{1,0},{2,3},{3,2},{4,5},{5,4},{6,7},{7,6},{8,9},{9,8},{10,11... | collective-permute-start | bytes 6291464 | tf_op jit(solution)/shard_map/ppermute | solution.py:124
  85.8 20.9 %copy-start.10 = (f32[512]{0:T(512)S(1)}, f32[512]{0:T(512)}, u32[]{:S(2)}) copy-start(f32[512]{0:T(512)} %param.17) | copy-start | bytes 6148
  85.8 20.9 %copy-start.11 = (f32[512]{0:T(512)S(1)}, f32[512]{0:T(512)}, u32[]{:S(2)}) copy-start(f32[512]{0:T(512)} %param.19) | copy-start | bytes 6148
  85.8 20.9 %copy-start.12 = (f32[512]{0:T(512)S(1)}, f32[512]{0:T(512)}, u32[]{:S(2)}) copy-start(f32[512]{0:T(512)} %param.18) | copy-start | bytes 6148
  100.7 6.0 %collective-permute-start.7 = (bf16[256,2048]{1,0:T(8,128)(2,1)S(1)}, bf16[256,2048]{1,0:T(8,128)(2,1)}, u32[]{:S(2)}, u32[]{:S(2)}) collective-permute-start(bf16[256,2048]{1,0:T(8,128)(2,1)S(1)} %collective-permute-done.2.refs_5_), channel_id=1, source_target_pairs={{0,1},{1,0},{2,3},{3,2},{4,5},{5,4},{6,7},{7,6},{8,9},{9,8},{10,11... | collective-permute-start | bytes 3145736 | tf_op jit(solution)/shard_map/ppermute | solution.py:124
  103.4 1.0 copy-start
  104.4 3.1 %collective-permute-start.8 = (bf16[256,2048]{1,0:T(8,128)(2,1)S(1)}, bf16[256,2048]{1,0:T(8,128)(2,1)}, u32[]{:S(2)}, u32[]{:S(2)}) collective-permute-start(bf16[256,2048]{1,0:T(8,128)(2,1)S(1)} %collective-permute-done.3.refs_6_), channel_id=1, source_target_pairs={{0,1},{1,0},{2,3},{3,2},{4,5},{5,4},{6,7},{7,6},{8,9},{9,8},{10,11... | collective-permute-start | bytes 3145736 | tf_op jit(solution)/shard_map/ppermute | solution.py:124
  105.1 1.0 copy-start.2
  126.2 1.2 copy-start.1
  127.4 1.2 copy-start.3
  153.9 32.6 %copy-start.13 = (f32[256]{0:T(256)S(1)}, f32[256]{0:T(256)}, u32[]{:S(2)}) copy-start(f32[256]{0:T(256)} %param.20) | copy-start | bytes 3076
  155.4 14.5 %all-to-all-start.1 = ((f32[32,1,768]{2,1,0:T(1,128)}), f32[32,1,768]{2,1,0:T(1,128)S(1)}, u32[]{:S(2)}, u32[]{:S(2)}) async-start(f32[32,1,768]{2,1,0:T(1,128)} %reshape.337), calls=%async_computation.1 | async-start | bytes 196608 | tf_op jit(solution)/shard_map/all_to_all | solution.py:169
  186.4 1.2 copy-start.9
Sparse Core Ops, SparseCore 0:
  26.4 99.7 all-gather.1

commit v10 on v9

--- a/solution.py
+++ b/solution.py
@@ -102,9 +102,17 @@
     reward_send = jnp.dot(
         onehot, reward_hidden.reshape(req_dev * max_len, width_dev), preferred_element_type=jnp.float32
     ).astype(jnp.bfloat16)
-    reward_packed = lax.all_to_all(
-        reward_send.reshape(shards, pair_len, width_dev), "dp", 0, 0, tiled=True
-    ).reshape(slot_dev, width_dev)
+    hidden_f = reward_send.astype(jnp.float32)
+    partial = jnp.stack(
+        [
+            jnp.sum(hidden_f * hidden_f, axis=1),
+            jnp.sum(hidden_f * (norm_gain * score_weight), axis=1),
+            jnp.sum(hidden_f * (norm_gain * value_weight), axis=1),
+        ],
+        axis=1,
+    )
+    sums = lax.all_to_all(partial.reshape(shards, pair_len, 3), "dp", 0, 0, tiled=True)
+    sums = sums.reshape(slot_dev, 3).T
 
     chips = ways // 2
     half = width_dev // 2
@@ -175,14 +183,6 @@
         holder, joint_target - joint_max - jnp.log(joint_total), 0.0
     ).reshape(-1)
 
-    hidden_f = reward_packed.astype(jnp.float32)
-    sums = jnp.stack(
-        [
-            jnp.sum(hidden_f * hidden_f, axis=1),
-            jnp.sum(hidden_f * (norm_gain * score_weight), axis=1),
-            jnp.sum(hidden_f * (norm_gain * value_weight), axis=1),
-        ]
-    )
     ref_logprob, squares, score_dot, value_dot = lax.psum(
         jnp.concatenate([block_logprob[None], sums]), "mp"
     )

time: 195 us -> 193 us (0.990)
  no operation moved by 1% of the time
where the time goes in v10:
time: 193 us
  waiting for transfers between devices  76.6 us (40%)
  starting transfers between devices  35.4 us (18%)
  Pallas kernels  23.9 us (12%)
  local copies, waits for them, and re-layouts  19.5 us (10%)
  blocking collectives  14.6 us (8%)
  between operations  14.5 us (8%)
  other arithmetic  6.51 us (3%)
    ppermute x4, waiting for transfers between devices, along_y(): lax.ppermute(x, 'mp', [(i, (i // 2 + shift) % chips * 2 + i % 2) for i in...  44.8 us
    pallas_call x1, Pallas kernels, logit_stats(): pl.pallas_call(lambda *refs: stats_kernel(heights, tile_n, *refs), grid=g...  23.9 us
    all_gather x1, waiting for transfers between devices, body(): block_rows = lax.all_gather(own_rows, 'dp', axis=0, tiled=True)  17 us
    psum x1, blocking collectives, body(): lax.psum(jnp.concatenate([block_logprob[None], sums]), 'mp')  14.6 us
    all_to_all x1, starting transfers between devices, body(): lax.all_to_all(partial.reshape(shards, pair_len, 3), 'dp', 0, 0, tiled=True)  10.5 us
    all_to_all x1, waiting for transfers between devices, body(): routed = lax.all_to_all(routed, 'dp', 0, 0, tiled=True)  8.81 us
    unnamed x34, local copies, waits for them, and re-layouts  8.15 us
    ppermute x5, starting transfers between devices, body(): lax.ppermute(block, 'mp', [(i, i ^ 1) for i in range(ways)])  7.52 us
  transfers between devices with their start and end apart: 13, of which 6 were waited for; matrix products, arithmetic and copies ran while one was open for 7% of the time, Pallas kernels for 12%

profile of v10, /device:TPU:1, one launch (start us, length us, event | category | flops | bytes accessed | tf_op | source)
XLA Modules:
  0.0 192.9 jit_solution(13975304566436118682)
XLA Ops:
  7.2 0.8 broadcast_multiply_fusion.1
  7.9 0.2 convert_reduce_fusion.1
  8.1 0.8 subtract_multiply_fusion.1
  9.7 1.3 copy.99
  11.2 1.0 convolution_convert_fusion.2
  12.2 6.6 %all-to-all-start = ((bf16[8,32,512]{2,1,0:T(8,128)(2,1)}), bf16[8,32,512]{2,1,0:T(8,128)(2,1)S(1)}, u32[]{:S(2)}, u32[]{:S(2)}) async-start(bf16[8,32,512]{2,1,0:T(8,128)(2,1)} %bitcast.2), calls=%async_computation | async-start | bytes 524288 | tf_op jit(solution)/shard_map/all_to_all | solution.py:142
  18.9 0.6 gather_fusion
  19.5 5.8 %all-to-all-done = bf16[8,32,512]{2,1,0:T(8,128)(2,1)S(1)} async-done(((bf16[8,32,512]{2,1,0:T(8,128)(2,1)}), bf16[8,32,512]{2,1,0:T(8,128)(2,1)S(1)}, u32[]{:S(2)}, u32[]{:S(2)}) %all-to-all-start) | async-done | bytes 262176 | tf_op jit(solution)/shard_map/all_to_all | solution.py:142
  25.3 0.3 convolution_convert_fusion.1
  25.6 0.8 copy.111
  26.4 0.4 collective-permute-start
  26.8 2.4 %collective-permute-start.1 = (bf16[512,2048]{1,0:T(8,128)(2,1)}, bf16[512,2048]{1,0:T(8,128)(2,1)}, u32[]{:S(2)}, u32[]{:S(2)}) collective-permute-start(bf16[512,2048]{1,0:T(8,128)(2,1)} %refs_2_.1), channel_id=1, source_target_pairs={{0,6},{1,7},{2,0},{3,1},{4,2},{5,3},{6,4},{7,5},{8,14},{9,15},{10,... | collective-permute-start | bytes 6291464 | tf_op jit(solution)/shard_map/ppermute | solution.py:121
  29.2 1.6 collective-permute-start.4
  30.8 0.3 copy.107
  31.3 0.5 multiply_reduce_fusion.2
  32.0 0.7 copy.108
  32.7 10.5 %all-to-all-start.2 = ((f32[32,8,3]{1,2,0:T(4,128)}), f32[32,8,3]{1,2,0:T(4,128)S(1)}, u32[]{:S(2)}, u32[]{:S(2)}) async-start(f32[32,8,3]{1,2,0:T(4,128)} %copy.108), calls=%async_computation.2 | async-start | bytes 131072 | tf_op jit(solution)/shard_map/all_to_all | solution.py:114
  43.3 30.9 %collective-permute-done.refs_3_ = bf16[512,2048]{1,0:T(8,128)(2,1)} collective-permute-done((bf16[512,2048]{1,0:T(8,128)(2,1)}, bf16[512,2048]{1,0:T(8,128)(2,1)}, u32[]{:S(2)}, u32[]{:S(2)}) %collective-permute-start) | collective-permute-done | bytes 2097184 | tf_op jit(solution)/shard_map/ppermute | solution.py:121
  74.2 2.3 %slice.91 = bf16[256,2048]{1,0:T(8,128)(2,1)} slice(bf16[512,2048]{1,0:T(8,128)(2,1)} %collective-permute-done.refs_3_), slice={[0:256], [0:2048]} | slice | bytes 2097152 | tf_op jit(solution)/shard_map/slice | solution.py:129
  76.5 2.3 %slice.92 = bf16[256,2048]{1,0:T(8,128)(2,1)} slice(bf16[512,2048]{1,0:T(8,128)(2,1)} %collective-permute-done.1.refs_4_), slice={[256:512], [0:2048]} | slice | bytes 2097152 | tf_op jit(solution)/shard_map/slice | solution.py:130
  78.8 2.7 %collective-permute-start.3 = (bf16[256,2048]{1,0:T(8,128)(2,1)}, bf16[256,2048]{1,0:T(8,128)(2,1)S(1)}, u32[]{:S(2)}, u32[]{:S(2)}) collective-permute-start(bf16[256,2048]{1,0:T(8,128)(2,1)} %slice.92), channel_id=1, source_target_pairs={{0,6},{1,7},{2,0},{3,1},{4,2},{5,3},{6,4},{7,5},{8,14},{9,15},{10,... | collective-permute-start | bytes 3145736 | tf_op jit(solution)/shard_map/ppermute | solution.py:121
  81.5 2.6 %collective-permute-start.5 = (bf16[512,2048]{1,0:T(8,128)(2,1)}, bf16[512,2048]{1,0:T(8,128)(2,1)}, u32[]{:S(2)}, u32[]{:S(2)}) collective-permute-start(bf16[512,2048]{1,0:T(8,128)(2,1)} %collective-permute-done.refs_3_), channel_id=1, source_target_pairs={{0,1},{1,0},{2,3},{3,2},{4,5},{5,4},{6,7},{7,6},{8,9},{9,8},{10,11... | collective-permute-start | bytes 6291464 | tf_op jit(solution)/shard_map/ppermute | solution.py:132
  84.2 0.2 reduce_window_sum.11
  84.5 0.9 convert_reduce_fusion
  86.1 0.4 copy.98
  86.5 0.5 broadcast_in_dim.106
  87.0 13.9 %collective-permute-done.2.refs_5_ = bf16[256,2048]{1,0:T(8,128)(2,1)S(1)} collective-permute-done((bf16[256,2048]{1,0:T(8,128)(2,1)}, bf16[256,2048]{1,0:T(8,128)(2,1)S(1)}, u32[]{:S(2)}, u32[]{:S(2)}) %collective-permute-start.2) | collective-permute-done | bytes 1048608 | tf_op jit(solution)/shard_map/ppermute | solution.py:121
  100.9 2.6 %collective-permute-start.7 = (bf16[256,2048]{1,0:T(8,128)(2,1)S(1)}, bf16[256,2048]{1,0:T(8,128)(2,1)}, u32[]{:S(2)}, u32[]{:S(2)}) collective-permute-start(bf16[256,2048]{1,0:T(8,128)(2,1)S(1)} %collective-permute-done.2.refs_5_), channel_id=1, source_target_pairs={{0,1},{1,0},{2,3},{3,2},{4,5},{5,4},{6,7},{7,6},{8,9},{9,8},{10,11... | collective-permute-start | bytes 3145736 | tf_op jit(solution)/shard_map/ppermute | solution.py:132
  103.5 1.0 copy-done
  104.5 0.7 collective-permute-start.8
  105.2 1.0 copy-done.2
  106.2 0.6 select_reduce_fusion
  106.9 0.5 sub.123.refs_0_
  107.6 17.0 %all-gather.2.cloned.1.call-done.refs_1_ = bf16[1024,4096]{1,0:T(8,128)(2,1)} async-done(((bf16[32,4096]{1,0:T(8,128)(2,1)}), bf16[1024,4096]{1,0:T(8,128)(2,1)}) %all-gather.2.cloned.1.call-update) | async-done | bytes 8388624 | tf_op jit(solution)/shard_map/all_gather | solution.py:146
  124.7 1.2 copy-done.1
  125.9 1.2 copy-done.3
  127.1 23.9 %shard_map.122 = (f32[2,1024,1]{2,1,0:T(8,128)S(1)}, f32[2,1024,1]{2,1,0:T(8,128)S(1)}, f32[2,1024,1]{2,1,0:T(8,128)S(1)}) custom-call(s32[1024,1]{1,0:T(8,128)S(1)} %sub.123.refs_0_, bf16[1024,4096]{1,0:T(8,128)(2,1)} %all-gather.2.cloned.1.call-done.refs_1_, bf16[512,2048]{1,0:T(8,128)(2,1)} %refs_2_.1, bf16[512,2048]{1,0:T(8,128)(2,1)} %collective-permute-done.refs_3_, ...), custom_call_target="tpu_custom_call" | custom-call | flops 17179869184 | bytes 33554432 | tf_op jit(solution)/shard_map/pallas_call | solution.py:50
  151.0 0.5 fusion.20
  151.7 0.3 reduce.4
  152.3 0.2 reduce_sum.112
  152.8 0.3 select_reduce_fusion.1
  153.1 0.8 reshape.327
  153.9 5.4 %all-to-all-start.1 = ((f32[32,1,768]{2,1,0:T(1,128)}), f32[32,1,768]{2,1,0:T(1,128)S(1)}, u32[]{:S(2)}, u32[]{:S(2)}) async-start(f32[32,1,768]{2,1,0:T(1,128)} %reshape.327), calls=%async_computation.1 | async-start | bytes 196608 | tf_op jit(solution)/shard_map/all_to_all | solution.py:177
  159.5 8.8 %all-to-all-done.1 = f32[32,1,768]{2,1,0:T(1,128)S(1)} async-done(((f32[32,1,768]{2,1,0:T(1,128)}), f32[32,1,768]{2,1,0:T(1,128)S(1)}, u32[]{:S(2)}, u32[]{:S(2)}) %all-to-all-start.1) | async-done | bytes 98336 | tf_op jit(solution)/shard_map/all_to_all | solution.py:177
  168.3 0.5 broadcast.333
  168.9 0.9 reduce.7
  170.2 14.6 %psum.7 = f32[4,256]{1,0:T(4,128)S(1)} all-reduce(f32[4,256]{1,0:T(4,128)S(1)} %pad_maximum_fusion.1), channel_id=1, replica_groups=mesh['dp'=32,'mp'=8] {'mp'}, use_global_device_ids=true, to_apply=%region_13.14 | all-reduce | flops 1024 | bytes 8192 | tf_op jit(solution)/shard_map/psum | solution.py:186
  185.3 0.7 reshape.315
  (103 shorter events, 4.4 us)
Async XLA Ops:
  7.2 11.7 %copy-start.4 = (s32[4]{0:T(128)S(1)}, s32[4]{0:T(128)}, u32[]{:S(2)}) copy-start(s32[4]{0:T(128)} %constant.105.clone) | copy-start | bytes 52
  11.0 19.8 %copy-start.5 = (bf16[64,7,512]{2,0,1:T(8,128)(2,1)S(1)}, bf16[64,7,512]{2,0,1:T(8,128)(2,1)}, u32[]{:S(2)}) copy-start(bf16[64,7,512]{2,0,1:T(8,128)(2,1)} %param.15) | copy-start | bytes 1376260
  12.2 19.0 %copy-start.10 = (f32[512]{0:T(512)S(1)}, f32[512]{0:T(512)}, u32[]{:S(2)}) copy-start(f32[512]{0:T(512)} %param.17) | copy-start | bytes 6148
  12.2 19.0 %copy-start.11 = (f32[512]{0:T(512)S(1)}, f32[512]{0:T(512)}, u32[]{:S(2)}) copy-start(f32[512]{0:T(512)} %param.18) | copy-start | bytes 6148
  12.2 19.1 %copy-start.12 = (f32[512]{0:T(512)S(1)}, f32[512]{0:T(512)}, u32[]{:S(2)}) copy-start(f32[512]{0:T(512)} %param.19) | copy-start | bytes 6148
  12.2 13.1 %all-to-all-start = ((bf16[8,32,512]{2,1,0:T(8,128)(2,1)}), bf16[8,32,512]{2,1,0:T(8,128)(2,1)S(1)}, u32[]{:S(2)}, u32[]{:S(2)}) async-start(bf16[8,32,512]{2,1,0:T(8,128)(2,1)} %bitcast.2), calls=%async_computation | async-start | bytes 524288 | tf_op jit(solution)/shard_map/all_to_all | solution.py:142
  18.8 105.8 %all-gather.2.cloned.1.call-start = ((), (), s32[]{:S(2)}) async-start(), calls=%async_computation.3 | async-start | bytes 8650752 | tf_op jit(solution)/shard_map/all_gather | solution.py:146
  26.4 16.8 %copy-start.7 = (s32[2048]{0:T(1024)S(1)}, s32[2048]{0:T(1024)}, u32[]{:S(2)}) copy-start(s32[2048]{0:T(1024)} %param.13) | copy-start | bytes 24580
  26.4 47.8 %collective-permute-start = (bf16[512,2048]{1,0:T(8,128)(2,1)}, bf16[512,2048]{1,0:T(8,128)(2,1)}, u32[]{:S(2)}, u32[]{:S(2)}) collective-permute-start(bf16[512,2048]{1,0:T(8,128)(2,1)} %refs_2_.1), channel_id=1, source_target_pairs={{0,2},{1,3},{2,4},{3,5},{4,6},{5,7},{6,0},{7,1},{8,10},{9,11},{10,... | collective-permute-start | bytes 6291464 | tf_op jit(solution)/shard_map/ppermute | solution.py:121
  26.8 49.7 %collective-permute-start.1 = (bf16[512,2048]{1,0:T(8,128)(2,1)}, bf16[512,2048]{1,0:T(8,128)(2,1)}, u32[]{:S(2)}, u32[]{:S(2)}) collective-permute-start(bf16[512,2048]{1,0:T(8,128)(2,1)} %refs_2_.1), channel_id=1, source_target_pairs={{0,6},{1,7},{2,0},{3,1},{4,2},{5,3},{6,4},{7,5},{8,14},{9,15},{10,... | collective-permute-start | bytes 6291464 | tf_op jit(solution)/shard_map/ppermute | solution.py:121
  29.2 78.3 %collective-permute-start.4 = (bf16[512,2048]{1,0:T(8,128)(2,1)}, bf16[512,2048]{1,0:T(8,128)(2,1)}, u32[]{:S(2)}, u32[]{:S(2)}) collective-permute-start(bf16[512,2048]{1,0:T(8,128)(2,1)} %refs_2_.1), channel_id=1, source_target_pairs={{0,1},{1,0},{2,3},{3,2},{4,5},{5,4},{6,7},{7,6},{8,9},{9,8},{10,11... | collective-permute-start | bytes 6291464 | tf_op jit(solution)/shard_map/ppermute | solution.py:132
  32.7 121.2 %all-to-all-start.2 = ((f32[32,8,3]{1,2,0:T(4,128)}), f32[32,8,3]{1,2,0:T(4,128)S(1)}, u32[]{:S(2)}, u32[]{:S(2)}) async-start(f32[32,8,3]{1,2,0:T(4,128)} %copy.108), calls=%async_computation.2 | async-start | bytes 131072 | tf_op jit(solution)/shard_map/all_to_all | solution.py:114
  43.3 40.8 %copy-start.8 = (s32[2048]{0:T(1024)S(1)}, s32[2048]{0:T(1024)}, u32[]{:S(2)}) copy-start(s32[2048]{0:T(1024)} %param.12) | copy-start | bytes 24580
  76.5 24.3 %collective-permute-start.2 = (bf16[256,2048]{1,0:T(8,128)(2,1)}, bf16[256,2048]{1,0:T(8,128)(2,1)S(1)}, u32[]{:S(2)}, u32[]{:S(2)}) collective-permute-start(bf16[256,2048]{1,0:T(8,128)(2,1)} %slice.91), channel_id=1, source_target_pairs={{0,2},{1,3},{2,4},{3,5},{4,6},{5,7},{6,0},{7,1},{8,10},{9,11},{10,... | collective-permute-start | bytes 3145736 | tf_op jit(solution)/shard_map/ppermute | solution.py:121
  78.8 7.3 %copy-start.6 = (s32[2048,7]{0,1:T(8,128)S(1)}, s32[2048,7]{0,1:T(8,128)}, u32[]{:S(2)}) copy-start(s32[2048,7]{0,1:T(8,128)} %param.11) | copy-start | bytes 172036
  78.8 25.6 %collective-permute-start.3 = (bf16[256,2048]{1,0:T(8,128)(2,1)}, bf16[256,2048]{1,0:T(8,128)(2,1)S(1)}, u32[]{:S(2)}, u32[]{:S(2)}) collective-permute-start(bf16[256,2048]{1,0:T(8,128)(2,1)} %slice.92), channel_id=1, source_target_pairs={{0,6},{1,7},{2,0},{3,1},{4,2},{5,3},{6,4},{7,5},{8,14},{9,15},{10,... | collective-permute-start | bytes 3145736 | tf_op jit(solution)/shard_map/ppermute | solution.py:121
  81.5 26.1 %collective-permute-start.5 = (bf16[512,2048]{1,0:T(8,128)(2,1)}, bf16[512,2048]{1,0:T(8,128)(2,1)}, u32[]{:S(2)}, u32[]{:S(2)}) collective-permute-start(bf16[512,2048]{1,0:T(8,128)(2,1)} %collective-permute-done.refs_3_), channel_id=1, source_target_pairs={{0,1},{1,0},{2,3},{3,2},{4,5},{5,4},{6,7},{7,6},{8,9},{9,8},{10,11... | collective-permute-start | bytes 6291464 | tf_op jit(solution)/shard_map/ppermute | solution.py:132
  84.1 23.6 %collective-permute-start.6 = (bf16[512,2048]{1,0:T(8,128)(2,1)}, bf16[512,2048]{1,0:T(8,128)(2,1)}, u32[]{:S(2)}, u32[]{:S(2)}) collective-permute-start(bf16[512,2048]{1,0:T(8,128)(2,1)} %collective-permute-done.1.refs_4_), channel_id=1, source_target_pairs={{0,1},{1,0},{2,3},{3,2},{4,5},{5,4},{6,7},{7,6},{8,9},{9,8},{10,11... | collective-permute-start | bytes 6291464 | tf_op jit(solution)/shard_map/ppermute | solution.py:132
  100.9 6.6 %collective-permute-start.7 = (bf16[256,2048]{1,0:T(8,128)(2,1)S(1)}, bf16[256,2048]{1,0:T(8,128)(2,1)}, u32[]{:S(2)}, u32[]{:S(2)}) collective-permute-start(bf16[256,2048]{1,0:T(8,128)(2,1)S(1)} %collective-permute-done.2.refs_5_), channel_id=1, source_target_pairs={{0,1},{1,0},{2,3},{3,2},{4,5},{5,4},{6,7},{7,6},{8,9},{9,8},{10,11... | collective-permute-start | bytes 3145736 | tf_op jit(solution)/shard_map/ppermute | solution.py:132
  103.5 1.0 copy-start
  104.5 3.1 %collective-permute-start.8 = (bf16[256,2048]{1,0:T(8,128)(2,1)S(1)}, bf16[256,2048]{1,0:T(8,128)(2,1)}, u32[]{:S(2)}, u32[]{:S(2)}) collective-permute-start(bf16[256,2048]{1,0:T(8,128)(2,1)S(1)} %collective-permute-done.3.refs_6_), channel_id=1, source_target_pairs={{0,1},{1,0},{2,3},{3,2},{4,5},{5,4},{6,7},{7,6},{8,9},{9,8},{10,11... | collective-permute-start | bytes 3145736 | tf_op jit(solution)/shard_map/ppermute | solution.py:132
  105.2 1.0 copy-start.2
  124.7 1.2 copy-start.1
  125.9 1.2 copy-start.3
  152.1 32.9 %copy-start.13 = (f32[256]{0:T(256)S(1)}, f32[256]{0:T(256)}, u32[]{:S(2)}) copy-start(f32[256]{0:T(256)} %param.20) | copy-start | bytes 3076
  153.9 14.5 %all-to-all-start.1 = ((f32[32,1,768]{2,1,0:T(1,128)}), f32[32,1,768]{2,1,0:T(1,128)S(1)}, u32[]{:S(2)}, u32[]{:S(2)}) async-start(f32[32,1,768]{2,1,0:T(1,128)} %reshape.327), calls=%async_computation.1 | async-start | bytes 196608 | tf_op jit(solution)/shard_map/all_to_all | solution.py:177
  184.9 1.2 copy-start.9
Sparse Core Ops, SparseCore 0:
  26.6 98.0 all-gather.1

commit v11 on v10

--- a/solution.py
+++ b/solution.py
@@ -40,7 +40,7 @@
     target_logit_ref[0] = target_logit
 
 
-def logit_stats(rows, pieces, local_target, tile_m=512, tile_n=1024):
+def logit_stats(rows, pieces, local_target, tile_m=1024, tile_n=512):
     count, width_full = rows.shape
     vocab = pieces[0].shape[1]
     heights = tuple(piece.shape[0] for piece in pieces)

time: 193 us -> 196 us (1.016)
  local copies, waits for them, and re-layouts: 19.5 us -> 15 us
  other arithmetic: 6.51 us -> 10.4 us
    unnamed x34 -> x28, local copies, waits for them, and re-layouts: 8.15 us -> 3.7 us
    reduce_max x1, other arithmetic: 0.49 us -> 2.5 us  [body(): row_max = jnp.max(tile_max[:, :, 0], axis=0)]
  transfers between devices with their start and end apart: 13 -> 13, of which waited for: 6 -> 6; matrix products, arithmetic and copies ran while one was open for 7% -> 9% of each run, Pallas kernels for 12% -> 13%
where the time goes in v11:
time: 196 us
  waiting for transfers between devices  77.6 us (40%)
  starting transfers between devices  36.4 us (19%)
  Pallas kernels  25.5 us (13%)
  local copies, waits for them, and re-layouts  15 us (8%)
  blocking collectives  14.6 us (7%)
  between operations  14.5 us (7%)
  other arithmetic  10.4 us (5%)
    ppermute x4, waiting for transfers between devices, along_y(): lax.ppermute(x, 'mp', [(i, (i // 2 + shift) % chips * 2 + i % 2) for i in...  44.8 us
    pallas_call x1, Pallas kernels, logit_stats(): pl.pallas_call(lambda *refs: stats_kernel(heights, tile_n, *refs), grid=g...  25.5 us
    all_gather x1, waiting for transfers between devices, body(): block_rows = lax.all_gather(own_rows, 'dp', axis=0, tiled=True)  17 us
    psum x1, blocking collectives, body(): lax.psum(jnp.concatenate([block_logprob[None], sums]), 'mp')  14.6 us
    all_to_all x1, starting transfers between devices, body(): lax.all_to_all(partial.reshape(shards, pair_len, 3), 'dp', 0, 0, tiled=True)  10.5 us
    all_to_all x1, waiting for transfers between devices, body(): routed = lax.all_to_all(routed, 'dp', 0, 0, tiled=True)  8.81 us
    ppermute x5, starting transfers between devices, body(): lax.ppermute(block, 'mp', [(i, i ^ 1) for i in range(ways)])  8.51 us
    all_to_all x1, starting transfers between devices, body(): lax.all_to_all(ref_send.reshape(ways, sub_len, width_dev), 'mp', 0, 0, ti...  6.64 us
  transfers between devices with their start and end apart: 13, of which 6 were waited for; matrix products, arithmetic and copies ran while one was open for 9% of the time, Pallas kernels for 13%

profile of v11, /device:TPU:1, one launch (start us, length us, event | category | flops | bytes accessed | tf_op | source)
XLA Modules:
  0.0 195.8 jit_solution(8633164289425476598)
XLA Ops:
  7.2 0.8 broadcast_multiply_fusion.1
  7.9 0.2 convert_reduce_fusion.1
  8.1 0.8 subtract_multiply_fusion.1
  9.2 0.1 lt.140
  9.7 1.3 copy.99
  11.0 0.2 reshape.309
  11.2 1.0 convolution_convert_fusion.2
  12.2 6.6 %all-to-all-start = ((bf16[8,32,512]{2,1,0:T(8,128)(2,1)}), bf16[8,32,512]{2,1,0:T(8,128)(2,1)S(1)}, u32[]{:S(2)}, u32[]{:S(2)}) async-start(bf16[8,32,512]{2,1,0:T(8,128)(2,1)} %bitcast.2), calls=%async_computation | async-start | bytes 524288 | tf_op jit(solution)/shard_map/all_to_all | solution.py:142
  18.9 0.6 gather_fusion
  19.6 5.8 %all-to-all-done = bf16[8,32,512]{2,1,0:T(8,128)(2,1)S(1)} async-done(((bf16[8,32,512]{2,1,0:T(8,128)(2,1)}), bf16[8,32,512]{2,1,0:T(8,128)(2,1)S(1)}, u32[]{:S(2)}, u32[]{:S(2)}) %all-to-all-start) | async-done | bytes 262176 | tf_op jit(solution)/shard_map/all_to_all | solution.py:142
  25.3 0.3 convolution_convert_fusion.1
  25.6 0.8 copy.111
  26.4 0.4 collective-permute-start
  26.8 2.4 %collective-permute-start.1 = (bf16[512,2048]{1,0:T(8,128)(2,1)}, bf16[512,2048]{1,0:T(8,128)(2,1)}, u32[]{:S(2)}, u32[]{:S(2)}) collective-permute-start(bf16[512,2048]{1,0:T(8,128)(2,1)} %refs_2_.1), channel_id=1, source_target_pairs={{0,6},{1,7},{2,0},{3,1},{4,2},{5,3},{6,4},{7,5},{8,14},{9,15},{10,... | collective-permute-start | bytes 6291464 | tf_op jit(solution)/shard_map/ppermute | solution.py:121
  29.2 1.6 collective-permute-start.4
  30.8 0.3 copy.107
  31.0 0.2 reshape.312
  31.3 0.5 multiply_reduce_fusion.2
  32.0 0.7 copy.108
  32.7 10.5 %all-to-all-start.2 = ((f32[32,8,3]{1,2,0:T(4,128)}), f32[32,8,3]{1,2,0:T(4,128)S(1)}, u32[]{:S(2)}, u32[]{:S(2)}) async-start(f32[32,8,3]{1,2,0:T(4,128)} %copy.108), calls=%async_computation.2 | async-start | bytes 131072 | tf_op jit(solution)/shard_map/all_to_all | solution.py:114
  43.2 30.9 %collective-permute-done.refs_3_ = bf16[512,2048]{1,0:T(8,128)(2,1)} collective-permute-done((bf16[512,2048]{1,0:T(8,128)(2,1)}, bf16[512,2048]{1,0:T(8,128)(2,1)}, u32[]{:S(2)}, u32[]{:S(2)}) %collective-permute-start) | collective-permute-done | bytes 2097184 | tf_op jit(solution)/shard_map/ppermute | solution.py:121
  74.2 2.3 %slice.91 = bf16[256,2048]{1,0:T(8,128)(2,1)} slice(bf16[512,2048]{1,0:T(8,128)(2,1)} %collective-permute-done.refs_3_), slice={[0:256], [0:2048]} | slice | bytes 2097152 | tf_op jit(solution)/shard_map/slice | solution.py:129
  76.5 2.3 %slice.92 = bf16[256,2048]{1,0:T(8,128)(2,1)} slice(bf16[512,2048]{1,0:T(8,128)(2,1)} %collective-permute-done.1.refs_4_), slice={[256:512], [0:2048]} | slice | bytes 2097152 | tf_op jit(solution)/shard_map/slice | solution.py:130
  78.8 2.7 %collective-permute-start.3 = (bf16[256,2048]{1,0:T(8,128)(2,1)}, bf16[256,2048]{1,0:T(8,128)(2,1)S(1)}, u32[]{:S(2)}, u32[]{:S(2)}) collective-permute-start(bf16[256,2048]{1,0:T(8,128)(2,1)} %slice.92), channel_id=1, source_target_pairs={{0,6},{1,7},{2,0},{3,1},{4,2},{5,3},{6,4},{7,5},{8,14},{9,15},{10,... | collective-permute-start | bytes 3145736 | tf_op jit(solution)/shard_map/ppermute | solution.py:121
  81.5 2.6 %collective-permute-start.5 = (bf16[512,2048]{1,0:T(8,128)(2,1)}, bf16[512,2048]{1,0:T(8,128)(2,1)}, u32[]{:S(2)}, u32[]{:S(2)}) collective-permute-start(bf16[512,2048]{1,0:T(8,128)(2,1)} %collective-permute-done.refs_3_), channel_id=1, source_target_pairs={{0,1},{1,0},{2,3},{3,2},{4,5},{5,4},{6,7},{7,6},{8,9},{9,8},{10,11... | collective-permute-start | bytes 6291464 | tf_op jit(solution)/shard_map/ppermute | solution.py:132
  84.1 0.2 reduce_window_sum.11
  84.5 0.9 convert_reduce_fusion
  86.1 0.4 copy.98
  86.5 0.5 broadcast_in_dim.106
  87.0 13.9 %collective-permute-done.2.refs_5_ = bf16[256,2048]{1,0:T(8,128)(2,1)S(1)} collective-permute-done((bf16[256,2048]{1,0:T(8,128)(2,1)}, bf16[256,2048]{1,0:T(8,128)(2,1)S(1)}, u32[]{:S(2)}, u32[]{:S(2)}) %collective-permute-start.2) | collective-permute-done | bytes 1048608 | tf_op jit(solution)/shard_map/ppermute | solution.py:121
  100.8 2.6 %collective-permute-start.7 = (bf16[256,2048]{1,0:T(8,128)(2,1)S(1)}, bf16[256,2048]{1,0:T(8,128)(2,1)}, u32[]{:S(2)}, u32[]{:S(2)}) collective-permute-start(bf16[256,2048]{1,0:T(8,128)(2,1)S(1)} %collective-permute-done.2.refs_5_), channel_id=1, source_target_pairs={{0,1},{1,0},{2,3},{3,2},{4,5},{5,4},{6,7},{7,6},{8,9},{9,8},{10,11... | collective-permute-start | bytes 3145736 | tf_op jit(solution)/shard_map/ppermute | solution.py:132
  103.5 1.7 collective-permute-start.8
  105.2 0.6 select_reduce_fusion
  105.8 0.5 sub.123.refs_0_
  106.5 1.1 collective-permute-done.8.refs_11_
  107.6 17.0 %all-gather.2.cloned.1.call-done.refs_1_ = bf16[1024,4096]{1,0:T(8,128)(2,1)} async-done(((bf16[32,4096]{1,0:T(8,128)(2,1)}), bf16[1024,4096]{1,0:T(8,128)(2,1)}) %all-gather.2.cloned.1.call-update) | async-done | bytes 8388624 | tf_op jit(solution)/shard_map/all_gather | solution.py:146
  124.6 25.5 %shard_map.122 = (f32[4,1024,1]{2,1,0:T(8,128)}, f32[4,1024,1]{2,1,0:T(8,128)}, f32[4,1024,1]{2,1,0:T(8,128)}) custom-call(s32[1024,1]{1,0:T(8,128)S(1)} %sub.123.refs_0_, bf16[1024,4096]{1,0:T(8,128)(2,1)} %all-gather.2.cloned.1.call-done.refs_1_, bf16[512,2048]{1,0:T(8,128)(2,1)} %refs_2_.1, bf16[512,2048]{1,0:T(8,128)(2,1)} %collective-permute-done.refs_3_, ...), custom_call_target="tpu_custom_call" | custom-call | flops 17179869184 | bytes 50331648 | tf_op jit(solution)/shard_map/pallas_call | solution.py:50
  150.1 2.5 %fusion.20 = (f32[1024]{0:T(1024)S(1)}, f32[4,1024]{1,0:T(4,128)S(1)}) fusion(f32[4,1024,1]{2,1,0:T(8,128)} %get-tuple-element.5), kind=kLoop, calls=%fused_computation.75 | loop fusion | flops 3072 | bytes 36864 | tf_op jit(solution)/shard_map/reduce_max | solution.py:167
  152.8 2.2 %reduce.4 = f32[4,1024]{1,0:T(4,128)S(1)} reduce(f32[4,1024,1]{2,1,0:T(8,128)} %get-tuple-element.6, f32[]{:T(128)} %constant.106), dimensions={2}, to_apply=%get-tuple-element.6.reduce_sub_computation | reduce | bytes 32772 | tf_op jit(solution)/shard_map/pallas_call | solution.py:50
  155.3 0.2 reduce_sum.112
  155.7 0.3 select_reduce_fusion.1
  156.0 0.8 reshape.327
  156.8 5.4 %all-to-all-start.1 = ((f32[32,1,768]{2,1,0:T(1,128)}), f32[32,1,768]{2,1,0:T(1,128)S(1)}, u32[]{:S(2)}, u32[]{:S(2)}) async-start(f32[32,1,768]{2,1,0:T(1,128)} %reshape.327), calls=%async_computation.1 | async-start | bytes 196608 | tf_op jit(solution)/shard_map/all_to_all | solution.py:177
  162.5 8.8 %all-to-all-done.1 = f32[32,1,768]{2,1,0:T(1,128)S(1)} async-done(((f32[32,1,768]{2,1,0:T(1,128)}), f32[32,1,768]{2,1,0:T(1,128)S(1)}, u32[]{:S(2)}, u32[]{:S(2)}) %all-to-all-start.1) | async-done | bytes 98336 | tf_op jit(solution)/shard_map/all_to_all | solution.py:177
  171.3 0.5 broadcast.333
  171.8 0.9 reduce.7
  173.2 14.6 %psum.7 = f32[4,256]{1,0:T(4,128)S(1)} all-reduce(f32[4,256]{1,0:T(4,128)S(1)} %pad_maximum_fusion.1), channel_id=1, replica_groups=mesh['dp'=32,'mp'=8] {'mp'}, use_global_device_ids=true, to_apply=%region_13.14 | all-reduce | flops 1024 | bytes 8192 | tf_op jit(solution)/shard_map/psum | solution.py:186
  188.3 0.7 reshape.315
  (97 shorter events, 3.8 us)
Async XLA Ops:
  7.2 11.7 %copy-start = (s32[4]{0:T(128)S(1)}, s32[4]{0:T(128)}, u32[]{:S(2)}) copy-start(s32[4]{0:T(128)} %constant.105.clone) | copy-start | bytes 52
  11.0 19.8 %copy-start.2 = (bf16[64,7,512]{2,0,1:T(8,128)(2,1)S(1)}, bf16[64,7,512]{2,0,1:T(8,128)(2,1)}, u32[]{:S(2)}) copy-start(bf16[64,7,512]{2,0,1:T(8,128)(2,1)} %param.15) | copy-start | bytes 1376260
  12.2 19.0 %copy-start.7 = (f32[512]{0:T(512)S(1)}, f32[512]{0:T(512)}, u32[]{:S(2)}) copy-start(f32[512]{0:T(512)} %param.17) | copy-start | bytes 6148
  12.2 19.0 %copy-start.8 = (f32[512]{0:T(512)S(1)}, f32[512]{0:T(512)}, u32[]{:S(2)}) copy-start(f32[512]{0:T(512)} %param.18) | copy-start | bytes 6148
  12.2 19.0 %copy-start.9 = (f32[512]{0:T(512)S(1)}, f32[512]{0:T(512)}, u32[]{:S(2)}) copy-start(f32[512]{0:T(512)} %param.19) | copy-start | bytes 6148
  12.2 13.1 %all-to-all-start = ((bf16[8,32,512]{2,1,0:T(8,128)(2,1)}), bf16[8,32,512]{2,1,0:T(8,128)(2,1)S(1)}, u32[]{:S(2)}, u32[]{:S(2)}) async-start(bf16[8,32,512]{2,1,0:T(8,128)(2,1)} %bitcast.2), calls=%async_computation | async-start | bytes 524288 | tf_op jit(solution)/shard_map/all_to_all | solution.py:142
  18.8 105.8 %all-gather.2.cloned.1.call-start = ((), (), s32[]{:S(2)}) async-start(), calls=%async_computation.3 | async-start | bytes 8650752 | tf_op jit(solution)/shard_map/all_gather | solution.py:146
  26.4 16.7 %copy-start.4 = (s32[2048]{0:T(1024)S(1)}, s32[2048]{0:T(1024)}, u32[]{:S(2)}) copy-start(s32[2048]{0:T(1024)} %param.13) | copy-start | bytes 24580
  26.4 47.8 %collective-permute-start = (bf16[512,2048]{1,0:T(8,128)(2,1)}, bf16[512,2048]{1,0:T(8,128)(2,1)}, u32[]{:S(2)}, u32[]{:S(2)}) collective-permute-start(bf16[512,2048]{1,0:T(8,128)(2,1)} %refs_2_.1), channel_id=1, source_target_pairs={{0,2},{1,3},{2,4},{3,5},{4,6},{5,7},{6,0},{7,1},{8,10},{9,11},{10,... | collective-permute-start | bytes 6291464 | tf_op jit(solution)/shard_map/ppermute | solution.py:121
  26.8 49.7 %collective-permute-start.1 = (bf16[512,2048]{1,0:T(8,128)(2,1)}, bf16[512,2048]{1,0:T(8,128)(2,1)}, u32[]{:S(2)}, u32[]{:S(2)}) collective-permute-start(bf16[512,2048]{1,0:T(8,128)(2,1)} %refs_2_.1), channel_id=1, source_target_pairs={{0,6},{1,7},{2,0},{3,1},{4,2},{5,3},{6,4},{7,5},{8,14},{9,15},{10,... | collective-permute-start | bytes 6291464 | tf_op jit(solution)/shard_map/ppermute | solution.py:121
  29.2 77.3 %collective-permute-start.4 = (bf16[512,2048]{1,0:T(8,128)(2,1)}, bf16[512,2048]{1,0:T(8,128)(2,1)}, u32[]{:S(2)}, u32[]{:S(2)}) collective-permute-start(bf16[512,2048]{1,0:T(8,128)(2,1)} %refs_2_.1), channel_id=1, source_target_pairs={{0,1},{1,0},{2,3},{3,2},{4,5},{5,4},{6,7},{7,6},{8,9},{9,8},{10,11... | collective-permute-start | bytes 6291464 | tf_op jit(solution)/shard_map/ppermute | solution.py:132
  32.7 124.2 %all-to-all-start.2 = ((f32[32,8,3]{1,2,0:T(4,128)}), f32[32,8,3]{1,2,0:T(4,128)S(1)}, u32[]{:S(2)}, u32[]{:S(2)}) async-start(f32[32,8,3]{1,2,0:T(4,128)} %copy.108), calls=%async_computation.2 | async-start | bytes 131072 | tf_op jit(solution)/shard_map/all_to_all | solution.py:114
  43.2 40.8 %copy-start.5 = (s32[2048]{0:T(1024)S(1)}, s32[2048]{0:T(1024)}, u32[]{:S(2)}) copy-start(s32[2048]{0:T(1024)} %param.12) | copy-start | bytes 24580
  76.5 24.3 %collective-permute-start.2 = (bf16[256,2048]{1,0:T(8,128)(2,1)}, bf16[256,2048]{1,0:T(8,128)(2,1)S(1)}, u32[]{:S(2)}, u32[]{:S(2)}) collective-permute-start(bf16[256,2048]{1,0:T(8,128)(2,1)} %slice.91), channel_id=1, source_target_pairs={{0,2},{1,3},{2,4},{3,5},{4,6},{5,7},{6,0},{7,1},{8,10},{9,11},{10,... | collective-permute-start | bytes 3145736 | tf_op jit(solution)/shard_map/ppermute | solution.py:121
  78.8 7.3 %copy-start.3 = (s32[2048,7]{0,1:T(8,128)S(1)}, s32[2048,7]{0,1:T(8,128)}, u32[]{:S(2)}) copy-start(s32[2048,7]{0,1:T(8,128)} %param.11) | copy-start | bytes 172036
  78.8 24.7 %collective-permute-start.3 = (bf16[256,2048]{1,0:T(8,128)(2,1)}, bf16[256,2048]{1,0:T(8,128)(2,1)S(1)}, u32[]{:S(2)}, u32[]{:S(2)}) collective-permute-start(bf16[256,2048]{1,0:T(8,128)(2,1)} %slice.92), channel_id=1, source_target_pairs={{0,6},{1,7},{2,0},{3,1},{4,2},{5,3},{6,4},{7,5},{8,14},{9,15},{10,... | collective-permute-start | bytes 3145736 | tf_op jit(solution)/shard_map/ppermute | solution.py:121
  81.5 26.1 %collective-permute-start.5 = (bf16[512,2048]{1,0:T(8,128)(2,1)}, bf16[512,2048]{1,0:T(8,128)(2,1)}, u32[]{:S(2)}, u32[]{:S(2)}) collective-permute-start(bf16[512,2048]{1,0:T(8,128)(2,1)} %collective-permute-done.refs_3_), channel_id=1, source_target_pairs={{0,1},{1,0},{2,3},{3,2},{4,5},{5,4},{6,7},{7,6},{8,9},{9,8},{10,11... | collective-permute-start | bytes 6291464 | tf_op jit(solution)/shard_map/ppermute | solution.py:132
  84.1 23.6 %collective-permute-start.6 = (bf16[512,2048]{1,0:T(8,128)(2,1)}, bf16[512,2048]{1,0:T(8,128)(2,1)}, u32[]{:S(2)}, u32[]{:S(2)}) collective-permute-start(bf16[512,2048]{1,0:T(8,128)(2,1)} %collective-permute-done.1.refs_4_), channel_id=1, source_target_pairs={{0,1},{1,0},{2,3},{3,2},{4,5},{5,4},{6,7},{7,6},{8,9},{9,8},{10,11... | collective-permute-start | bytes 6291464 | tf_op jit(solution)/shard_map/ppermute | solution.py:132
  100.8 5.6 %collective-permute-start.7 = (bf16[256,2048]{1,0:T(8,128)(2,1)S(1)}, bf16[256,2048]{1,0:T(8,128)(2,1)}, u32[]{:S(2)}, u32[]{:S(2)}) collective-permute-start(bf16[256,2048]{1,0:T(8,128)(2,1)S(1)} %collective-permute-done.2.refs_5_), channel_id=1, source_target_pairs={{0,1},{1,0},{2,3},{3,2},{4,5},{5,4},{6,7},{7,6},{8,9},{9,8},{10,11... | collective-permute-start | bytes 3145736 | tf_op jit(solution)/shard_map/ppermute | solution.py:132
  103.5 4.1 %collective-permute-start.8 = (bf16[256,2048]{1,0:T(8,128)(2,1)S(1)}, bf16[256,2048]{1,0:T(8,128)(2,1)}, u32[]{:S(2)}, u32[]{:S(2)}) collective-permute-start(bf16[256,2048]{1,0:T(8,128)(2,1)S(1)} %collective-permute-done.3.refs_6_), channel_id=1, source_target_pairs={{0,1},{1,0},{2,3},{3,2},{4,5},{5,4},{6,7},{7,6},{8,9},{9,8},{10,11... | collective-permute-start | bytes 3145736 | tf_op jit(solution)/shard_map/ppermute | solution.py:132
  150.1 5.2 %copy-start.1 = (f32[4,1024,1]{2,1,0:T(8,128)S(1)}, f32[4,1024,1]{2,1,0:T(8,128)}, u32[]{:S(2)}) copy-start(f32[4,1024,1]{2,1,0:T(8,128)} %get-tuple-element.7) | copy-start | bytes 49156
  155.3 32.6 %copy-start.10 = (f32[256]{0:T(256)S(1)}, f32[256]{0:T(256)}, u32[]{:S(2)}) copy-start(f32[256]{0:T(256)} %param.20) | copy-start | bytes 3076
  156.8 14.5 %all-to-all-start.1 = ((f32[32,1,768]{2,1,0:T(1,128)}), f32[32,1,768]{2,1,0:T(1,128)S(1)}, u32[]{:S(2)}, u32[]{:S(2)}) async-start(f32[32,1,768]{2,1,0:T(1,128)} %reshape.327), calls=%async_computation.1 | async-start | bytes 196608 | tf_op jit(solution)/shard_map/all_to_all | solution.py:177
  187.8 1.2 copy-start.6
Sparse Core Ops, SparseCore 0:
  26.6 98.0 all-gather.1
